TPU v7x, 768 devices: a whole 4x8x12 slice. The times are simulated.
768 devices in a mesh: segment: 4 (over x), mp: 96 (over z, y), seq: 2 (over core).
Axes of the slice: x: 4, y: 8, z: 12, core: 2. Of those that a mesh axis runs over, the one named last changes fastest.
Arguments:
- frames_in: bfloat16 [96, 8, 4, 24, 128], P('mp', 'segment', 'seq'), may hold values from -6 to 6
- valid_frames: int32 [96], P('mp'), may hold values from 1 to 4, as said below
- tokenizer_slot: int32 [96], P('mp'), may hold values from 0 to 95, as said below
- conv_w: bfloat16 [3, 128, 128], replicated, may hold values from -0.3125 to 0.3125
- embed_w: bfloat16 [128, 5120], P(None, 'seq'), may hold values from -0.5 to 0.5
- qkv_w: bfloat16 [5120, 20, 384], P('seq', 'segment'), may hold values from -0.078125 to 0.078125
- out_grad: bfloat16 [96, 4, 4, 24, 20, 128], P('mp', None, 'seq', None, 'segment'), may hold values from -6 to 6
Outputs:
- attn_out: bfloat16 [96, 4, 4, 24, 20, 128], P('mp', None, 'seq', None, 'segment')
- q_grad: bfloat16 [96, 4, 4, 24, 20, 128], P('mp', None, 'seq', None, 'segment')
- k_grad: bfloat16 [96, 4, 4, 24, 20, 128], P('mp', None, 'seq', None, 'segment')
- v_grad: bfloat16 [96, 4, 4, 24, 20, 128], P('mp', None, 'seq', None, 'segment')
Inputs may be any that keep to these rules, and one draw needn't show every extreme that they name: valid_frames[b] counts the leading latent frames of clip b that hold video; some clip has all 4. `tokenizer_slot`: every tokenizer slot encodes exactly one clip; some clip b takes the slot (b + 48) modulo 96.
All inputs are finite; a program needn't handle non-finite values.
Results may differ from a plain program's by a relative error of at most 0.012.
Values may be sent and summed in bfloat16 or wider, within the bound.
No kernel may reach another device: no remote copies, remote signals or barrier semaphores. Data moves between devices by JAX's collectives and lax.ppermute only.
A program may use at most 32 MiB of HBM per device.

v0:
```python
import math

import jax
import jax.numpy as jnp
from jax import lax
from jax.sharding import PartitionSpec as P


def passed_along(shard, axis, by):
    count = lax.axis_size(axis)
    pairs = [(i, i + by) for i in range(count) if 0 <= i + by < count]
    return lax.ppermute(shard, axis, pairs)


def causal_conv(frames, conv_w):
    earlier = passed_along(frames[1:2], "segment", 1)[0]
    total = jnp.einsum("rcx,xy->rcy", frames[1], conv_w[0], preferred_element_type=jnp.float32)
    total = total + jnp.einsum(
        "rcx,xy->rcy", frames[0], conv_w[1], preferred_element_type=jnp.float32
    )
    total = total + jnp.einsum(
        "rcx,xy->rcy", earlier, conv_w[2], preferred_element_type=jnp.float32
    )
    return jax.nn.silu(total).astype(jnp.bfloat16)


def masked_scores(queries, keys, keep, scale):
    scores = jnp.einsum("qhd,khd->hqk", queries, keys, preferred_element_type=jnp.float32) * scale
    return jnp.where(keep[None, None, :], scores, -jnp.inf)


def on_device(frames_in, valid_frames, tokenizer_slot, conv_w, embed_w, qkv_w, out_grad):
    act = causal_conv(frames_in[0], conv_w)
    row_dev, cols, channels = act.shape
    source = tokenizer_slot[0]
    piece = lax.all_gather(act[None], "mp", axis=0, tiled=True)
    start = jnp.int32(0)
    count = piece.shape[0]
    offset = jnp.clip(source, 0, count - 1)
    chosen = lax.dynamic_index_in_dim(piece, offset, 0, keepdims=False)
    inside = (source >= start) & (source < start + count)
    routed = jnp.where(inside, chosen, jnp.zeros_like(act))
    latent = lax.all_gather(routed[None], ("segment", "seq"), axis=0, tiled=True)
    n_seg = lax.axis_size("segment")
    n_seq = lax.axis_size("seq")
    latent = latent.reshape(n_seg, n_seq * row_dev, cols, channels)
    hidden = jnp.einsum(
        "frcx,xd->frcd", latent, embed_w, preferred_element_type=jnp.float32
    ).astype(jnp.bfloat16)
    partial_qkv = jnp.einsum("frcd,dhe->frche", hidden, qkv_w, preferred_element_type=jnp.float32)
    heads_local = qkv_w.shape[1]
    head_size = qkv_w.shape[2] // 3
    rows = n_seq * row_dev
    summed = lax.psum(partial_qkv, "seq").astype(jnp.bfloat16)
    begin = lax.axis_index("seq") * row_dev
    queries5 = lax.dynamic_slice_in_dim(summed[..., :head_size], begin, row_dev, 1)
    all_pair = summed[..., head_size:]
    scale = 1.0 / math.sqrt(head_size)
    n_query = n_seg * row_dev * cols
    n_key = n_seg * rows * cols
    q_flat = queries5.reshape(n_query, heads_local, head_size)
    keys = all_pair[..., :head_size].reshape(n_key, heads_local, head_size)
    values = all_pair[..., head_size:].reshape(n_key, heads_local, head_size)
    limit = valid_frames[0]
    keep = jnp.arange(n_key, dtype=jnp.int32) // (rows * cols) < limit
    scores = masked_scores(q_flat, keys, keep, scale)
    top = jnp.max(scores, axis=-1, keepdims=True)
    lse = top + jnp.log(jnp.sum(jnp.exp(scores - top), axis=-1, keepdims=True))
    prob = jnp.exp(scores - lse)
    prob_b = prob.astype(jnp.bfloat16)
    attn = jnp.einsum("hqk,khd->qhd", prob_b, values, preferred_element_type=jnp.float32).astype(
        jnp.bfloat16
    )
    grad = out_grad.reshape(n_query, heads_local, head_size)
    dprob = jnp.einsum("qhd,khd->hqk", grad, values, preferred_element_type=jnp.float32)
    delta = jnp.sum(grad.astype(jnp.float32) * attn.astype(jnp.float32), axis=-1).T
    dscore = (prob * (dprob - delta[:, :, None])).astype(jnp.bfloat16)
    q_grad = (
        jnp.einsum("hqk,khd->qhd", dscore, keys, preferred_element_type=jnp.float32) * scale
    ).astype(jnp.bfloat16)
    key_part = (
        jnp.einsum("hqk,qhd->khd", dscore, q_flat, preferred_element_type=jnp.float32) * scale
    )
    value_part = jnp.einsum("hqk,qhd->khd", prob_b, grad, preferred_element_type=jnp.float32)
    key_part = key_part.reshape(n_seg, rows, cols, heads_local, head_size)
    value_part = value_part.reshape(n_seg, rows, cols, heads_local, head_size)
    key_sum, value_sum = (
        lax.psum_scatter(
            key_part.astype(jnp.bfloat16), "seq", scatter_dimension=1, tiled=True
        ).astype(jnp.float32),
        lax.psum_scatter(
            value_part.astype(jnp.bfloat16), "seq", scatter_dimension=1, tiled=True
        ).astype(jnp.float32),
    )
    k_grad = key_sum.astype(jnp.bfloat16)
    v_grad = value_sum.astype(jnp.bfloat16)
    shape6 = (1, n_seg, row_dev, cols, heads_local, head_size)
    return (
        attn.reshape(shape6),
        q_grad.reshape(shape6),
        k_grad.reshape(shape6),
        v_grad.reshape(shape6),
    )


def solution(mesh):
    placed = (
        P("mp", "segment", "seq", None, None),
        P("mp"),
        P("mp"),
        P(),
        P(None, "seq"),
        P("seq", "segment", None),
        P("mp", None, "seq", None, "segment", None),
    )
    return jax.shard_map(
        on_device,
        mesh=mesh,
        in_specs=placed,
        out_specs=(
            P("mp", None, "seq", None, "segment", None),
            P("mp", None, "seq", None, "segment", None),
            P("mp", None, "seq", None, "segment", None),
            P("mp", None, "seq", None, "segment", None),
        ),
        check_vma=False,
    )
```

profile of v0, /device:TPU:1, one launch (start us, length us, event | category | flops | bytes accessed | tf_op | source)
XLA Modules:
  0.0 235.7 jit_solution(8530294283521246200)
XLA Ops:
  7.2 0.8 slice_bitcast_fusion
  8.0 3.9 %collective-permute-start = (bf16[1,2,24,128]{3,2,1,0:T(8,128)(2,1)S(1)}, bf16[1,2,24,128]{3,2,1,0:T(8,128)(2,1)S(1)}, u32[]{:S(2)}, u32[]{:S(2)}) collective-permute-start(bf16[1,2,24,128]{3,2,1,0:T(8,128)(2,1)S(1)} %slice_bitcast_fusion), channel_id=1, source_target_pairs={{0,192},{192,384},{384,576},{1,193},{193,385},{385,577},{2,194},{1... | collective-permute-start | bytes 36872 | tf_op jit(solution)/shard_map/ppermute | solution.py:12
  11.9 0.9 fusion.14
  12.8 0.9 convolution_add_fusion.1
  13.7 1.5 multiply_convert_fusion
  15.3 0.0 all-reduce.6.cloned.1.call-start
  16.6 1.0 copy.28
  17.6 120.3 %all-gather.3.cloned.1.call-done = bf16[192,24,128]{2,1,0:T(8,128)(2,1)} async-done(((bf16[2,24,128]{2,1,0:T(8,128)(2,1)}), bf16[192,24,128]{2,1,0:T(8,128)(2,1)}) %all-gather.3.cloned.1.call-update) | async-done | bytes 1179664 | tf_op jit(solution)/shard_map/all_gather | solution.py:36
  137.9 0.7 dynamic-slice_select_fusion
  138.6 21.2 %all_gather.7 = bf16[8,2,24,128]{3,2,1,0:T(8,128)(2,1)S(1)} all-gather(bf16[1,2,24,128]{3,2,1,0:T(8,128)(2,1)S(1)} %dynamic-slice_select_fusion), channel_id=1, replica_groups=mesh['segment'=4,'mp'=96,'seq'=2] {'segment','seq'}, dimensions={0}, use_global_device_ids=true | all-gather | bytes 110592 | tf_op jit(solution)/shard_map/all_gather | solution.py:43
  159.8 0.7 fusion.2
  160.5 8.4 %fusion = f32[4,4,24,5,384]{4,2,3,1,0:T(8,128)} fusion(bf16[4,4,24,2560,1]{3,2,4,1,0:T(8,128)(2,1)S(1)} %fusion.2, bf16[2560,5,384]{2,0,1:T(8,128)(2,1)} %param.12), kind=kOutput, calls=%fused_computation | convolution fusion | flops 3774873600 | bytes 14745600 | tf_op jit(solution)/shard_map/frcd,dhe->frche/dot_general | solution.py:50
  168.9 11.7 %all-reduce.7 = bf16[4,4,24,5,384]{4,2,3,1,0:T(8,128)(2,1)S(1)} all-reduce(f32[4,4,24,5,384]{4,2,3,1,0:T(8,128)} %fusion), channel_id=1, replica_groups=mesh['segment'=4,'mp'=96,'seq'=2] {'seq'}, use_global_device_ids=true, to_apply=%region_0.1 | all-reduce | flops 737280 | bytes 4423680 | tf_op jit(solution)/shard_map/psum | solution.py:54
  180.6 0.3 fusion.30
  180.9 0.1 copy.27
  181.0 0.5 fusion.31
  181.5 0.6 exponential_reduce_fusion
  182.0 0.8 convolution_convert_fusion.1
  182.8 0.8 copy.30
  183.7 0.1 copy.25
  183.7 0.5 multiply_reduce_fusion
  184.3 0.5 fusion.3
  184.8 0.4 fusion.6
  185.1 1.0 copy.29
  186.2 1.3 dynamic-slice
  188.1 0.4 fusion.7
  188.5 0.7 copy.32
  189.2 0.7 copy.31
  189.9 35.6 %all-reduce.6.cloned.1.call-done = (bf16[4,4,24,5,128]{4,2,1,0,3:T(8,128)(2,1)}, bf16[4,4,24,5,128]{4,2,3,1,0:T(8,128)(2,1)}) async-done(((bf16[4,4,24,5,128]{4,2,1,0,3:T(8,128)(2,1)}, bf16[4,4,24,5,128]{4,2,3,1,0:T(8,128)(2,1)}), (bf16[4,4,24,5,128]{4,2,1,0,3:T(8,128)(2,1)}, bf16[4,4,24,5,128]{4,2,3,1,0:T(8,128)(2,1)})) %all-reduce.6.cloned.1.call-update) | async-done | bytes 983056
  225.5 1.0 dynamic-slice_bitcast_fusion.1
  226.4 0.7 copy.33
  227.2 1.7 dynamic-slice_bitcast_fusion
  (10 shorter events, 0.2 us)
Async XLA Ops:
  7.2 152.6 %copy-start = (bf16[128,2560]{1,0:T(8,128)(2,1)S(1)}, bf16[128,2560]{1,0:T(8,128)(2,1)}, u32[]{:S(2)}) copy-start(bf16[128,2560]{1,0:T(8,128)(2,1)} %param.11) | copy-start | bytes 1966084
  7.2 130.7 %all-gather.3.cloned.1.call-start = ((), (), s32[]{:S(2)}) async-start(), calls=%async_computation | async-start | bytes 1191936 | tf_op jit(solution)/shard_map/all_gather | solution.py:36
  8.0 5.8 %collective-permute-start = (bf16[1,2,24,128]{3,2,1,0:T(8,128)(2,1)S(1)}, bf16[1,2,24,128]{3,2,1,0:T(8,128)(2,1)S(1)}, u32[]{:S(2)}, u32[]{:S(2)}) collective-permute-start(bf16[1,2,24,128]{3,2,1,0:T(8,128)(2,1)S(1)} %slice_bitcast_fusion), channel_id=1, source_target_pairs={{0,192},{192,384},{384,576},{1,193},{193,385},{385,577},{2,194},{1... | collective-permute-start | bytes 36872 | tf_op jit(solution)/shard_map/ppermute | solution.py:12
  15.3 210.2 %all-reduce.6.cloned.1.call-start = ((), (), s32[]{:S(2)}) async-start(), calls=%async_computation.1 | async-start | bytes 1966080
Sparse Core Ops, SparseCore 0:
  15.4 122.4 all-gather.2
  186.3 39.1 all-reduce.5
where the time goes:
time: 236 us
  waiting for transfers between devices  156 us (66%)
  blocking collectives  32.8 us (14%)
  between operations  16.1 us (7%)
  matrix products  15.4 us (7%)
  local copies, waits for them, and re-layouts  10.1 us (4%)
  starting transfers between devices  4 us (2%)
    all_gather x1, waiting for transfers between devices, on_device(): piece = lax.all_gather(act[None], 'mp', axis=0, tiled=True)  120 us
    unnamed x3, waiting for transfers between devices  35.6 us
    all_gather x1, blocking collectives, on_device(): lax.all_gather(routed[None], ('segment', 'seq'), axis=0, tiled=True)  21.2 us
    psum x1, blocking collectives, on_device(): summed = lax.psum(partial_qkv, 'seq').astype(jnp.bfloat16)  11.7 us
    dot_general x1, matrix products, on_device(): jnp.einsum('frcd,dhe->frche', hidden, qkv_w, preferred_element_type=jnp.f...  8.44 us
  transfers between devices with their start and end apart: 3, of which 2 were waited for; matrix products, arithmetic and copies ran while one was open for 2% of the time, Pallas kernels for 0%

commit v1 on v0

v1 whole, which is shorter than its diff:
```python
import math

import jax
import jax.numpy as jnp
import numpy as np
from jax import lax
from jax.sharding import Mesh
from jax.sharding import PartitionSpec as P

OUTER = "mp_outer"
INNER = "mp_inner"
MP = (OUTER, INNER)


def passed_along(shard, axis, by):
    count = lax.axis_size(axis)
    pairs = [(i, i + by) for i in range(count) if 0 <= i + by < count]
    return lax.ppermute(shard, axis, pairs)


def swap_seq(x):
    return lax.ppermute(x, "seq", [(0, 1), (1, 0)])


def causal_conv(frames, conv_w):
    earlier = passed_along(frames[1:2], "segment", 1)[0]
    total = jnp.einsum("rcx,xy->rcy", frames[1], conv_w[0], preferred_element_type=jnp.float32)
    total = total + jnp.einsum(
        "rcx,xy->rcy", frames[0], conv_w[1], preferred_element_type=jnp.float32
    )
    total = total + jnp.einsum(
        "rcx,xy->rcy", earlier, conv_w[2], preferred_element_type=jnp.float32
    )
    return jax.nn.silu(total).astype(jnp.bfloat16)


def route(act, tokenizer_slot):
    n_in = lax.axis_size(INNER)
    n_out = lax.axis_size(OUTER)
    my_out = lax.axis_index(OUTER)
    source = tokenizer_slot[0]
    row = lax.all_gather(act, INNER, axis=0)
    wanted = lax.all_gather(tokenizer_slot, OUTER, axis=0, tiled=True)
    pick = jnp.clip(wanted % n_in, 0, n_in - 1)
    mine = (wanted // n_in) == my_out
    send = jnp.take(row, pick, axis=0)
    send = jnp.where(mine.reshape((n_out,) + (1,) * act.ndim), send, jnp.zeros_like(send))
    got = lax.all_to_all(send, OUTER, 0, 0, tiled=True)
    origin = jnp.clip(source // n_in, 0, n_out - 1)
    return lax.dynamic_index_in_dim(got, origin, 0, keepdims=False)


def masked_scores(queries, keys, keep, scale):
    scores = jnp.einsum("qhd,khd->hqk", queries, keys, preferred_element_type=jnp.float32) * scale
    return jnp.where(keep[None, None, :], scores, -jnp.inf)


def on_device(frames_in, valid_frames, tokenizer_slot, conv_w, embed_w, qkv_w, out_grad):
    act = causal_conv(frames_in[0], conv_w)
    row_dev, cols, channels = act.shape
    routed = route(act, tokenizer_slot)
    latent = lax.all_gather(routed[None], ("segment", "seq"), axis=0, tiled=True)
    n_seg = lax.axis_size("segment")
    n_seq = lax.axis_size("seq")
    latent = latent.reshape(n_seg, n_seq * row_dev, cols, channels)
    hidden = jnp.einsum(
        "frcx,xd->frcd", latent, embed_w, preferred_element_type=jnp.float32
    ).astype(jnp.bfloat16)
    partial_qkv = jnp.einsum("frcd,dhe->frche", hidden, qkv_w, preferred_element_type=jnp.float32)
    heads_local = qkv_w.shape[1]
    head_size = qkv_w.shape[2] // 3
    rows = n_seq * row_dev
    me = lax.axis_index("seq")
    other = 1 - me
    own_part = lax.dynamic_slice_in_dim(partial_qkv, me * row_dev, row_dev, 1)
    sent_part = lax.dynamic_slice_in_dim(partial_qkv, other * row_dev, row_dev, 1)
    own_qkv = (own_part + swap_seq(sent_part)).astype(jnp.bfloat16)
    own_pair = own_qkv[..., head_size:]
    other_pair = swap_seq(own_pair)
    all_pair = jnp.concatenate([own_pair, other_pair], axis=1)
    queries5 = own_qkv[..., :head_size]
    scale = 1.0 / math.sqrt(head_size)
    n_query = n_seg * row_dev * cols
    n_key = n_seg * rows * cols
    q_flat = queries5.reshape(n_query, heads_local, head_size)
    keys = all_pair[..., :head_size].reshape(n_key, heads_local, head_size)
    values = all_pair[..., head_size:].reshape(n_key, heads_local, head_size)
    limit = valid_frames[0]
    keep = jnp.arange(n_key, dtype=jnp.int32) // (rows * cols) < limit
    scores = masked_scores(q_flat, keys, keep, scale)
    top = jnp.max(scores, axis=-1, keepdims=True)
    lse = top + jnp.log(jnp.sum(jnp.exp(scores - top), axis=-1, keepdims=True))
    prob = jnp.exp(scores - lse)
    prob_b = prob.astype(jnp.bfloat16)
    attn = jnp.einsum("hqk,khd->qhd", prob_b, values, preferred_element_type=jnp.float32).astype(
        jnp.bfloat16
    )
    grad = out_grad.reshape(n_query, heads_local, head_size)
    dprob = jnp.einsum("qhd,khd->hqk", grad, values, preferred_element_type=jnp.float32)
    delta = jnp.sum(grad.astype(jnp.float32) * attn.astype(jnp.float32), axis=-1).T
    dscore = (prob * (dprob - delta[:, :, None])).astype(jnp.bfloat16)
    q_grad = (
        jnp.einsum("hqk,khd->qhd", dscore, keys, preferred_element_type=jnp.float32) * scale
    ).astype(jnp.bfloat16)
    key_part = (
        jnp.einsum("hqk,qhd->khd", dscore, q_flat, preferred_element_type=jnp.float32) * scale
    ).astype(jnp.bfloat16)
    value_part = jnp.einsum(
        "hqk,qhd->khd", prob_b, grad, preferred_element_type=jnp.float32
    ).astype(jnp.bfloat16)
    kv_part = jnp.stack([key_part, value_part]).reshape(
        2, n_seg, 2, row_dev, cols, heads_local, head_size
    )
    kv_sum = kv_part[:, :, 0].astype(jnp.float32) + swap_seq(kv_part[:, :, 1]).astype(jnp.float32)
    kv_sum = kv_sum.astype(jnp.bfloat16)
    k_grad = kv_sum[0]
    v_grad = kv_sum[1]
    shape6 = (1, n_seg, row_dev, cols, heads_local, head_size)
    return (
        attn.reshape(shape6),
        q_grad.reshape(shape6),
        k_grad.reshape(shape6),
        v_grad.reshape(shape6),
    )


def inner_size(mesh):
    column = np.asarray(mesh.devices)[0, :, 0]
    try:
        count = len({d.coords[1] for d in column})
    except AttributeError:
        count = 1
    if count < 1 or column.size % count:
        count = 1
    return count


def solution(mesh):
    devices = np.asarray(mesh.devices)
    n_seg, n_mp, n_seq = devices.shape
    n_in = inner_size(mesh)
    split = Mesh(
        devices.reshape(n_seg, n_mp // n_in, n_in, n_seq), ("segment", OUTER, INNER, "seq")
    )
    placed = (
        P(MP, "segment", "seq", None, None),
        P(MP),
        P(MP),
        P(),
        P(None, "seq"),
        P("seq", "segment", None),
        P(MP, None, "seq", None, "segment", None),
    )
    out = P(MP, None, "seq", None, "segment", None)
    return jax.shard_map(
        on_device,
        mesh=split,
        in_specs=placed,
        out_specs=(out, out, out, out),
        check_vma=False,
    )
```

time: 236 us -> 132 us (0.56)
  waiting for transfers between devices: 156 us -> 15.2 us
  blocking collectives: 32.8 us -> 74.2 us
  between operations: 16.1 us -> 2.3 us
  starting transfers between devices: 4 us -> 13.8 us
  other arithmetic: 1.31 us -> 3.68 us
    all_gather x1 -> x0, waiting for transfers between devices: 120 us -> none  [on_device(): piece = lax.all_gather(act[None], 'mp', axis=0, tiled=True)]
    unnamed x3 -> x0, waiting for transfers between devices: 35.6 us -> none
    unnamed x0 -> x1, blocking collectives: none -> 27.8 us
    all_gather x0 -> x1, blocking collectives: none -> 19.8 us  [route(): row = lax.all_gather(act, INNER, axis=0)]
    psum x1 -> x0, blocking collectives: 11.7 us -> none  [on_device(): summed = lax.psum(partial_qkv, 'seq').astype(jnp.bfloat16)]
    all_to_all x0 -> x1, waiting for transfers between devices: none -> 11.1 us  [route(): got = lax.all_to_all(send, OUTER, 0, 0, tiled=True)]
    ppermute x0 -> x3, starting transfers between devices: none -> 6.34 us  [swap_seq(): return lax.ppermute(x, 'seq', [(0, 1), (1, 0)])]
    all_gather x1, blocking collectives: 21.2 us -> 26.5 us  [on_device(): lax.all_gather(routed[None], ('segment', 'seq'), axis=0, tiled=True)]
  transfers between devices with their start and end apart: 3 -> 5, of which waited for: 2 -> 3; matrix products, arithmetic and copies ran while one was open for 2% -> 3% of each run, Pallas kernels for 0% -> 0%
where the time goes in v1:
time: 132 us; the launch traced here: 131 us
  blocking collectives  74.2 us (56%)
  waiting for transfers between devices  15.2 us (12%)
  matrix products  13.9 us (11%)
  starting transfers between devices  13.8 us (10%)
  local copies, waits for them, and re-layouts  8.36 us (6%)
  other arithmetic  3.68 us (3%)
  between operations  2.3 us (2%)
    unnamed x1, blocking collectives  27.8 us
    all_gather x1, blocking collectives, on_device(): lax.all_gather(routed[None], ('segment', 'seq'), axis=0, tiled=True)  26.5 us
    all_gather x1, blocking collectives, route(): row = lax.all_gather(act, INNER, axis=0)  19.8 us
    all_to_all x1, waiting for transfers between devices, route(): got = lax.all_to_all(send, OUTER, 0, 0, tiled=True)  11.1 us
    dot_general x1, matrix products, on_device(): jnp.einsum('frcd,dhe->frche', hidden, qkv_w, preferred_element_type=jnp.f...  6.87 us
    unnamed x16, local copies, waits for them, and re-layouts  6.42 us
    ppermute x3, starting transfers between devices, swap_seq(): return lax.ppermute(x, 'seq', [(0, 1), (1, 0)])  6.34 us
    ppermute x3, waiting for transfers between devices, swap_seq(): return lax.ppermute(x, 'seq', [(0, 1), (1, 0)])  4.08 us
  transfers between devices with their start and end apart: 5, of which 3 were waited for; matrix products, arithmetic and copies ran while one was open for 3% of the time, Pallas kernels for 0%

profile of v1, /device:TPU:1, one launch (start us, length us, event | category | flops | bytes accessed | tf_op | source)
XLA Modules:
  0.0 131.4 jit_solution(11743080781997917192)
XLA Ops:
  1.4 0.7 slice_bitcast_fusion
  2.1 1.3 dynamic-slice
  3.3 0.8 dynamic-update-slice
  4.1 3.9 %collective-permute-start = (bf16[1,2,24,128]{3,2,1,0:T(8,128)(2,1)S(1)}, bf16[1,2,24,128]{3,2,1,0:T(8,128)(2,1)S(1)}, u32[]{:S(2)}, u32[]{:S(2)}) collective-permute-start(bf16[1,2,24,128]{3,2,1,0:T(8,128)(2,1)S(1)} %slice_bitcast_fusion), channel_id=1, source_target_pairs={{0,192},{192,384},{384,576},{1,193},{193,385},{385,577},{2,194},{1... | collective-permute-start | bytes 36872 | tf_op jit(solution)/shard_map/ppermute | solution.py:18
  8.0 27.8 %all-reduce = s32[12]{0:T(128)S(1)} all-reduce(s32[12]{0:T(128)S(1)} %dynamic-update-slice), channel_id=1, replica_groups=mesh['segment'=4,'mp_outer'=12,'mp_inner'=8,'seq'=2] {'mp_outer'}, use_global_device_ids=true, to_apply=%add | all-reduce | flops 12 | bytes 96
  35.9 0.9 fusion.19
  36.8 0.9 convolution_add_fusion.1
  37.7 0.9 multiply_convert_fusion
  38.7 19.8 %all-gather = bf16[16,24,128]{2,1,0:T(8,128)(2,1)S(1)} all-gather(bf16[2,24,128]{2,1,0:T(8,128)(2,1)S(1)} %multiply_convert_fusion), channel_id=2, replica_groups=mesh['segment'=4,'mp_outer'=12,'mp_inner'=8,'seq'=2] {'mp_inner'}, dimensions={0}, use_global_device_ids=true | all-gather | bytes 110592 | tf_op jit(solution)/shard_map/all_gather | solution.py:42
  58.5 0.6 gather_fusion
  59.1 0.8 select_select_fusion
  59.8 3.5 %all-to-all-start = ((bf16[12,2,24,128]{3,2,1,0:T(8,128)(2,1)}), bf16[12,2,24,128]{3,2,1,0:T(8,128)(2,1)S(1)}, u32[]{:S(2)}, u32[]{:S(2)}) async-start(bf16[12,2,24,128]{3,2,1,0:T(8,128)(2,1)} %select_select_fusion), calls=%async_computation | async-start | bytes 294912 | tf_op jit(solution)/shard_map/all_to_all | solution.py:48
  63.4 11.1 %all-to-all-done = bf16[12,2,24,128]{3,2,1,0:T(8,128)(2,1)S(1)} async-done(((bf16[12,2,24,128]{3,2,1,0:T(8,128)(2,1)}), bf16[12,2,24,128]{3,2,1,0:T(8,128)(2,1)S(1)}, u32[]{:S(2)}, u32[]{:S(2)}) %all-to-all-start) | async-done | bytes 147488 | tf_op jit(solution)/shard_map/all_to_all | solution.py:48
  74.5 26.5 %all_gather.15 = bf16[8,2,24,128]{3,2,1,0:T(8,128)(2,1)S(1)} all-gather(bf16[1,2,24,128]{3,2,1,0:T(8,128)(2,1)S(1)} %constant_dynamic-slice_fusion.1), channel_id=1, replica_groups=mesh['segment'=4,'mp_outer'=12,'mp_inner'=8,'seq'=2] {'segment','seq'}, dimensions={0}, use_global_device_ids=true | all-gather | bytes 110592 | tf_op jit(solution)/shard_map/all_gather | solution.py:62
  101.1 0.7 fusion.2
  101.7 6.9 %fusion = f32[4,4,24,5,384]{4,2,3,1,0:T(8,128)S(1)} fusion(bf16[4,4,24,2560,1]{3,2,4,1,0:T(8,128)(2,1)S(1)} %fusion.2, bf16[2560,5,384]{2,0,1:T(8,128)(2,1)} %param.12), kind=kOutput, calls=%fused_computation.1 | convolution fusion | flops 3774873600 | bytes 14745600 | tf_op jit(solution)/shard_map/frcd,dhe->frche/dot_general | solution.py:69
  108.7 1.5 %copy-done.1 = f32[4,4,24,5,384]{4,2,3,1,0:T(8,128)} copy-done((f32[4,4,24,5,384]{4,2,3,1,0:T(8,128)}, f32[4,4,24,5,384]{4,2,3,1,0:T(8,128)S(1)}, u32[]{:S(2)}) %copy-start.1) | copy-done | bytes 2949144
  110.2 2.1 %collective-permute-start.1 = (f32[4,2,24,5,384]{4,2,3,1,0:T(8,128)S(1)}, f32[4,2,24,5,384]{4,2,3,1,0:T(8,128)}, u32[]{:S(2)}, u32[]{:S(2)}) collective-permute-start(f32[4,2,24,5,384]{4,2,3,1,0:T(8,128)S(1)} %constant_dynamic-slice_fusion), channel_id=1, source_target_pairs={{0,1},{1,0},{2,3},{3,2},{4,5},{5,4},{6,7},{7,6},{8,9},{9,8},{10,11... | collective-permute-start | bytes 4423688 | tf_op jit(solution)/shard_map/ppermute | solution.py:22
  112.3 3.2 %collective-permute-done.1 = f32[4,2,24,5,384]{4,2,3,1,0:T(8,128)} collective-permute-done((f32[4,2,24,5,384]{4,2,3,1,0:T(8,128)S(1)}, f32[4,2,24,5,384]{4,2,3,1,0:T(8,128)}, u32[]{:S(2)}, u32[]{:S(2)}) %collective-permute-start.1) | collective-permute-done | bytes 1474592 | tf_op jit(solution)/shard_map/ppermute | solution.py:22
  115.5 2.0 %add_convert_fusion = bf16[4,2,24,5,384]{4,2,3,1,0:T(8,128)(2,1)S(1)} fusion(f32[4,2,24,5,384]{4,2,3,1,0:T(8,128)} %collective-permute-done.1, f32[4,4,24,5,384]{4,2,3,1,0:T(8,128)} %copy-done.1, s32[]{:T(128)S(6)} %select_n.55), kind=kLoop, calls=%fused_computation.10 | loop fusion | flops 737280 | bytes 3686404 | tf_op jit(solution)/shard_map/convert_element_type | solution.py:77
  117.5 2.1 %collective-permute-start.2 = (bf16[4,2,24,5,256]{4,2,3,1,0:T(8,128)(2,1)S(1)}, bf16[4,2,24,5,256]{4,2,3,1,0:T(8,128)(2,1)S(1)}, u32[]{:S(2)}, u32[]{:S(2)}) collective-permute-start(bf16[4,2,24,5,256]{4,2,3,1,0:T(8,128)(2,1)S(1)} %slice.61), channel_id=1, source_target_pairs={{0,1},{1,0},{2,3},{3,2},{4,5},{5,4},{6,7},{7,6},{8,9},{9,8},{10,11... | collective-permute-start | bytes 1474568 | tf_op jit(solution)/shard_map/ppermute | solution.py:22
  120.4 0.9 collective-permute-done.2
  121.5 0.5 fusion.38
  122.0 0.6 exponential_reduce_fusion
  122.6 0.8 convolution_convert_fusion.1
  123.4 1.1 multiply_reduce_fusion
  124.5 0.5 fusion.3
  125.7 2.2 %collective-permute-start.3 = (bf16[2,4,2,24,5,128]{5,3,2,1,4,0:T(8,128)(2,1)S(1)}, bf16[2,4,2,24,5,128]{5,3,2,1,4,0:T(8,128)(2,1)S(1)}, u32[]{:S(2)}, u32[]{:S(2)}) collective-permute-start(bf16[2,4,2,24,5,128]{5,3,2,1,4,0:T(8,128)(2,1)S(1)} %fusion.13), channel_id=1, source_target_pairs={{0,1},{1,0},{2,3},{3,2},{4,5},{5,4},{6,7},{7,6},{8,9},{9,8},{10,11... | collective-permute-start | bytes 1474568 | tf_op jit(solution)/shard_map/ppermute | solution.py:22
  128.3 0.7 copy.33
  129.0 0.7 copy.32
  129.9 0.7 copy.34
  130.7 0.7 copy.35
  (29 shorter events, 1.8 us)
Async XLA Ops:
  0.6 100.4 %copy-start = (bf16[128,2560]{1,0:T(8,128)(2,1)S(1)}, bf16[128,2560]{1,0:T(8,128)(2,1)}, u32[]{:S(2)}) copy-start(bf16[128,2560]{1,0:T(8,128)(2,1)} %param.11) | copy-start | bytes 1966084
  4.1 33.6 %collective-permute-start = (bf16[1,2,24,128]{3,2,1,0:T(8,128)(2,1)S(1)}, bf16[1,2,24,128]{3,2,1,0:T(8,128)(2,1)S(1)}, u32[]{:S(2)}, u32[]{:S(2)}) collective-permute-start(bf16[1,2,24,128]{3,2,1,0:T(8,128)(2,1)S(1)} %slice_bitcast_fusion), channel_id=1, source_target_pairs={{0,192},{192,384},{384,576},{1,193},{193,385},{385,577},{2,194},{1... | collective-permute-start | bytes 36872 | tf_op jit(solution)/shard_map/ppermute | solution.py:18
  59.8 14.7 %all-to-all-start = ((bf16[12,2,24,128]{3,2,1,0:T(8,128)(2,1)}), bf16[12,2,24,128]{3,2,1,0:T(8,128)(2,1)S(1)}, u32[]{:S(2)}, u32[]{:S(2)}) async-start(bf16[12,2,24,128]{3,2,1,0:T(8,128)(2,1)} %select_select_fusion), calls=%async_computation | async-start | bytes 294912 | tf_op jit(solution)/shard_map/all_to_all | solution.py:48
  108.6 1.6 %copy-start.1 = (f32[4,4,24,5,384]{4,2,3,1,0:T(8,128)}, f32[4,4,24,5,384]{4,2,3,1,0:T(8,128)S(1)}, u32[]{:S(2)}) copy-start(f32[4,4,24,5,384]{4,2,3,1,0:T(8,128)S(1)} %fusion) | copy-start | bytes 8847364
  110.2 5.3 %collective-permute-start.1 = (f32[4,2,24,5,384]{4,2,3,1,0:T(8,128)S(1)}, f32[4,2,24,5,384]{4,2,3,1,0:T(8,128)}, u32[]{:S(2)}, u32[]{:S(2)}) collective-permute-start(f32[4,2,24,5,384]{4,2,3,1,0:T(8,128)S(1)} %constant_dynamic-slice_fusion), channel_id=1, source_target_pairs={{0,1},{1,0},{2,3},{3,2},{4,5},{5,4},{6,7},{7,6},{8,9},{9,8},{10,11... | collective-permute-start | bytes 4423688 | tf_op jit(solution)/shard_map/ppermute | solution.py:22
  112.3 7.9 %copy-start.3 = (bf16[1,4,2,24,5,128]{5,3,4,2,1,0:T(8,128)(2,1)S(1)}, bf16[1,4,2,24,5,128]{5,3,4,2,1,0:T(8,128)(2,1)}, u32[]{:S(2)}) copy-start(bf16[1,4,2,24,5,128]{5,3,4,2,1,0:T(8,128)(2,1)} %param.13) | copy-start | bytes 737284
  117.5 3.8 %collective-permute-start.2 = (bf16[4,2,24,5,256]{4,2,3,1,0:T(8,128)(2,1)S(1)}, bf16[4,2,24,5,256]{4,2,3,1,0:T(8,128)(2,1)S(1)}, u32[]{:S(2)}, u32[]{:S(2)}) collective-permute-start(bf16[4,2,24,5,256]{4,2,3,1,0:T(8,128)(2,1)S(1)} %slice.61), channel_id=1, source_target_pairs={{0,1},{1,0},{2,3},{3,2},{4,5},{5,4},{6,7},{7,6},{8,9},{9,8},{10,11... | collective-permute-start | bytes 1474568 | tf_op jit(solution)/shard_map/ppermute | solution.py:22
  125.7 3.4 %copy-start.2 = (bf16[5,128,192]{1,2,0:T(8,128)(2,1)S(1)}, bf16[5,128,192]{1,2,0:T(8,128)(2,1)}, u32[]{:S(2)}) copy-start(bf16[5,128,192]{1,2,0:T(8,128)(2,1)} %get-tuple-element.26) | copy-start | bytes 737284
  125.7 4.0 %collective-permute-start.3 = (bf16[2,4,2,24,5,128]{5,3,2,1,4,0:T(8,128)(2,1)S(1)}, bf16[2,4,2,24,5,128]{5,3,2,1,4,0:T(8,128)(2,1)S(1)}, u32[]{:S(2)}, u32[]{:S(2)}) collective-permute-start(bf16[2,4,2,24,5,128]{5,3,2,1,4,0:T(8,128)(2,1)S(1)} %fusion.13), channel_id=1, source_target_pairs={{0,1},{1,0},{2,3},{3,2},{4,5},{5,4},{6,7},{7,6},{8,9},{9,8},{10,11... | collective-permute-start | bytes 1474568 | tf_op jit(solution)/shard_map/ppermute | solution.py:22

commit v2 on v1

--- a/solution.py
+++ b/solution.py
@@ -34,14 +34,36 @@
     return jax.nn.silu(total).astype(jnp.bfloat16)
 
 
+def gather_rotated(x, axis):
+    n = lax.axis_size(axis)
+    have = x[None]
+    shift = 1
+    while have.shape[0] < n:
+        need = min(have.shape[0], n - have.shape[0])
+        pairs = [(j, (j - shift) % n) for j in range(n)]
+        have = jnp.concatenate([have, lax.ppermute(have[:need], axis, pairs)], axis=0)
+        shift *= 2
+    return have
+
+
+def gather_ordered(x, axis):
+    n = lax.axis_size(axis)
+    have = gather_rotated(x, axis)
+    if n == 1:
+        return have
+    me = lax.axis_index(axis)
+    return jnp.take(have, (jnp.arange(n) - me) % n, axis=0)
+
+
 def route(act, tokenizer_slot):
     n_in = lax.axis_size(INNER)
     n_out = lax.axis_size(OUTER)
     my_out = lax.axis_index(OUTER)
+    my_in = lax.axis_index(INNER)
     source = tokenizer_slot[0]
-    row = lax.all_gather(act, INNER, axis=0)
-    wanted = lax.all_gather(tokenizer_slot, OUTER, axis=0, tiled=True)
-    pick = jnp.clip(wanted % n_in, 0, n_in - 1)
+    row = gather_rotated(act, INNER)
+    wanted = gather_ordered(tokenizer_slot, OUTER)[:, 0]
+    pick = (wanted % n_in - my_in) % n_in
     mine = (wanted // n_in) == my_out
     send = jnp.take(row, pick, axis=0)
     send = jnp.where(mine.reshape((n_out,) + (1,) * act.ndim), send, jnp.zeros_like(send))
@@ -59,22 +81,22 @@
     act = causal_conv(frames_in[0], conv_w)
     row_dev, cols, channels = act.shape
     routed = route(act, tokenizer_slot)
-    latent = lax.all_gather(routed[None], ("segment", "seq"), axis=0, tiled=True)
     n_seg = lax.axis_size("segment")
     n_seq = lax.axis_size("seq")
-    latent = latent.reshape(n_seg, n_seq * row_dev, cols, channels)
-    hidden = jnp.einsum(
-        "frcx,xd->frcd", latent, embed_w, preferred_element_type=jnp.float32
-    ).astype(jnp.bfloat16)
-    partial_qkv = jnp.einsum("frcd,dhe->frche", hidden, qkv_w, preferred_element_type=jnp.float32)
+    pair = gather_rotated(routed, "seq")
+    latent = gather_ordered(pair, "segment")
     heads_local = qkv_w.shape[1]
     head_size = qkv_w.shape[2] // 3
     rows = n_seq * row_dev
-    me = lax.axis_index("seq")
-    other = 1 - me
-    own_part = lax.dynamic_slice_in_dim(partial_qkv, me * row_dev, row_dev, 1)
-    sent_part = lax.dynamic_slice_in_dim(partial_qkv, other * row_dev, row_dev, 1)
-    own_qkv = (own_part + swap_seq(sent_part)).astype(jnp.bfloat16)
+
+    def project(piece):
+        hidden = jnp.einsum(
+            "frcx,xd->frcd", piece, embed_w, preferred_element_type=jnp.float32
+        ).astype(jnp.bfloat16)
+        return jnp.einsum("frcd,dhe->frche", hidden, qkv_w, preferred_element_type=jnp.float32)
+
+    received = swap_seq(project(latent[:, 1]))
+    own_qkv = (project(latent[:, 0]) + received).astype(jnp.bfloat16)
     own_pair = own_qkv[..., head_size:]
     other_pair = swap_seq(own_pair)
     all_pair = jnp.concatenate([own_pair, other_pair], axis=1)

time: 132 us -> 141 us (1.068)
  blocking collectives: 74.2 us -> 0 us
  starting transfers between devices: 13.8 us -> 79.3 us
  waiting for transfers between devices: 15.2 us -> 27.8 us
  matrix products: 13.9 us -> 20 us
  local copies, waits for them, and re-layouts: 8.36 us -> 6.7 us
    ppermute x0 -> x10, starting transfers between devices: none -> 59.1 us  [gather_rotated(): lax.ppermute(have[:need], axis, pairs)]
    all_gather x2 -> x0, blocking collectives: 46.3 us -> none  [the longest x1 26.5 us: on_device(): lax.all_gather(routed[None], ('segment', 'seq'), axis=0, tiled=True)]
    unnamed x1 -> x0, blocking collectives: 27.8 us -> none
    ppermute x0 -> x10, waiting for transfers between devices: none -> 13.4 us  [gather_rotated(): lax.ppermute(have[:need], axis, pairs)]
    dot_general x2, matrix products: 7.53 us -> 13.6 us  [project(): jnp.einsum('frcd,dhe->frche', hidden, qkv_w, preferred_element_type=jnp.f...]
    all_to_all x1, starting transfers between devices: 3.52 us -> 7.82 us  [route(): got = lax.all_to_all(send, OUTER, 0, 0, tiled=True)]
    unnamed x16 -> x11, local copies, waits for them, and re-layouts: 6.42 us -> 2.92 us
    ppermute x3, starting transfers between devices: 6.34 us -> 9.35 us  [swap_seq(): return lax.ppermute(x, 'seq', [(0, 1), (1, 0)])]
  transfers between devices with their start and end apart: 5 -> 15, of which waited for: 3 -> 11; matrix products, arithmetic and copies ran while one was open for 3% -> 5% of each run, Pallas kernels for 0% -> 0%
where the time goes in v2:
time: 141 us; the launch traced here: 140 us
  starting transfers between devices  79.3 us (56%)
  waiting for transfers between devices  27.8 us (20%)
  matrix products  20 us (14%)
  local copies, waits for them, and re-layouts  6.7 us (5%)
  other arithmetic  3.38 us (2%)
  between operations  2.34 us (2%)
    ppermute x10, starting transfers between devices, gather_rotated(): lax.ppermute(have[:need], axis, pairs)  59.1 us
    dot_general x2, matrix products, project(): jnp.einsum('frcd,dhe->frche', hidden, qkv_w, preferred_element_type=jnp.f...  13.6 us
    ppermute x10, waiting for transfers between devices, gather_rotated(): lax.ppermute(have[:need], axis, pairs)  13.4 us
    all_to_all x1, waiting for transfers between devices, route(): got = lax.all_to_all(send, OUTER, 0, 0, tiled=True)  10.7 us
    ppermute x3, starting transfers between devices, swap_seq(): return lax.ppermute(x, 'seq', [(0, 1), (1, 0)])  9.35 us
    all_to_all x1, starting transfers between devices, route(): got = lax.all_to_all(send, OUTER, 0, 0, tiled=True)  7.82 us
    ppermute x3, waiting for transfers between devices, swap_seq(): return lax.ppermute(x, 'seq', [(0, 1), (1, 0)])  3.76 us
    ppermute x1, starting transfers between devices, passed_along(): return lax.ppermute(shard, axis, pairs)  3.1 us
  transfers between devices with their start and end apart: 15, of which 11 were waited for; matrix products, arithmetic and copies ran while one was open for 5% of the time, Pallas kernels for 0%

profile of v2, /device:TPU:1, one launch (start us, length us, event | category | flops | bytes accessed | tf_op | source)
XLA Modules:
  0.0 139.6 jit_solution(15276125609801122471)
XLA Ops:
  0.6 15.3 %collective-permute-start = (s32[1,1]{0,1:T(1,128)}, s32[1,1]{0,1:T(1,128)}, u32[]{:S(2)}, u32[]{:S(2)}) collective-permute-start(s32[1,1]{0,1:T(1,128)} %bitcast), channel_id=1, source_target_pairs={{0,176},{16,0},{32,16},{48,32},{64,48},{80,64},{96,80},{112,96},{1... | collective-permute-start | bytes 20 | tf_op jit(solution)/shard_map/ppermute | solution.py:44
  16.6 3.1 %collective-permute-start.4 = (bf16[1,2,24,128]{3,2,1,0:T(8,128)(2,1)S(1)}, bf16[1,2,24,128]{3,2,1,0:T(8,128)(2,1)S(1)}, u32[]{:S(2)}, u32[]{:S(2)}) collective-permute-start(bf16[1,2,24,128]{3,2,1,0:T(8,128)(2,1)S(1)} %slice_bitcast_fusion.6), channel_id=1, source_target_pairs={{0,192},{192,384},{384,576},{1,193},{193,385},{385,577},{2,194},{1... | collective-permute-start | bytes 36872 | tf_op jit(solution)/shard_map/ppermute | solution.py:18
  20.4 0.9 fusion.28
  21.3 0.9 convolution_add_fusion.1
  23.0 2.2 %collective-permute-start.1 = (s32[2,1]{0,1:T(1,128)S(1)}, s32[2,1]{0,1:T(1,128)S(1)}, u32[]{:S(2)}, u32[]{:S(2)}) collective-permute-start(s32[2,1]{0,1:T(1,128)S(1)} %pad_add_fusion), channel_id=1, source_target_pairs={{0,160},{16,176},{32,0},{48,16},{64,32},{80,48},{96,64},{112,80},{... | collective-permute-start | bytes 32 | tf_op jit(solution)/shard_map/ppermute | solution.py:44
  25.1 3.0 %collective-permute-done.1 = s32[2,1]{0,1:T(1,128)S(1)} collective-permute-done((s32[2,1]{0,1:T(1,128)S(1)}, s32[2,1]{0,1:T(1,128)S(1)}, u32[]{:S(2)}, u32[]{:S(2)}) %collective-permute-start.1) | collective-permute-done | bytes 40 | tf_op jit(solution)/shard_map/ppermute | solution.py:44
  28.8 1.9 %collective-permute-start.3 = (s32[4,1]{0,1:T(1,128)S(1)}, s32[4,1]{0,1:T(1,128)S(1)}, u32[]{:S(2)}, u32[]{:S(2)}) collective-permute-start(s32[4,1]{0,1:T(1,128)S(1)} %pad_add_fusion.1), channel_id=1, source_target_pairs={{0,64},{16,80},{32,96},{48,112},{64,128},{80,144},{96,160},{112,17... | collective-permute-start | bytes 56 | tf_op jit(solution)/shard_map/ppermute | solution.py:44
  30.8 7.3 %collective-permute-start.2 = (s32[4,1]{0,1:T(1,128)S(1)}, s32[4,1]{0,1:T(1,128)S(1)}, u32[]{:S(2)}, u32[]{:S(2)}) collective-permute-start(s32[4,1]{0,1:T(1,128)S(1)} %pad_add_fusion.1), channel_id=1, source_target_pairs={{0,128},{16,144},{32,160},{48,176},{64,0},{80,16},{96,32},{112,48}... | collective-permute-start | bytes 56 | tf_op jit(solution)/shard_map/ppermute | solution.py:44
  38.1 0.9 collective-permute-done.2
  40.4 0.9 fusion.35
  41.3 5.1 %collective-permute-start.5 = (bf16[1,2,24,128]{3,2,1,0:T(8,128)(2,1)S(1)}, bf16[1,2,24,128]{3,2,1,0:T(8,128)(2,1)S(1)}, u32[]{:S(2)}, u32[]{:S(2)}) collective-permute-start(bf16[1,2,24,128]{3,2,1,0:T(8,128)(2,1)S(1)} %fusion.35), channel_id=1, source_target_pairs={{0,14},{2,0},{4,2},{6,4},{8,6},{10,8},{12,10},{14,12},{1,15},{3,1}... | collective-permute-start | bytes 36872 | tf_op jit(solution)/shard_map/ppermute | solution.py:44
  46.5 0.8 collective-permute-done.5
  47.3 4.4 %collective-permute-start.6 = (bf16[2,2,24,128]{3,2,1,0:T(8,128)(2,1)S(1)}, bf16[2,2,24,128]{3,2,1,0:T(8,128)(2,1)S(1)}, u32[]{:S(2)}, u32[]{:S(2)}) collective-permute-start(bf16[2,2,24,128]{3,2,1,0:T(8,128)(2,1)S(1)} %pad_maximum_fusion.6), channel_id=1, source_target_pairs={{0,12},{2,14},{4,0},{6,2},{8,4},{10,6},{12,8},{14,10},{1,13},{3,15... | collective-permute-start | bytes 73736 | tf_op jit(solution)/shard_map/ppermute | solution.py:44
  51.7 1.0 collective-permute-done.6
  52.7 6.2 %collective-permute-start.7 = (bf16[4,2,24,128]{3,2,1,0:T(8,128)(2,1)S(1)}, bf16[4,2,24,128]{3,2,1,0:T(8,128)(2,1)S(1)}, u32[]{:S(2)}, u32[]{:S(2)}) collective-permute-start(bf16[4,2,24,128]{3,2,1,0:T(8,128)(2,1)S(1)} %pad_maximum_fusion.4), channel_id=1, source_target_pairs={{0,8},{2,10},{4,12},{6,14},{8,0},{10,2},{12,4},{14,6},{1,9},{3,11}... | collective-permute-start | bytes 147464 | tf_op jit(solution)/shard_map/ppermute | solution.py:44
  59.0 2.6 %collective-permute-done.7 = bf16[4,2,24,128]{3,2,1,0:T(8,128)(2,1)S(1)} collective-permute-done((bf16[4,2,24,128]{3,2,1,0:T(8,128)(2,1)S(1)}, bf16[4,2,24,128]{3,2,1,0:T(8,128)(2,1)S(1)}, u32[]{:S(2)}, u32[]{:S(2)}) %collective-permute-start.7) | collective-permute-done | bytes 49184 | tf_op jit(solution)/shard_map/ppermute | solution.py:44
  62.9 7.8 %all-to-all-start = ((bf16[12,2,24,128]{3,2,1,0:T(8,128)(2,1)}), bf16[12,2,24,128]{3,2,1,0:T(8,128)(2,1)S(1)}, u32[]{:S(2)}, u32[]{:S(2)}) async-start(bf16[12,2,24,128]{3,2,1,0:T(8,128)(2,1)} %select_select_fusion), calls=%async_computation | async-start | bytes 294912 | tf_op jit(solution)/shard_map/all_to_all | solution.py:70
  70.8 10.7 %all-to-all-done = bf16[12,2,24,128]{3,2,1,0:T(8,128)(2,1)S(1)} async-done(((bf16[12,2,24,128]{3,2,1,0:T(8,128)(2,1)}), bf16[12,2,24,128]{3,2,1,0:T(8,128)(2,1)S(1)}, u32[]{:S(2)}, u32[]{:S(2)}) %all-to-all-start) | async-done | bytes 147488 | tf_op jit(solution)/shard_map/all_to_all | solution.py:70
  81.5 10.1 %collective-permute-start.8 = (bf16[1,2,24,128]{3,2,1,0:T(8,128)(2,1)S(1)}, bf16[1,2,24,128]{3,2,1,0:T(8,128)(2,1)S(1)}, u32[]{:S(2)}, u32[]{:S(2)}) collective-permute-start(bf16[1,2,24,128]{3,2,1,0:T(8,128)(2,1)S(1)} %constant_dynamic-slice_fusion), channel_id=1, source_target_pairs={{0,1},{1,0},{2,3},{3,2},{4,5},{5,4},{6,7},{7,6},{8,9},{9,8},{10,11... | collective-permute-start | bytes 36872 | tf_op jit(solution)/shard_map/ppermute | solution.py:44
  91.6 0.8 collective-permute-done.8
  92.4 2.3 %collective-permute-start.9 = (bf16[1,2,2,24,128]{4,3,2,1,0:T(8,128)(2,1)S(1)}, bf16[1,2,2,24,128]{4,3,2,1,0:T(8,128)(2,1)S(1)}, u32[]{:S(2)}, u32[]{:S(2)}) collective-permute-start(bf16[1,2,2,24,128]{4,3,2,1,0:T(8,128)(2,1)S(1)} %maximum_bitcast_fusion), channel_id=1, source_target_pairs={{0,576},{192,0},{384,192},{576,384},{1,577},{193,1},{385,193},{577... | collective-permute-start | bytes 73736 | tf_op jit(solution)/shard_map/ppermute | solution.py:44
  94.7 2.3 %collective-permute-done.9 = bf16[1,2,2,24,128]{4,3,2,1,0:T(8,128)(2,1)S(1)} collective-permute-done((bf16[1,2,2,24,128]{4,3,2,1,0:T(8,128)(2,1)S(1)}, bf16[1,2,2,24,128]{4,3,2,1,0:T(8,128)(2,1)S(1)}, u32[]{:S(2)}, u32[]{:S(2)}) %collective-permute-start.9) | collective-permute-done | bytes 24608 | tf_op jit(solution)/shard_map/ppermute | solution.py:44
  97.0 4.4 %collective-permute-start.10 = (bf16[2,2,2,24,128]{4,3,2,1,0:T(8,128)(2,1)S(1)}, bf16[2,2,2,24,128]{4,3,2,1,0:T(8,128)(2,1)S(1)}, u32[]{:S(2)}, u32[]{:S(2)}) collective-permute-start(bf16[2,2,2,24,128]{4,3,2,1,0:T(8,128)(2,1)S(1)} %pad_maximum_fusion.5), channel_id=1, source_target_pairs={{0,384},{192,576},{384,0},{576,192},{1,385},{193,577},{385,1},{577... | collective-permute-start | bytes 147464 | tf_op jit(solution)/shard_map/ppermute | solution.py:44
  101.4 1.9 %collective-permute-done.10 = bf16[2,2,2,24,128]{4,3,2,1,0:T(8,128)(2,1)S(1)} collective-permute-done((bf16[2,2,2,24,128]{4,3,2,1,0:T(8,128)(2,1)S(1)}, bf16[2,2,2,24,128]{4,3,2,1,0:T(8,128)(2,1)S(1)}, u32[]{:S(2)}, u32[]{:S(2)}) %collective-permute-start.10) | collective-permute-done | bytes 49184 | tf_op jit(solution)/shard_map/ppermute | solution.py:44
  104.0 7.4 %fusion = f32[4,2,24,5,384]{4,2,3,1,0:T(8,128)} fusion(bf16[2560,5,384]{2,0,1:T(8,128)(2,1)} %param.12, bf16[128,2560]{1,0:T(8,128)(2,1)S(1)} %copy-done, bf16[4,2,2,24,128]{4,3,2,1,0:T(8,128)(2,1)S(1)} %broadcast_select_fusion), kind=kOutput, calls=%fused_computation.3 | convolution fusion | flops 2013757440 | bytes 12009472 | tf_op jit(solution)/shard_map/frcd,dhe->frche/dot_general | solution.py:96
  111.4 4.7 %collective-permute-start.11 = (f32[4,2,24,5,384]{4,2,3,1,0:T(8,128)}, f32[4,2,24,5,384]{4,2,3,1,0:T(8,128)S(1)}, u32[]{:S(2)}, u32[]{:S(2)}) collective-permute-start(f32[4,2,24,5,384]{4,2,3,1,0:T(8,128)} %fusion), channel_id=1, source_target_pairs={{0,1},{1,0},{2,3},{3,2},{4,5},{5,4},{6,7},{7,6},{8,9},{9,8},{10,11... | collective-permute-start | bytes 4423688 | tf_op jit(solution)/shard_map/ppermute | solution.py:22
  116.1 3.1 %collective-permute-done.11 = f32[4,2,24,5,384]{4,2,3,1,0:T(8,128)S(1)} collective-permute-done((f32[4,2,24,5,384]{4,2,3,1,0:T(8,128)}, f32[4,2,24,5,384]{4,2,3,1,0:T(8,128)S(1)}, u32[]{:S(2)}, u32[]{:S(2)}) %collective-permute-start.11) | collective-permute-done | bytes 1474592 | tf_op jit(solution)/shard_map/ppermute | solution.py:22
  119.1 6.3 %add_convert_fusion = bf16[4,2,24,5,384]{4,2,3,1,0:T(8,128)(2,1)S(1)} fusion(f32[4,2,24,5,384]{4,2,3,1,0:T(8,128)S(1)} %collective-permute-done.11, bf16[2560,5,384]{2,0,1:T(8,128)(2,1)} %param.12, bf16[128,2560]{1,0:T(8,128)(2,1)S(1)} %copy-done, bf16[4,2,2,24,128]{4,3,2,1,0:T(8,128)(2,1)S(1)} %broadcast_select_fusion), kind=kOutput, calls=%fused_computation.16 | convolution fusion | flops 2014494720 | bytes 12746752 | tf_op jit(solution)/shard_map/frcd,dhe->frche/dot_general | solution.py:96
  125.4 2.3 %collective-permute-start.12 = (bf16[4,2,24,5,256]{4,2,3,1,0:T(8,128)(2,1)S(1)}, bf16[4,2,24,5,256]{4,2,3,1,0:T(8,128)(2,1)S(1)}, u32[]{:S(2)}, u32[]{:S(2)}) collective-permute-start(bf16[4,2,24,5,256]{4,2,3,1,0:T(8,128)(2,1)S(1)} %slice.75), channel_id=1, source_target_pairs={{0,1},{1,0},{2,3},{3,2},{4,5},{5,4},{6,7},{7,6},{8,9},{9,8},{10,11... | collective-permute-start | bytes 1474568 | tf_op jit(solution)/shard_map/ppermute | solution.py:22
  130.6 0.8 convolution_convert_fusion.2
  131.4 1.1 multiply_reduce_fusion
  133.7 2.4 %collective-permute-start.13 = (bf16[2,4,2,24,5,128]{5,3,2,1,4,0:T(8,128)(2,1)S(1)}, bf16[2,4,2,24,5,128]{5,3,2,1,4,0:T(8,128)(2,1)S(1)}, u32[]{:S(2)}, u32[]{:S(2)}) collective-permute-start(bf16[2,4,2,24,5,128]{5,3,2,1,4,0:T(8,128)(2,1)S(1)} %fusion.19), channel_id=1, source_target_pairs={{0,1},{1,0},{2,3},{3,2},{4,5},{5,4},{6,7},{7,6},{8,9},{9,8},{10,11... | collective-permute-start | bytes 1474568 | tf_op jit(solution)/shard_map/ppermute | solution.py:22
  (58 shorter events, 12.5 us)
Async XLA Ops:
  0.6 103.4 %copy-start = (bf16[128,2560]{1,0:T(8,128)(2,1)S(1)}, bf16[128,2560]{1,0:T(8,128)(2,1)}, u32[]{:S(2)}) copy-start(bf16[128,2560]{1,0:T(8,128)(2,1)} %param.11) | copy-start | bytes 1966084
  0.6 21.6 %collective-permute-start = (s32[1,1]{0,1:T(1,128)}, s32[1,1]{0,1:T(1,128)}, u32[]{:S(2)}, u32[]{:S(2)}) collective-permute-start(s32[1,1]{0,1:T(1,128)} %bitcast), channel_id=1, source_target_pairs={{0,176},{16,0},{32,16},{48,32},{64,48},{80,64},{96,80},{112,96},{1... | collective-permute-start | bytes 20 | tf_op jit(solution)/shard_map/ppermute | solution.py:44
  16.6 23.8 %collective-permute-start.4 = (bf16[1,2,24,128]{3,2,1,0:T(8,128)(2,1)S(1)}, bf16[1,2,24,128]{3,2,1,0:T(8,128)(2,1)S(1)}, u32[]{:S(2)}, u32[]{:S(2)}) collective-permute-start(bf16[1,2,24,128]{3,2,1,0:T(8,128)(2,1)S(1)} %slice_bitcast_fusion.6), channel_id=1, source_target_pairs={{0,192},{192,384},{384,576},{1,193},{193,385},{385,577},{2,194},{1... | collective-permute-start | bytes 36872 | tf_op jit(solution)/shard_map/ppermute | solution.py:18
  23.0 5.2 %collective-permute-start.1 = (s32[2,1]{0,1:T(1,128)S(1)}, s32[2,1]{0,1:T(1,128)S(1)}, u32[]{:S(2)}, u32[]{:S(2)}) collective-permute-start(s32[2,1]{0,1:T(1,128)S(1)} %pad_add_fusion), channel_id=1, source_target_pairs={{0,160},{16,176},{32,0},{48,16},{64,32},{80,48},{96,64},{112,80},{... | collective-permute-start | bytes 32 | tf_op jit(solution)/shard_map/ppermute | solution.py:44
  28.8 9.2 %collective-permute-start.3 = (s32[4,1]{0,1:T(1,128)S(1)}, s32[4,1]{0,1:T(1,128)S(1)}, u32[]{:S(2)}, u32[]{:S(2)}) collective-permute-start(s32[4,1]{0,1:T(1,128)S(1)} %pad_add_fusion.1), channel_id=1, source_target_pairs={{0,64},{16,80},{32,96},{48,112},{64,128},{80,144},{96,160},{112,17... | collective-permute-start | bytes 56 | tf_op jit(solution)/shard_map/ppermute | solution.py:44
  30.8 8.2 %collective-permute-start.2 = (s32[4,1]{0,1:T(1,128)S(1)}, s32[4,1]{0,1:T(1,128)S(1)}, u32[]{:S(2)}, u32[]{:S(2)}) collective-permute-start(s32[4,1]{0,1:T(1,128)S(1)} %pad_add_fusion.1), channel_id=1, source_target_pairs={{0,128},{16,144},{32,160},{48,176},{64,0},{80,16},{96,32},{112,48}... | collective-permute-start | bytes 56 | tf_op jit(solution)/shard_map/ppermute | solution.py:44
  41.3 5.9 %collective-permute-start.5 = (bf16[1,2,24,128]{3,2,1,0:T(8,128)(2,1)S(1)}, bf16[1,2,24,128]{3,2,1,0:T(8,128)(2,1)S(1)}, u32[]{:S(2)}, u32[]{:S(2)}) collective-permute-start(bf16[1,2,24,128]{3,2,1,0:T(8,128)(2,1)S(1)} %fusion.35), channel_id=1, source_target_pairs={{0,14},{2,0},{4,2},{6,4},{8,6},{10,8},{12,10},{14,12},{1,15},{3,1}... | collective-permute-start | bytes 36872 | tf_op jit(solution)/shard_map/ppermute | solution.py:44
  47.3 5.5 %collective-permute-start.6 = (bf16[2,2,24,128]{3,2,1,0:T(8,128)(2,1)S(1)}, bf16[2,2,24,128]{3,2,1,0:T(8,128)(2,1)S(1)}, u32[]{:S(2)}, u32[]{:S(2)}) collective-permute-start(bf16[2,2,24,128]{3,2,1,0:T(8,128)(2,1)S(1)} %pad_maximum_fusion.6), channel_id=1, source_target_pairs={{0,12},{2,14},{4,0},{6,2},{8,4},{10,6},{12,8},{14,10},{1,13},{3,15... | collective-permute-start | bytes 73736 | tf_op jit(solution)/shard_map/ppermute | solution.py:44
  52.7 8.8 %collective-permute-start.7 = (bf16[4,2,24,128]{3,2,1,0:T(8,128)(2,1)S(1)}, bf16[4,2,24,128]{3,2,1,0:T(8,128)(2,1)S(1)}, u32[]{:S(2)}, u32[]{:S(2)}) collective-permute-start(bf16[4,2,24,128]{3,2,1,0:T(8,128)(2,1)S(1)} %pad_maximum_fusion.4), channel_id=1, source_target_pairs={{0,8},{2,10},{4,12},{6,14},{8,0},{10,2},{12,4},{14,6},{1,9},{3,11}... | collective-permute-start | bytes 147464 | tf_op jit(solution)/shard_map/ppermute | solution.py:44
  62.9 18.6 %all-to-all-start = ((bf16[12,2,24,128]{3,2,1,0:T(8,128)(2,1)}), bf16[12,2,24,128]{3,2,1,0:T(8,128)(2,1)S(1)}, u32[]{:S(2)}, u32[]{:S(2)}) async-start(bf16[12,2,24,128]{3,2,1,0:T(8,128)(2,1)} %select_select_fusion), calls=%async_computation | async-start | bytes 294912 | tf_op jit(solution)/shard_map/all_to_all | solution.py:70
  81.5 10.9 %collective-permute-start.8 = (bf16[1,2,24,128]{3,2,1,0:T(8,128)(2,1)S(1)}, bf16[1,2,24,128]{3,2,1,0:T(8,128)(2,1)S(1)}, u32[]{:S(2)}, u32[]{:S(2)}) collective-permute-start(bf16[1,2,24,128]{3,2,1,0:T(8,128)(2,1)S(1)} %constant_dynamic-slice_fusion), channel_id=1, source_target_pairs={{0,1},{1,0},{2,3},{3,2},{4,5},{5,4},{6,7},{7,6},{8,9},{9,8},{10,11... | collective-permute-start | bytes 36872 | tf_op jit(solution)/shard_map/ppermute | solution.py:44
  92.4 4.6 %collective-permute-start.9 = (bf16[1,2,2,24,128]{4,3,2,1,0:T(8,128)(2,1)S(1)}, bf16[1,2,2,24,128]{4,3,2,1,0:T(8,128)(2,1)S(1)}, u32[]{:S(2)}, u32[]{:S(2)}) collective-permute-start(bf16[1,2,2,24,128]{4,3,2,1,0:T(8,128)(2,1)S(1)} %maximum_bitcast_fusion), channel_id=1, source_target_pairs={{0,576},{192,0},{384,192},{576,384},{1,577},{193,1},{385,193},{577... | collective-permute-start | bytes 73736 | tf_op jit(solution)/shard_map/ppermute | solution.py:44
  97.0 6.3 %collective-permute-start.10 = (bf16[2,2,2,24,128]{4,3,2,1,0:T(8,128)(2,1)S(1)}, bf16[2,2,2,24,128]{4,3,2,1,0:T(8,128)(2,1)S(1)}, u32[]{:S(2)}, u32[]{:S(2)}) collective-permute-start(bf16[2,2,2,24,128]{4,3,2,1,0:T(8,128)(2,1)S(1)} %pad_maximum_fusion.5), channel_id=1, source_target_pairs={{0,384},{192,576},{384,0},{576,192},{1,385},{193,577},{385,1},{577... | collective-permute-start | bytes 147464 | tf_op jit(solution)/shard_map/ppermute | solution.py:44
  111.4 17.0 %copy-start.2 = (bf16[1,4,2,24,5,128]{5,3,4,2,1,0:T(8,128)(2,1)S(1)}, bf16[1,4,2,24,5,128]{5,3,4,2,1,0:T(8,128)(2,1)}, u32[]{:S(2)}) copy-start(bf16[1,4,2,24,5,128]{5,3,4,2,1,0:T(8,128)(2,1)} %param.13) | copy-start | bytes 737284
  111.4 7.8 %collective-permute-start.11 = (f32[4,2,24,5,384]{4,2,3,1,0:T(8,128)}, f32[4,2,24,5,384]{4,2,3,1,0:T(8,128)S(1)}, u32[]{:S(2)}, u32[]{:S(2)}) collective-permute-start(f32[4,2,24,5,384]{4,2,3,1,0:T(8,128)} %fusion), channel_id=1, source_target_pairs={{0,1},{1,0},{2,3},{3,2},{4,5},{5,4},{6,7},{7,6},{8,9},{9,8},{10,11... | collective-permute-start | bytes 4423688 | tf_op jit(solution)/shard_map/ppermute | solution.py:22
  125.4 3.8 %collective-permute-start.12 = (bf16[4,2,24,5,256]{4,2,3,1,0:T(8,128)(2,1)S(1)}, bf16[4,2,24,5,256]{4,2,3,1,0:T(8,128)(2,1)S(1)}, u32[]{:S(2)}, u32[]{:S(2)}) collective-permute-start(bf16[4,2,24,5,256]{4,2,3,1,0:T(8,128)(2,1)S(1)} %slice.75), channel_id=1, source_target_pairs={{0,1},{1,0},{2,3},{3,2},{4,5},{5,4},{6,7},{7,6},{8,9},{9,8},{10,11... | collective-permute-start | bytes 1474568 | tf_op jit(solution)/shard_map/ppermute | solution.py:22
  133.6 2.5 %copy-start.1 = (bf16[5,128,192]{1,2,0:T(8,128)(2,1)S(1)}, bf16[5,128,192]{1,2,0:T(8,128)(2,1)}, u32[]{:S(2)}) copy-start(bf16[5,128,192]{1,2,0:T(8,128)(2,1)} %get-tuple-element.21) | copy-start | bytes 737284
  133.7 4.2 %collective-permute-start.13 = (bf16[2,4,2,24,5,128]{5,3,2,1,4,0:T(8,128)(2,1)S(1)}, bf16[2,4,2,24,5,128]{5,3,2,1,4,0:T(8,128)(2,1)S(1)}, u32[]{:S(2)}, u32[]{:S(2)}) collective-permute-start(bf16[2,4,2,24,5,128]{5,3,2,1,4,0:T(8,128)(2,1)S(1)} %fusion.19), channel_id=1, source_target_pairs={{0,1},{1,0},{2,3},{3,2},{4,5},{5,4},{6,7},{7,6},{8,9},{9,8},{10,11... | collective-permute-start | bytes 1474568 | tf_op jit(solution)/shard_map/ppermute | solution.py:22

commit v3 on v2

--- a/solution.py
+++ b/solution.py
@@ -10,6 +10,10 @@
 OUTER = "mp_outer"
 INNER = "mp_inner"
 MP = (OUTER, INNER)
+SLOT_MODE = 'a2a'
+ROW_MODE = 'a2a'
+FANOUT = 'a2a'
+RAW = True
 
 
 def passed_along(shard, axis, by):
@@ -55,21 +59,56 @@
     return jnp.take(have, (jnp.arange(n) - me) % n, axis=0)
 
 
-def route(act, tokenizer_slot):
+def gather_a2a(x, axis):
+    n = lax.axis_size(axis)
+    send = jnp.broadcast_to(x[None], (n,) + x.shape)
+    return lax.all_to_all(send, axis, 0, 0, tiled=True)
+
+
+def gather(x, axis, mode):
+    if mode == "a2a":
+        return gather_a2a(x, axis)
+    if mode == "ag":
+        return lax.all_gather(x, axis, axis=0)
+    return gather_ordered(x, axis)
+
+
+def route(piece, tokenizer_slot):
     n_in = lax.axis_size(INNER)
     n_out = lax.axis_size(OUTER)
     my_out = lax.axis_index(OUTER)
-    my_in = lax.axis_index(INNER)
     source = tokenizer_slot[0]
-    row = gather_rotated(act, INNER)
-    wanted = gather_ordered(tokenizer_slot, OUTER)[:, 0]
-    pick = (wanted % n_in - my_in) % n_in
+    wanted = gather(tokenizer_slot, OUTER, SLOT_MODE)[:, 0]
+    row = gather(piece, INNER, ROW_MODE)
+    pick = jnp.clip(wanted % n_in, 0, n_in - 1)
     mine = (wanted // n_in) == my_out
     send = jnp.take(row, pick, axis=0)
-    send = jnp.where(mine.reshape((n_out,) + (1,) * act.ndim), send, jnp.zeros_like(send))
+    send = jnp.where(mine.reshape((n_out,) + (1,) * piece.ndim), send, jnp.zeros_like(send))
+    origin = jnp.clip(source // n_in, 0, n_out - 1)
+    if FANOUT == "merged":
+        n_grp = lax.axis_size("segment") * lax.axis_size("seq")
+        wide = jnp.broadcast_to(send[:, None], (n_out, n_grp) + piece.shape)
+        wide = wide.reshape((n_out * n_grp,) + piece.shape)
+        got = lax.all_to_all(wide, (OUTER, "segment", "seq"), 0, 0, tiled=True)
+        got = got.reshape((n_out, n_grp) + piece.shape)
+        return lax.dynamic_index_in_dim(got, origin, 0, keepdims=False)
     got = lax.all_to_all(send, OUTER, 0, 0, tiled=True)
-    origin = jnp.clip(source // n_in, 0, n_out - 1)
-    return lax.dynamic_index_in_dim(got, origin, 0, keepdims=False)
+    routed = lax.dynamic_index_in_dim(got, origin, 0, keepdims=False)
+    return gather(routed, ("segment", "seq"), FANOUT)
+
+
+def conv_all(frames, conv_w):
+    current = frames[1::2]
+    middle = frames[0::2]
+    earlier = jnp.concatenate([jnp.zeros_like(current[:1]), current[:-1]], axis=0)
+    total = jnp.einsum("frcx,xy->frcy", current, conv_w[0], preferred_element_type=jnp.float32)
+    total = total + jnp.einsum(
+        "frcx,xy->frcy", middle, conv_w[1], preferred_element_type=jnp.float32
+    )
+    total = total + jnp.einsum(
+        "frcx,xy->frcy", earlier, conv_w[2], preferred_element_type=jnp.float32
+    )
+    return jax.nn.silu(total).astype(jnp.bfloat16)
 
 
 def masked_scores(queries, keys, keep, scale):
@@ -78,13 +117,26 @@
 
 
 def on_device(frames_in, valid_frames, tokenizer_slot, conv_w, embed_w, qkv_w, out_grad):
-    act = causal_conv(frames_in[0], conv_w)
-    row_dev, cols, channels = act.shape
-    routed = route(act, tokenizer_slot)
     n_seg = lax.axis_size("segment")
     n_seq = lax.axis_size("seq")
-    pair = gather_rotated(routed, "seq")
-    latent = gather_ordered(pair, "segment")
+    me = lax.axis_index("seq")
+    if RAW:
+        local = frames_in[0]
+        n_fr, row_dev, cols, channels = local.shape
+        pieces = route(local, tokenizer_slot).reshape(
+            (n_seg, n_seq, n_fr, row_dev, cols, channels)
+        )
+        frames = pieces.transpose(0, 2, 1, 3, 4, 5).reshape(
+            n_seg * n_fr, n_seq * row_dev, cols, channels
+        )
+        act_all = conv_all(frames, conv_w).reshape(n_seg, n_seq, row_dev, cols, channels)
+    else:
+        act = causal_conv(frames_in[0], conv_w)
+        row_dev, cols, channels = act.shape
+        act_all = route(act, tokenizer_slot).reshape(n_seg, n_seq, row_dev, cols, channels)
+    own_rows = lax.dynamic_index_in_dim(act_all, me, 1, keepdims=False)
+    other_rows = lax.dynamic_index_in_dim(act_all, 1 - me, 1, keepdims=False)
+    latent = jnp.stack([own_rows, other_rows], axis=1)
     heads_local = qkv_w.shape[1]
     head_size = qkv_w.shape[2] // 3
     rows = n_seq * row_dev

time: 141 us -> 114 us (0.81)
  starting transfers between devices: 79.3 us -> 44.1 us
  waiting for transfers between devices: 27.8 us -> 39.6 us
  matrix products: 20 us -> 17.9 us
    ppermute x11 -> x0, starting transfers between devices: 62.2 us -> none  [the longest x10 59.1 us: gather_rotated(): lax.ppermute(have[:need], axis, pairs)]
    all_to_all x0 -> x3, starting transfers between devices: none -> 33 us  [gather_a2a(): return lax.all_to_all(send, axis, 0, 0, tiled=True)]
    all_to_all x0 -> x3, waiting for transfers between devices: none -> 23.1 us  [gather_a2a(): return lax.all_to_all(send, axis, 0, 0, tiled=True)]
    ppermute x11 -> x0, waiting for transfers between devices: 13.4 us -> none  [the longest x10 13.4 us: gather_rotated(): lax.ppermute(have[:need], axis, pairs)]
    all_to_all x1, starting transfers between devices: 7.82 us -> 3.55 us  [route(): got = lax.all_to_all(send, OUTER, 0, 0, tiled=True)]
    broadcast_in_dim x0 -> x4, local copies, waits for them, and re-layouts: none -> 2.75 us  [gather_a2a(): send = jnp.broadcast_to(x[None], (n,) + x.shape)]
    dot_general x3, matrix products: 2.73 us -> 0.61 us  [the longest x1 0.23 us: conv_all(): jnp.einsum('frcx,xy->frcy', middle, conv_w[1], preferred_element_type=jnp...]
    all_to_all x1, waiting for transfers between devices: 10.7 us -> 12.7 us  [route(): got = lax.all_to_all(send, OUTER, 0, 0, tiled=True)]
  transfers between devices with their start and end apart: 15 -> 7, of which waited for: 11 -> 6; matrix products, arithmetic and copies ran while one was open for 5% -> 2% of each run, Pallas kernels for 0% -> 0%
where the time goes in v3:
time: 114 us; the launch traced here: 113 us
  starting transfers between devices  44.1 us (39%)
  waiting for transfers between devices  39.6 us (35%)
  matrix products  17.9 us (16%)
  local copies, waits for them, and re-layouts  6.85 us (6%)
  between operations  2.32 us (2%)
  other arithmetic  2.12 us (2%)
    all_to_all x3, starting transfers between devices, gather_a2a(): return lax.all_to_all(send, axis, 0, 0, tiled=True)  33 us
    all_to_all x3, waiting for transfers between devices, gather_a2a(): return lax.all_to_all(send, axis, 0, 0, tiled=True)  23.1 us
    dot_general x2, matrix products, project(): jnp.einsum('frcd,dhe->frche', hidden, qkv_w, preferred_element_type=jnp.f...  13.7 us
    all_to_all x1, waiting for transfers between devices, route(): got = lax.all_to_all(send, OUTER, 0, 0, tiled=True)  12.7 us
    ppermute x3, starting transfers between devices, swap_seq(): return lax.ppermute(x, 'seq', [(0, 1), (1, 0)])  7.55 us
    ppermute x3, waiting for transfers between devices, swap_seq(): return lax.ppermute(x, 'seq', [(0, 1), (1, 0)])  3.75 us
    all_to_all x1, starting transfers between devices, route(): got = lax.all_to_all(send, OUTER, 0, 0, tiled=True)  3.55 us
    unnamed x13, local copies, waits for them, and re-layouts  2.93 us
  transfers between devices with their start and end apart: 7, of which 6 were waited for; matrix products, arithmetic and copies ran while one was open for 2% of the time, Pallas kernels for 0%

profile of v3, /device:TPU:1, one launch (start us, length us, event | category | flops | bytes accessed | tf_op | source)
XLA Modules:
  0.0 112.8 jit_solution(706397511086510901)
XLA Ops:
  1.4 0.6 broadcast_in_dim.62
  2.0 15.7 %all-to-all-start = ((s32[12,1,1]{2,1,0:T(1,128)}), s32[12,1,1]{2,1,0:T(1,128)S(1)}, u32[]{:S(2)}, u32[]{:S(2)}) async-start(s32[12,1,1]{2,1,0:T(1,128)} %broadcast_in_dim.62), calls=%async_computation | async-start | bytes 12288 | tf_op jit(solution)/shard_map/all_to_all | solution.py:65
  17.7 8.9 %all-to-all-done = s32[12,1,1]{2,1,0:T(1,128)S(1)} async-done(((s32[12,1,1]{2,1,0:T(1,128)}), s32[12,1,1]{2,1,0:T(1,128)S(1)}, u32[]{:S(2)}, u32[]{:S(2)}) %all-to-all-start) | async-done | bytes 80 | tf_op jit(solution)/shard_map/all_to_all | solution.py:65
  26.5 1.4 %broadcast_in_dim.66 = bf16[8,2,2,24,128]{4,3,2,1,0:T(8,128)(2,1)} broadcast(bf16[2,2,24,128]{3,2,1,0:T(8,128)(2,1)} %bitcast.142), dimensions={1,2,3,4} | broadcast | bytes 221184 | tf_op jit(solution)/shard_map/broadcast_in_dim | solution.py:64
  28.0 6.8 %all-to-all-start.1 = ((bf16[8,2,2,24,128]{4,3,2,1,0:T(8,128)(2,1)}), bf16[8,2,2,24,128]{4,3,2,1,0:T(8,128)(2,1)S(1)}, u32[]{:S(2)}, u32[]{:S(2)}) async-start(bf16[8,2,2,24,128]{4,3,2,1,0:T(8,128)(2,1)} %broadcast_in_dim.66), calls=%async_computation.1 | async-start | bytes 393216 | tf_op jit(solution)/shard_map/all_to_all | solution.py:65
  34.8 0.3 reduce
  35.2 8.4 %all-to-all-done.1 = bf16[8,2,2,24,128]{4,3,2,1,0:T(8,128)(2,1)S(1)} async-done(((bf16[8,2,2,24,128]{4,3,2,1,0:T(8,128)(2,1)}), bf16[8,2,2,24,128]{4,3,2,1,0:T(8,128)(2,1)S(1)}, u32[]{:S(2)}, u32[]{:S(2)}) %all-to-all-start.1) | async-done | bytes 196640 | tf_op jit(solution)/shard_map/all_to_all | solution.py:65
  43.5 0.6 gather_fusion
  44.1 0.8 select_select_fusion
  45.0 3.5 %all-to-all-start.2 = ((bf16[12,2,2,24,128]{4,3,2,1,0:T(8,128)(2,1)}), bf16[12,2,2,24,128]{4,3,2,1,0:T(8,128)(2,1)S(1)}, u32[]{:S(2)}, u32[]{:S(2)}) async-start(bf16[12,2,2,24,128]{4,3,2,1,0:T(8,128)(2,1)} %select_select_fusion), calls=%async_computation.2 | async-start | bytes 589824 | tf_op jit(solution)/shard_map/all_to_all | solution.py:95
  48.6 12.7 %all-to-all-done.2 = bf16[12,2,2,24,128]{4,3,2,1,0:T(8,128)(2,1)S(1)} async-done(((bf16[12,2,2,24,128]{4,3,2,1,0:T(8,128)(2,1)}), bf16[12,2,2,24,128]{4,3,2,1,0:T(8,128)(2,1)S(1)}, u32[]{:S(2)}, u32[]{:S(2)}) %all-to-all-start.2) | async-done | bytes 294944 | tf_op jit(solution)/shard_map/all_to_all | solution.py:95
  61.3 0.7 broadcast_in_dim.70
  62.0 10.5 %all-to-all-start.3 = ((bf16[8,2,2,24,128]{4,3,2,1,0:T(8,128)(2,1)}), bf16[8,2,2,24,128]{4,3,2,1,0:T(8,128)(2,1)S(1)}, u32[]{:S(2)}, u32[]{:S(2)}) async-start(bf16[8,2,2,24,128]{4,3,2,1,0:T(8,128)(2,1)} %broadcast_in_dim.70), calls=%async_computation.3 | async-start | bytes 393216 | tf_op jit(solution)/shard_map/all_to_all | solution.py:65
  72.5 5.9 %all-to-all-done.3 = bf16[8,2,2,24,128]{4,3,2,1,0:T(8,128)(2,1)S(1)} async-done(((bf16[8,2,2,24,128]{4,3,2,1,0:T(8,128)(2,1)}), bf16[8,2,2,24,128]{4,3,2,1,0:T(8,128)(2,1)S(1)}, u32[]{:S(2)}, u32[]{:S(2)}) %all-to-all-start.3) | async-done | bytes 196640 | tf_op jit(solution)/shard_map/all_to_all | solution.py:65
  79.1 7.4 %fusion = f32[4,2,24,5,384]{4,2,3,1,0:T(8,128)} fusion(bf16[2560,5,384]{2,0,1:T(8,128)(2,1)} %param.12, bf16[128,2560]{1,0:T(8,128)(2,1)S(1)} %copy-done, bf16[4,2,2,24,128]{4,3,2,1,0:T(8,128)(2,1)S(1)} %bitcast.143, s32[]{:T(128)S(6)} %select_n.85), kind=kOutput, calls=%fused_computation.1 | convolution fusion | flops 2013757440 | bytes 12009476 | tf_op jit(solution)/shard_map/frcd,dhe->frche/dot_general | solution.py:148
  86.5 2.9 %collective-permute-start = (f32[4,2,24,5,384]{4,2,3,1,0:T(8,128)}, f32[4,2,24,5,384]{4,2,3,1,0:T(8,128)S(1)}, u32[]{:S(2)}, u32[]{:S(2)}) collective-permute-start(f32[4,2,24,5,384]{4,2,3,1,0:T(8,128)} %fusion), channel_id=1, source_target_pairs={{0,1},{1,0},{2,3},{3,2},{4,5},{5,4},{6,7},{7,6},{8,9},{9,8},{10,11... | collective-permute-start | bytes 4423688 | tf_op jit(solution)/shard_map/ppermute | solution.py:26
  89.3 3.1 %collective-permute-done = f32[4,2,24,5,384]{4,2,3,1,0:T(8,128)S(1)} collective-permute-done((f32[4,2,24,5,384]{4,2,3,1,0:T(8,128)}, f32[4,2,24,5,384]{4,2,3,1,0:T(8,128)S(1)}, u32[]{:S(2)}, u32[]{:S(2)}) %collective-permute-start) | collective-permute-done | bytes 1474592 | tf_op jit(solution)/shard_map/ppermute | solution.py:26
  92.4 6.3 %add_convert_fusion = bf16[4,2,24,5,384]{4,2,3,1,0:T(8,128)(2,1)S(1)} fusion(f32[4,2,24,5,384]{4,2,3,1,0:T(8,128)S(1)} %collective-permute-done, bf16[2560,5,384]{2,0,1:T(8,128)(2,1)} %param.12, bf16[128,2560]{1,0:T(8,128)(2,1)S(1)} %copy-done, bf16[4,2,2,24,128]{4,3,2,1,0:T(8,128)(2,1)S(1)} %bitcast.144, s32[]{:T(128)S(6)} %select_n.84), kind=kOutput, calls=%fused_computation.14 | convolution fusion | flops 2014494720 | bytes 12746756 | tf_op jit(solution)/shard_map/frcd,dhe->frche/dot_general | solution.py:148
  98.7 2.3 %collective-permute-start.1 = (bf16[4,2,24,5,256]{4,2,3,1,0:T(8,128)(2,1)S(1)}, bf16[4,2,24,5,256]{4,2,3,1,0:T(8,128)(2,1)S(1)}, u32[]{:S(2)}, u32[]{:S(2)}) collective-permute-start(bf16[4,2,24,5,256]{4,2,3,1,0:T(8,128)(2,1)S(1)} %slice.60), channel_id=1, source_target_pairs={{0,1},{1,0},{2,3},{3,2},{4,5},{5,4},{6,7},{7,6},{8,9},{9,8},{10,11... | collective-permute-start | bytes 1474568 | tf_op jit(solution)/shard_map/ppermute | solution.py:26
  101.8 0.7 collective-permute-done.1
  102.8 0.5 fusion.60
  103.3 0.6 exponential_reduce_fusion
  103.8 0.8 convolution_convert_fusion.2
  104.6 1.1 %multiply_reduce_fusion = (f32[192,5]{0,1:T(8,128)S(1)}, bf16[5,128,192]{1,2,0:T(8,128)(2,1)}) fusion(bf16[192,5,128]{2,0,1:T(8,128)(2,1)S(1)} %bitcast.131, bf16[384,5,128]{2,0,1:T(8,128)(2,1)S(1)} %bitcast.122, f32[5,192,384]{2,1,0:T(8,128)S(1)} %get-tuple-element.27, f32[5,192]{1,0:T(8,128)S(1)} %log_add_fusion), kind=kOutput, calls=%fused_computation.39 | convolution fusion | flops 95722560 | bytes 2465280 | tf_op jit(solution)/shard_map/hqk,khd->qhd/dot_general | solution.py:169
  105.8 0.5 fusion.6
  106.2 0.4 fusion.11
  107.0 2.4 %collective-permute-start.2 = (bf16[2,4,2,24,5,128]{5,3,2,1,4,0:T(8,128)(2,1)S(1)}, bf16[2,4,2,24,5,128]{5,3,2,1,4,0:T(8,128)(2,1)S(1)}, u32[]{:S(2)}, u32[]{:S(2)}) collective-permute-start(bf16[2,4,2,24,5,128]{5,3,2,1,4,0:T(8,128)(2,1)S(1)} %fusion.20), channel_id=1, source_target_pairs={{0,1},{1,0},{2,3},{3,2},{4,5},{5,4},{6,7},{7,6},{8,9},{9,8},{10,11... | collective-permute-start | bytes 1474568 | tf_op jit(solution)/shard_map/ppermute | solution.py:26
  109.4 0.7 copy.45
  110.1 0.4 fusion.12
  110.5 0.7 copy.46
  111.4 0.7 copy.48
  112.1 0.7 copy.47
  (31 shorter events, 1.7 us)
Async XLA Ops:
  0.6 78.4 %copy-start = (bf16[128,2560]{1,0:T(8,128)(2,1)S(1)}, bf16[128,2560]{1,0:T(8,128)(2,1)}, u32[]{:S(2)}) copy-start(bf16[128,2560]{1,0:T(8,128)(2,1)} %param.11) | copy-start | bytes 1966084
  2.0 24.6 %all-to-all-start = ((s32[12,1,1]{2,1,0:T(1,128)}), s32[12,1,1]{2,1,0:T(1,128)S(1)}, u32[]{:S(2)}, u32[]{:S(2)}) async-start(s32[12,1,1]{2,1,0:T(1,128)} %broadcast_in_dim.62), calls=%async_computation | async-start | bytes 12288 | tf_op jit(solution)/shard_map/all_to_all | solution.py:65
  28.0 15.6 %all-to-all-start.1 = ((bf16[8,2,2,24,128]{4,3,2,1,0:T(8,128)(2,1)}), bf16[8,2,2,24,128]{4,3,2,1,0:T(8,128)(2,1)S(1)}, u32[]{:S(2)}, u32[]{:S(2)}) async-start(bf16[8,2,2,24,128]{4,3,2,1,0:T(8,128)(2,1)} %broadcast_in_dim.66), calls=%async_computation.1 | async-start | bytes 393216 | tf_op jit(solution)/shard_map/all_to_all | solution.py:65
  35.2 43.3 %copy-start.3 = (bf16[3,128,128]{2,1,0:T(8,128)(2,1)S(1)}, bf16[3,128,128]{2,1,0:T(8,128)(2,1)}, u32[]{:S(2)}) copy-start(bf16[3,128,128]{2,1,0:T(8,128)(2,1)} %param.10) | copy-start | bytes 294916
  45.0 16.3 %all-to-all-start.2 = ((bf16[12,2,2,24,128]{4,3,2,1,0:T(8,128)(2,1)}), bf16[12,2,2,24,128]{4,3,2,1,0:T(8,128)(2,1)S(1)}, u32[]{:S(2)}, u32[]{:S(2)}) async-start(bf16[12,2,2,24,128]{4,3,2,1,0:T(8,128)(2,1)} %select_select_fusion), calls=%async_computation.2 | async-start | bytes 589824 | tf_op jit(solution)/shard_map/all_to_all | solution.py:95
  62.0 16.4 %all-to-all-start.3 = ((bf16[8,2,2,24,128]{4,3,2,1,0:T(8,128)(2,1)}), bf16[8,2,2,24,128]{4,3,2,1,0:T(8,128)(2,1)S(1)}, u32[]{:S(2)}, u32[]{:S(2)}) async-start(bf16[8,2,2,24,128]{4,3,2,1,0:T(8,128)(2,1)} %broadcast_in_dim.70), calls=%async_computation.3 | async-start | bytes 393216 | tf_op jit(solution)/shard_map/all_to_all | solution.py:65
  86.5 6.0 %collective-permute-start = (f32[4,2,24,5,384]{4,2,3,1,0:T(8,128)}, f32[4,2,24,5,384]{4,2,3,1,0:T(8,128)S(1)}, u32[]{:S(2)}, u32[]{:S(2)}) collective-permute-start(f32[4,2,24,5,384]{4,2,3,1,0:T(8,128)} %fusion), channel_id=1, source_target_pairs={{0,1},{1,0},{2,3},{3,2},{4,5},{5,4},{6,7},{7,6},{8,9},{9,8},{10,11... | collective-permute-start | bytes 4423688 | tf_op jit(solution)/shard_map/ppermute | solution.py:26
  89.3 12.3 %copy-start.2 = (bf16[1,4,2,24,5,128]{5,3,4,2,1,0:T(8,128)(2,1)S(1)}, bf16[1,4,2,24,5,128]{5,3,4,2,1,0:T(8,128)(2,1)}, u32[]{:S(2)}) copy-start(bf16[1,4,2,24,5,128]{5,3,4,2,1,0:T(8,128)(2,1)} %param.13) | copy-start | bytes 737284
  98.7 3.8 %collective-permute-start.1 = (bf16[4,2,24,5,256]{4,2,3,1,0:T(8,128)(2,1)S(1)}, bf16[4,2,24,5,256]{4,2,3,1,0:T(8,128)(2,1)S(1)}, u32[]{:S(2)}, u32[]{:S(2)}) collective-permute-start(bf16[4,2,24,5,256]{4,2,3,1,0:T(8,128)(2,1)S(1)} %slice.60), channel_id=1, source_target_pairs={{0,1},{1,0},{2,3},{3,2},{4,5},{5,4},{6,7},{7,6},{8,9},{9,8},{10,11... | collective-permute-start | bytes 1474568 | tf_op jit(solution)/shard_map/ppermute | solution.py:26
  106.9 2.5 %copy-start.1 = (bf16[5,128,192]{1,2,0:T(8,128)(2,1)S(1)}, bf16[5,128,192]{1,2,0:T(8,128)(2,1)}, u32[]{:S(2)}) copy-start(bf16[5,128,192]{1,2,0:T(8,128)(2,1)} %get-tuple-element.29) | copy-start | bytes 737284
  107.0 4.2 %collective-permute-start.2 = (bf16[2,4,2,24,5,128]{5,3,2,1,4,0:T(8,128)(2,1)S(1)}, bf16[2,4,2,24,5,128]{5,3,2,1,4,0:T(8,128)(2,1)S(1)}, u32[]{:S(2)}, u32[]{:S(2)}) collective-permute-start(bf16[2,4,2,24,5,128]{5,3,2,1,4,0:T(8,128)(2,1)S(1)} %fusion.20), channel_id=1, source_target_pairs={{0,1},{1,0},{2,3},{3,2},{4,5},{5,4},{6,7},{7,6},{8,9},{9,8},{10,11... | collective-permute-start | bytes 1474568 | tf_op jit(solution)/shard_map/ppermute | solution.py:26

commit v4 on v3

--- a/solution.py
+++ b/solution.py
@@ -10,7 +10,7 @@
 OUTER = "mp_outer"
 INNER = "mp_inner"
 MP = (OUTER, INNER)
-SLOT_MODE = 'a2a'
+SLOT_MODE = 'bruck'
 ROW_MODE = 'a2a'
 FANOUT = 'a2a'
 RAW = True
@@ -148,7 +148,8 @@
         return jnp.einsum("frcd,dhe->frche", hidden, qkv_w, preferred_element_type=jnp.float32)
 
     received = swap_seq(project(latent[:, 1]))
-    own_qkv = (project(latent[:, 0]) + received).astype(jnp.bfloat16)
+    own_partial = lax.optimization_barrier(project(latent[:, 0]))
+    own_qkv = (own_partial + received).astype(jnp.bfloat16)
     own_pair = own_qkv[..., head_size:]
     other_pair = swap_seq(own_pair)
     all_pair = jnp.concatenate([own_pair, other_pair], axis=1)

time: 114 us -> 116 us (1.018)
  waiting for transfers between devices: 39.6 us -> 25.2 us
  starting transfers between devices: 44.1 us -> 56.1 us
  other arithmetic: 2.12 us -> 4.7 us
    ppermute x0 -> x4, starting transfers between devices: none -> 26.6 us  [gather_rotated(): lax.ppermute(have[:need], axis, pairs)]
    all_to_all x3 -> x2, waiting for transfers between devices: 23.1 us -> 5.86 us  [gather_a2a(): return lax.all_to_all(send, axis, 0, 0, tiled=True)]
    all_to_all x3 -> x2, starting transfers between devices: 33 us -> 17.4 us  [gather_a2a(): return lax.all_to_all(send, axis, 0, 0, tiled=True)]
    ppermute x0 -> x4, waiting for transfers between devices: none -> 5.71 us  [gather_rotated(): lax.ppermute(have[:need], axis, pairs)]
    ppermute x3, waiting for transfers between devices: 3.75 us -> 1.04 us  [swap_seq(): return lax.ppermute(x, 'seq', [(0, 1), (1, 0)])]
    all_to_all x1, starting transfers between devices: 3.55 us -> 5.23 us  [route(): got = lax.all_to_all(send, OUTER, 0, 0, tiled=True)]
    convert_element_type x0 -> x1, other arithmetic: none -> 1.55 us  [on_device(): own_qkv = (own_partial + received).astype(jnp.bfloat16)]
    concatenate x0 -> x2, other arithmetic: none -> 1.27 us  [gather_rotated(): jnp.concatenate([have, lax.ppermute(have[:need], axis, pairs)], axis=0)]
  transfers between devices with their start and end apart: 7 -> 10, of which waited for: 6 -> 5; matrix products, arithmetic and copies ran while one was open for 2% -> 12% of each run, Pallas kernels for 0% -> 0%
where the time goes in v4:
time: 116 us; the launch traced here: 115 us
  starting transfers between devices  56.1 us (48%)
  waiting for transfers between devices  25.2 us (22%)
  matrix products  19 us (16%)
  local copies, waits for them, and re-layouts  7.58 us (7%)
  other arithmetic  4.7 us (4%)
  between operations  2.29 us (2%)
    ppermute x4, starting transfers between devices, gather_rotated(): lax.ppermute(have[:need], axis, pairs)  26.6 us
    all_to_all x2, starting transfers between devices, gather_a2a(): return lax.all_to_all(send, axis, 0, 0, tiled=True)  17.4 us
    dot_general x2, matrix products, project(): jnp.einsum('frcd,dhe->frche', hidden, qkv_w, preferred_element_type=jnp.f...  14.8 us
    all_to_all x1, waiting for transfers between devices, route(): got = lax.all_to_all(send, OUTER, 0, 0, tiled=True)  12.6 us
    ppermute x3, starting transfers between devices, swap_seq(): return lax.ppermute(x, 'seq', [(0, 1), (1, 0)])  6.92 us
    all_to_all x2, waiting for transfers between devices, gather_a2a(): return lax.all_to_all(send, axis, 0, 0, tiled=True)  5.86 us
    ppermute x4, waiting for transfers between devices, gather_rotated(): lax.ppermute(have[:need], axis, pairs)  5.71 us
    all_to_all x1, starting transfers between devices, route(): got = lax.all_to_all(send, OUTER, 0, 0, tiled=True)  5.23 us
  transfers between devices with their start and end apart: 10, of which 5 were waited for; matrix products, arithmetic and copies ran while one was open for 12% of the time, Pallas kernels for 0%

profile of v4, /device:TPU:1, one launch (start us, length us, event | category | flops | bytes accessed | tf_op | source)
XLA Modules:
  0.0 114.8 jit_solution(6817473170797215467)
XLA Ops:
  0.6 15.3 %collective-permute-start = (s32[1,1]{0,1:T(1,128)}, s32[1,1]{0,1:T(1,128)}, u32[]{:S(2)}, u32[]{:S(2)}) collective-permute-start(s32[1,1]{0,1:T(1,128)} %bitcast), channel_id=1, source_target_pairs={{0,176},{16,0},{32,16},{48,32},{64,48},{80,64},{96,80},{112,96},{1... | collective-permute-start | bytes 20 | tf_op jit(solution)/shard_map/ppermute | solution.py:48
  15.9 1.4 %broadcast_in_dim.64 = bf16[8,2,2,24,128]{4,3,2,1,0:T(8,128)(2,1)} broadcast(bf16[2,2,24,128]{3,2,1,0:T(8,128)(2,1)} %bitcast.149), dimensions={1,2,3,4} | broadcast | bytes 221184 | tf_op jit(solution)/shard_map/broadcast_in_dim | solution.py:64
  17.4 6.8 %all-to-all-start = ((bf16[8,2,2,24,128]{4,3,2,1,0:T(8,128)(2,1)}), bf16[8,2,2,24,128]{4,3,2,1,0:T(8,128)(2,1)S(1)}, u32[]{:S(2)}, u32[]{:S(2)}) async-start(bf16[8,2,2,24,128]{4,3,2,1,0:T(8,128)(2,1)} %broadcast_in_dim.64), calls=%async_computation | async-start | bytes 393216 | tf_op jit(solution)/shard_map/all_to_all | solution.py:65
  24.9 0.6 pad_add_fusion
  25.5 2.2 %collective-permute-start.1 = (s32[2,1]{0,1:T(1,128)S(1)}, s32[2,1]{0,1:T(1,128)S(1)}, u32[]{:S(2)}, u32[]{:S(2)}) collective-permute-start(s32[2,1]{0,1:T(1,128)S(1)} %pad_add_fusion), channel_id=1, source_target_pairs={{0,160},{16,176},{32,0},{48,16},{64,32},{80,48},{96,64},{112,80},{... | collective-permute-start | bytes 32 | tf_op jit(solution)/shard_map/ppermute | solution.py:48
  27.7 3.3 %collective-permute-done.1 = s32[2,1]{0,1:T(1,128)S(1)} collective-permute-done((s32[2,1]{0,1:T(1,128)S(1)}, s32[2,1]{0,1:T(1,128)S(1)}, u32[]{:S(2)}, u32[]{:S(2)}) %collective-permute-start.1) | collective-permute-done | bytes 40 | tf_op jit(solution)/shard_map/ppermute | solution.py:48
  31.0 0.6 pad_add_fusion.1
  31.6 3.4 %collective-permute-start.2 = (s32[4,1]{0,1:T(1,128)S(1)}, s32[4,1]{0,1:T(1,128)S(1)}, u32[]{:S(2)}, u32[]{:S(2)}) collective-permute-start(s32[4,1]{0,1:T(1,128)S(1)} %pad_add_fusion.1), channel_id=1, source_target_pairs={{0,128},{16,144},{32,160},{48,176},{64,0},{80,16},{96,32},{112,48}... | collective-permute-start | bytes 56 | tf_op jit(solution)/shard_map/ppermute | solution.py:48
  35.0 5.8 %collective-permute-start.3 = (s32[4,1]{0,1:T(1,128)S(1)}, s32[4,1]{0,1:T(1,128)S(1)}, u32[]{:S(2)}, u32[]{:S(2)}) collective-permute-start(s32[4,1]{0,1:T(1,128)S(1)} %pad_add_fusion.1), channel_id=1, source_target_pairs={{0,64},{16,80},{32,96},{48,112},{64,128},{80,144},{96,160},{112,17... | collective-permute-start | bytes 56 | tf_op jit(solution)/shard_map/ppermute | solution.py:48
  40.9 2.4 %collective-permute-done.3 = s32[4,1]{0,1:T(1,128)S(1)} collective-permute-done((s32[4,1]{0,1:T(1,128)S(1)}, s32[4,1]{0,1:T(1,128)S(1)}, u32[]{:S(2)}, u32[]{:S(2)}) %collective-permute-start.3) | collective-permute-done | bytes 48 | tf_op jit(solution)/shard_map/ppermute | solution.py:48
  43.2 0.7 concatenate.20
  43.9 0.7 gather_fusion
  44.7 0.6 gather_fusion.1
  45.3 0.8 select_select_fusion
  46.1 5.2 %all-to-all-start.1 = ((bf16[12,2,2,24,128]{4,3,2,1,0:T(8,128)(2,1)}), bf16[12,2,2,24,128]{4,3,2,1,0:T(8,128)(2,1)S(1)}, u32[]{:S(2)}, u32[]{:S(2)}) async-start(bf16[12,2,2,24,128]{4,3,2,1,0:T(8,128)(2,1)} %select_select_fusion), calls=%async_computation.1 | async-start | bytes 589824 | tf_op jit(solution)/shard_map/all_to_all | solution.py:95
  51.4 12.6 %all-to-all-done.1 = bf16[12,2,2,24,128]{4,3,2,1,0:T(8,128)(2,1)S(1)} async-done(((bf16[12,2,2,24,128]{4,3,2,1,0:T(8,128)(2,1)}), bf16[12,2,2,24,128]{4,3,2,1,0:T(8,128)(2,1)S(1)}, u32[]{:S(2)}, u32[]{:S(2)}) %all-to-all-start.1) | async-done | bytes 294944 | tf_op jit(solution)/shard_map/all_to_all | solution.py:95
  63.9 0.7 broadcast_in_dim.68
  64.6 10.5 %all-to-all-start.2 = ((bf16[8,2,2,24,128]{4,3,2,1,0:T(8,128)(2,1)}), bf16[8,2,2,24,128]{4,3,2,1,0:T(8,128)(2,1)S(1)}, u32[]{:S(2)}, u32[]{:S(2)}) async-start(bf16[8,2,2,24,128]{4,3,2,1,0:T(8,128)(2,1)} %broadcast_in_dim.68), calls=%async_computation.2 | async-start | bytes 393216 | tf_op jit(solution)/shard_map/all_to_all | solution.py:65
  75.2 5.9 %all-to-all-done.2 = bf16[8,2,2,24,128]{4,3,2,1,0:T(8,128)(2,1)S(1)} async-done(((bf16[8,2,2,24,128]{4,3,2,1,0:T(8,128)(2,1)}), bf16[8,2,2,24,128]{4,3,2,1,0:T(8,128)(2,1)S(1)}, u32[]{:S(2)}, u32[]{:S(2)}) %all-to-all-start.2) | async-done | bytes 196640 | tf_op jit(solution)/shard_map/all_to_all | solution.py:65
  81.7 7.4 %fusion = f32[4,2,24,5,384]{4,2,3,1,0:T(8,128)} fusion(bf16[2560,5,384]{2,0,1:T(8,128)(2,1)} %param.12, bf16[128,2560]{1,0:T(8,128)(2,1)S(1)} %copy-done, bf16[4,2,2,24,128]{4,3,2,1,0:T(8,128)(2,1)S(1)} %bitcast.150, s32[]{:T(128)S(6)} %select_n.167), kind=kOutput, calls=%fused_computation.2 | convolution fusion | flops 2013757440 | bytes 12009476 | tf_op jit(solution)/shard_map/frcd,dhe->frche/dot_general | solution.py:148
  89.1 2.8 %collective-permute-start.4 = (f32[4,2,24,5,384]{4,2,3,1,0:T(8,128)}, f32[4,2,24,5,384]{4,2,3,1,0:T(8,128)S(1)}, u32[]{:S(2)}, u32[]{:S(2)}) collective-permute-start(f32[4,2,24,5,384]{4,2,3,1,0:T(8,128)} %fusion), channel_id=1, source_target_pairs={{0,1},{1,0},{2,3},{3,2},{4,5},{5,4},{6,7},{7,6},{8,9},{9,8},{10,11... | collective-permute-start | bytes 4423688 | tf_op jit(solution)/shard_map/ppermute | solution.py:26
  91.9 7.4 %fusion.2 = f32[4,2,24,5,384]{4,2,3,1,0:T(8,128)} fusion(bf16[2560,5,384]{2,0,1:T(8,128)(2,1)} %param.12, bf16[128,2560]{1,0:T(8,128)(2,1)S(1)} %copy-done, bf16[4,2,2,24,128]{4,3,2,1,0:T(8,128)(2,1)S(1)} %bitcast.151, s32[]{:T(128)S(6)} %select_n.166), kind=kOutput, calls=%fused_computation.4 | convolution fusion | flops 2013757440 | bytes 12009476 | tf_op jit(solution)/shard_map/frcd,dhe->frche/dot_general | solution.py:148
  99.3 1.6 %add_convert_fusion = bf16[4,2,24,5,384]{4,2,3,1,0:T(8,128)(2,1)S(1)} fusion(f32[4,2,24,5,384]{4,2,3,1,0:T(8,128)} %fusion.2, f32[4,2,24,5,384]{4,2,3,1,0:T(8,128)S(1)} %collective-permute-done.4), kind=kLoop, calls=%fused_computation.15 | loop fusion | flops 737280 | bytes 3686400 | tf_op jit(solution)/shard_map/convert_element_type | solution.py:152
  100.9 1.9 %collective-permute-start.5 = (bf16[4,2,24,5,256]{4,2,3,1,0:T(8,128)(2,1)S(1)}, bf16[4,2,24,5,256]{4,2,3,1,0:T(8,128)(2,1)S(1)}, u32[]{:S(2)}, u32[]{:S(2)}) collective-permute-start(bf16[4,2,24,5,256]{4,2,3,1,0:T(8,128)(2,1)S(1)} %slice.62), channel_id=1, source_target_pairs={{0,1},{1,0},{2,3},{3,2},{4,5},{5,4},{6,7},{7,6},{8,9},{9,8},{10,11... | collective-permute-start | bytes 1474568 | tf_op jit(solution)/shard_map/ppermute | solution.py:26
  103.7 1.0 collective-permute-done.5
  106.1 0.8 convolution_convert_fusion.2
  106.8 1.1 multiply_reduce_fusion
  109.2 2.2 %collective-permute-start.6 = (bf16[2,4,2,24,5,128]{5,3,2,1,4,0:T(8,128)(2,1)S(1)}, bf16[2,4,2,24,5,128]{5,3,2,1,4,0:T(8,128)(2,1)S(1)}, u32[]{:S(2)}, u32[]{:S(2)}) collective-permute-start(bf16[2,4,2,24,5,128]{5,3,2,1,4,0:T(8,128)(2,1)S(1)} %fusion.18), channel_id=1, source_target_pairs={{0,1},{1,0},{2,3},{3,2},{4,5},{5,4},{6,7},{7,6},{8,9},{9,8},{10,11... | collective-permute-start | bytes 1474568 | tf_op jit(solution)/shard_map/ppermute | solution.py:26
  111.7 0.7 copy.24
  112.4 0.7 copy.23
  113.4 0.7 copy.25
  114.1 0.7 copy.26
  (43 shorter events, 4.0 us)
Async XLA Ops:
  0.6 81.1 %copy-start = (bf16[128,2560]{1,0:T(8,128)(2,1)S(1)}, bf16[128,2560]{1,0:T(8,128)(2,1)}, u32[]{:S(2)}) copy-start(bf16[128,2560]{1,0:T(8,128)(2,1)} %param.11) | copy-start | bytes 1966084
  0.6 24.2 %collective-permute-start = (s32[1,1]{0,1:T(1,128)}, s32[1,1]{0,1:T(1,128)}, u32[]{:S(2)}, u32[]{:S(2)}) collective-permute-start(s32[1,1]{0,1:T(1,128)} %bitcast), channel_id=1, source_target_pairs={{0,176},{16,0},{32,16},{48,32},{64,48},{80,64},{96,80},{112,96},{1... | collective-permute-start | bytes 20 | tf_op jit(solution)/shard_map/ppermute | solution.py:48
  17.4 27.3 %all-to-all-start = ((bf16[8,2,2,24,128]{4,3,2,1,0:T(8,128)(2,1)}), bf16[8,2,2,24,128]{4,3,2,1,0:T(8,128)(2,1)S(1)}, u32[]{:S(2)}, u32[]{:S(2)}) async-start(bf16[8,2,2,24,128]{4,3,2,1,0:T(8,128)(2,1)} %broadcast_in_dim.64), calls=%async_computation | async-start | bytes 393216 | tf_op jit(solution)/shard_map/all_to_all | solution.py:65
  25.5 5.5 %collective-permute-start.1 = (s32[2,1]{0,1:T(1,128)S(1)}, s32[2,1]{0,1:T(1,128)S(1)}, u32[]{:S(2)}, u32[]{:S(2)}) collective-permute-start(s32[2,1]{0,1:T(1,128)S(1)} %pad_add_fusion), channel_id=1, source_target_pairs={{0,160},{16,176},{32,0},{48,16},{64,32},{80,48},{96,64},{112,80},{... | collective-permute-start | bytes 32 | tf_op jit(solution)/shard_map/ppermute | solution.py:48
  31.6 9.2 %collective-permute-start.2 = (s32[4,1]{0,1:T(1,128)S(1)}, s32[4,1]{0,1:T(1,128)S(1)}, u32[]{:S(2)}, u32[]{:S(2)}) collective-permute-start(s32[4,1]{0,1:T(1,128)S(1)} %pad_add_fusion.1), channel_id=1, source_target_pairs={{0,128},{16,144},{32,160},{48,176},{64,0},{80,16},{96,32},{112,48}... | collective-permute-start | bytes 56 | tf_op jit(solution)/shard_map/ppermute | solution.py:48
  35.0 8.2 %collective-permute-start.3 = (s32[4,1]{0,1:T(1,128)S(1)}, s32[4,1]{0,1:T(1,128)S(1)}, u32[]{:S(2)}, u32[]{:S(2)}) collective-permute-start(s32[4,1]{0,1:T(1,128)S(1)} %pad_add_fusion.1), channel_id=1, source_target_pairs={{0,64},{16,80},{32,96},{48,112},{64,128},{80,144},{96,160},{112,17... | collective-permute-start | bytes 56 | tf_op jit(solution)/shard_map/ppermute | solution.py:48
  44.6 36.4 %copy-start.3 = (bf16[3,128,128]{2,1,0:T(8,128)(2,1)S(1)}, bf16[3,128,128]{2,1,0:T(8,128)(2,1)}, u32[]{:S(2)}) copy-start(bf16[3,128,128]{2,1,0:T(8,128)(2,1)} %param.10) | copy-start | bytes 294916
  46.1 17.8 %all-to-all-start.1 = ((bf16[12,2,2,24,128]{4,3,2,1,0:T(8,128)(2,1)}), bf16[12,2,2,24,128]{4,3,2,1,0:T(8,128)(2,1)S(1)}, u32[]{:S(2)}, u32[]{:S(2)}) async-start(bf16[12,2,2,24,128]{4,3,2,1,0:T(8,128)(2,1)} %select_select_fusion), calls=%async_computation.1 | async-start | bytes 589824 | tf_op jit(solution)/shard_map/all_to_all | solution.py:95
  64.6 16.4 %all-to-all-start.2 = ((bf16[8,2,2,24,128]{4,3,2,1,0:T(8,128)(2,1)}), bf16[8,2,2,24,128]{4,3,2,1,0:T(8,128)(2,1)S(1)}, u32[]{:S(2)}, u32[]{:S(2)}) async-start(bf16[8,2,2,24,128]{4,3,2,1,0:T(8,128)(2,1)} %broadcast_in_dim.68), calls=%async_computation.2 | async-start | bytes 393216 | tf_op jit(solution)/shard_map/all_to_all | solution.py:65
  89.1 10.2 %collective-permute-start.4 = (f32[4,2,24,5,384]{4,2,3,1,0:T(8,128)}, f32[4,2,24,5,384]{4,2,3,1,0:T(8,128)S(1)}, u32[]{:S(2)}, u32[]{:S(2)}) collective-permute-start(f32[4,2,24,5,384]{4,2,3,1,0:T(8,128)} %fusion), channel_id=1, source_target_pairs={{0,1},{1,0},{2,3},{3,2},{4,5},{5,4},{6,7},{7,6},{8,9},{9,8},{10,11... | collective-permute-start | bytes 4423688 | tf_op jit(solution)/shard_map/ppermute | solution.py:26
  99.3 4.2 %copy-start.2 = (bf16[1,4,2,24,5,128]{5,3,4,2,1,0:T(8,128)(2,1)S(1)}, bf16[1,4,2,24,5,128]{5,3,4,2,1,0:T(8,128)(2,1)}, u32[]{:S(2)}) copy-start(bf16[1,4,2,24,5,128]{5,3,4,2,1,0:T(8,128)(2,1)} %param.13) | copy-start | bytes 737284
  100.9 3.8 %collective-permute-start.5 = (bf16[4,2,24,5,256]{4,2,3,1,0:T(8,128)(2,1)S(1)}, bf16[4,2,24,5,256]{4,2,3,1,0:T(8,128)(2,1)S(1)}, u32[]{:S(2)}, u32[]{:S(2)}) collective-permute-start(bf16[4,2,24,5,256]{4,2,3,1,0:T(8,128)(2,1)S(1)} %slice.62), channel_id=1, source_target_pairs={{0,1},{1,0},{2,3},{3,2},{4,5},{5,4},{6,7},{7,6},{8,9},{9,8},{10,11... | collective-permute-start | bytes 1474568 | tf_op jit(solution)/shard_map/ppermute | solution.py:26
  109.1 3.3 %copy-start.1 = (bf16[5,128,192]{1,2,0:T(8,128)(2,1)S(1)}, bf16[5,128,192]{1,2,0:T(8,128)(2,1)}, u32[]{:S(2)}) copy-start(bf16[5,128,192]{1,2,0:T(8,128)(2,1)} %get-tuple-element.21) | copy-start | bytes 737284
  109.2 4.0 %collective-permute-start.6 = (bf16[2,4,2,24,5,128]{5,3,2,1,4,0:T(8,128)(2,1)S(1)}, bf16[2,4,2,24,5,128]{5,3,2,1,4,0:T(8,128)(2,1)S(1)}, u32[]{:S(2)}, u32[]{:S(2)}) collective-permute-start(bf16[2,4,2,24,5,128]{5,3,2,1,4,0:T(8,128)(2,1)S(1)} %fusion.18), channel_id=1, source_target_pairs={{0,1},{1,0},{2,3},{3,2},{4,5},{5,4},{6,7},{7,6},{8,9},{9,8},{10,11... | collective-permute-start | bytes 1474568 | tf_op jit(solution)/shard_map/ppermute | solution.py:26

commit v5 on v3

--- a/solution.py
+++ b/solution.py
@@ -11,7 +11,7 @@
 INNER = "mp_inner"
 MP = (OUTER, INNER)
 SLOT_MODE = 'a2a'
-ROW_MODE = 'a2a'
+ROW_MODE = 'bruck'
 FANOUT = 'a2a'
 RAW = True
 
@@ -143,12 +143,12 @@
 
     def project(piece):
         hidden = jnp.einsum(
-            "frcx,xd->frcd", piece, embed_w, preferred_element_type=jnp.float32
+            "...x,xd->...d", piece, embed_w, preferred_element_type=jnp.float32
         ).astype(jnp.bfloat16)
-        return jnp.einsum("frcd,dhe->frche", hidden, qkv_w, preferred_element_type=jnp.float32)
-
-    received = swap_seq(project(latent[:, 1]))
-    own_qkv = (project(latent[:, 0]) + received).astype(jnp.bfloat16)
+        return jnp.einsum("...d,dhe->...he", hidden, qkv_w, preferred_element_type=jnp.float32)
+
+    partial_qkv = project(latent)
+    own_qkv = (partial_qkv[:, 0] + swap_seq(partial_qkv[:, 1])).astype(jnp.bfloat16)
     own_pair = own_qkv[..., head_size:]
     other_pair = swap_seq(own_pair)
     all_pair = jnp.concatenate([own_pair, other_pair], axis=1)

time: 114 us -> 115 us (level)
  starting transfers between devices: 44.1 us -> 50.5 us
  matrix products: 17.9 us -> 11.7 us
  other arithmetic: 2.12 us -> 4.71 us
    ppermute x0 -> x3, starting transfers between devices: none -> 14.1 us  [gather_rotated(): lax.ppermute(have[:need], axis, pairs)]
    all_to_all x3 -> x2, waiting for transfers between devices: 23.1 us -> 14.7 us  [gather_a2a(): return lax.all_to_all(send, axis, 0, 0, tiled=True)]
    all_to_all x3 -> x2, starting transfers between devices: 33 us -> 25.1 us  [gather_a2a(): return lax.all_to_all(send, axis, 0, 0, tiled=True)]
    ppermute x0 -> x3, waiting for transfers between devices: none -> 6.96 us  [gather_rotated(): lax.ppermute(have[:need], axis, pairs)]
    dot_general x2, matrix products: 13.7 us -> 7.53 us  [the longest x1 6.87 us: project(): jnp.einsum('...d,dhe->...he', hidden, qkv_w, preferred_element_type=jnp.f...]
    concatenate x0 -> x3, other arithmetic: none -> 2.25 us  [gather_rotated(): jnp.concatenate([have, lax.ppermute(have[:need], axis, pairs)], axis=0)]
    broadcast_in_dim x4 -> x3, local copies, waits for them, and re-layouts: 2.75 us -> 1.31 us  [gather_a2a(): send = jnp.broadcast_to(x[None], (n,) + x.shape)]
  transfers between devices with their start and end apart: 7 -> 9, of which waited for: 6 -> 7; matrix products, arithmetic and copies ran while one was open for 2% -> 3% of each run, Pallas kernels for 0% -> 0%
where the time goes in v5:
time: 115 us; the launch traced here: 114 us
  starting transfers between devices  50.5 us (44%)
  waiting for transfers between devices  38.8 us (34%)
  matrix products  11.7 us (10%)
  local copies, waits for them, and re-layouts  6.13 us (5%)
  other arithmetic  4.71 us (4%)
  between operations  2.34 us (2%)
    all_to_all x2, starting transfers between devices, gather_a2a(): return lax.all_to_all(send, axis, 0, 0, tiled=True)  25.1 us
    all_to_all x2, waiting for transfers between devices, gather_a2a(): return lax.all_to_all(send, axis, 0, 0, tiled=True)  14.7 us
    ppermute x3, starting transfers between devices, gather_rotated(): lax.ppermute(have[:need], axis, pairs)  14.1 us
    all_to_all x1, waiting for transfers between devices, route(): got = lax.all_to_all(send, OUTER, 0, 0, tiled=True)  13.6 us
    ppermute x3, starting transfers between devices, swap_seq(): return lax.ppermute(x, 'seq', [(0, 1), (1, 0)])  7.68 us
    ppermute x3, waiting for transfers between devices, gather_rotated(): lax.ppermute(have[:need], axis, pairs)  6.96 us
    dot_general x1, matrix products, project(): jnp.einsum('...d,dhe->...he', hidden, qkv_w, preferred_element_type=jnp.f...  6.87 us
    ppermute x3, waiting for transfers between devices, swap_seq(): return lax.ppermute(x, 'seq', [(0, 1), (1, 0)])  3.55 us
  transfers between devices with their start and end apart: 9, of which 7 were waited for; matrix products, arithmetic and copies ran while one was open for 3% of the time, Pallas kernels for 0%

profile of v5, /device:TPU:1, one launch (start us, length us, event | category | flops | bytes accessed | tf_op | source)
XLA Modules:
  0.0 114.2 jit_solution(14508283657881799181)
XLA Ops:
  0.6 6.0 %collective-permute-start = (bf16[1,2,2,24,128]{4,3,2,1,0:T(8,128)(2,1)}, bf16[1,2,2,24,128]{4,3,2,1,0:T(8,128)(2,1)S(1)}, u32[]{:S(2)}, u32[]{:S(2)}) collective-permute-start(bf16[1,2,2,24,128]{4,3,2,1,0:T(8,128)(2,1)} %param.7), channel_id=1, source_target_pairs={{0,14},{2,0},{4,2},{6,4},{8,6},{10,8},{12,10},{14,12},{1,15},{3,1}... | collective-permute-start | bytes 73736 | tf_op jit(solution)/shard_map/ppermute | solution.py:48
  7.3 0.6 broadcast_in_dim.65
  7.9 14.9 %all-to-all-start = ((s32[12,1,1]{2,1,0:T(1,128)}), s32[12,1,1]{2,1,0:T(1,128)S(1)}, u32[]{:S(2)}, u32[]{:S(2)}) async-start(s32[12,1,1]{2,1,0:T(1,128)} %broadcast_in_dim.65), calls=%async_computation | async-start | bytes 12288 | tf_op jit(solution)/shard_map/all_to_all | solution.py:65
  22.9 8.8 %all-to-all-done = s32[12,1,1]{2,1,0:T(1,128)S(1)} async-done(((s32[12,1,1]{2,1,0:T(1,128)}), s32[12,1,1]{2,1,0:T(1,128)S(1)}, u32[]{:S(2)}, u32[]{:S(2)}) %all-to-all-start) | async-done | bytes 80 | tf_op jit(solution)/shard_map/all_to_all | solution.py:65
  32.0 0.7 pad_maximum_fusion.4
  32.8 3.8 %collective-permute-start.1 = (bf16[2,2,2,24,128]{4,3,2,1,0:T(8,128)(2,1)S(1)}, bf16[2,2,2,24,128]{4,3,2,1,0:T(8,128)(2,1)S(1)}, u32[]{:S(2)}, u32[]{:S(2)}) collective-permute-start(bf16[2,2,2,24,128]{4,3,2,1,0:T(8,128)(2,1)S(1)} %pad_maximum_fusion.4), channel_id=1, source_target_pairs={{0,12},{2,14},{4,0},{6,2},{8,4},{10,6},{12,8},{14,10},{1,13},{3,15... | collective-permute-start | bytes 147464 | tf_op jit(solution)/shard_map/ppermute | solution.py:48
  36.6 2.0 %collective-permute-done.1 = bf16[2,2,2,24,128]{4,3,2,1,0:T(8,128)(2,1)S(1)} collective-permute-done((bf16[2,2,2,24,128]{4,3,2,1,0:T(8,128)(2,1)S(1)}, bf16[2,2,2,24,128]{4,3,2,1,0:T(8,128)(2,1)S(1)}, u32[]{:S(2)}, u32[]{:S(2)}) %collective-permute-start.1) | collective-permute-done | bytes 49184 | tf_op jit(solution)/shard_map/ppermute | solution.py:48
  38.6 0.7 pad_maximum_fusion.3
  39.4 4.3 %collective-permute-start.2 = (bf16[4,2,2,24,128]{4,3,2,1,0:T(8,128)(2,1)S(1)}, bf16[4,2,2,24,128]{4,3,2,1,0:T(8,128)(2,1)S(1)}, u32[]{:S(2)}, u32[]{:S(2)}) collective-permute-start(bf16[4,2,2,24,128]{4,3,2,1,0:T(8,128)(2,1)S(1)} %pad_maximum_fusion.3), channel_id=1, source_target_pairs={{0,8},{2,10},{4,12},{6,14},{8,0},{10,2},{12,4},{14,6},{1,9},{3,11}... | collective-permute-start | bytes 294920 | tf_op jit(solution)/shard_map/ppermute | solution.py:48
  43.7 4.9 %collective-permute-done.2 = bf16[4,2,2,24,128]{4,3,2,1,0:T(8,128)(2,1)S(1)} collective-permute-done((bf16[4,2,2,24,128]{4,3,2,1,0:T(8,128)(2,1)S(1)}, bf16[4,2,2,24,128]{4,3,2,1,0:T(8,128)(2,1)S(1)}, u32[]{:S(2)}, u32[]{:S(2)}) %collective-permute-start.2) | collective-permute-done | bytes 98336 | tf_op jit(solution)/shard_map/ppermute | solution.py:48
  48.6 0.8 pad_maximum_fusion.2
  49.4 0.6 gather_fusion
  50.1 0.6 gather_fusion.1
  50.7 0.8 select_select_fusion
  51.5 3.5 %all-to-all-start.1 = ((bf16[12,2,2,24,128]{4,3,2,1,0:T(8,128)(2,1)}), bf16[12,2,2,24,128]{4,3,2,1,0:T(8,128)(2,1)S(1)}, u32[]{:S(2)}, u32[]{:S(2)}) async-start(bf16[12,2,2,24,128]{4,3,2,1,0:T(8,128)(2,1)} %select_select_fusion), calls=%async_computation.1 | async-start | bytes 589824 | tf_op jit(solution)/shard_map/all_to_all | solution.py:95
  55.1 13.6 %all-to-all-done.1 = bf16[12,2,2,24,128]{4,3,2,1,0:T(8,128)(2,1)S(1)} async-done(((bf16[12,2,2,24,128]{4,3,2,1,0:T(8,128)(2,1)}), bf16[12,2,2,24,128]{4,3,2,1,0:T(8,128)(2,1)S(1)}, u32[]{:S(2)}, u32[]{:S(2)}) %all-to-all-start.1) | async-done | bytes 294944 | tf_op jit(solution)/shard_map/all_to_all | solution.py:95
  68.7 0.7 broadcast_in_dim.73
  69.4 10.2 %all-to-all-start.2 = ((bf16[8,2,2,24,128]{4,3,2,1,0:T(8,128)(2,1)}), bf16[8,2,2,24,128]{4,3,2,1,0:T(8,128)(2,1)S(1)}, u32[]{:S(2)}, u32[]{:S(2)}) async-start(bf16[8,2,2,24,128]{4,3,2,1,0:T(8,128)(2,1)} %broadcast_in_dim.73), calls=%async_computation.2 | async-start | bytes 393216 | tf_op jit(solution)/shard_map/all_to_all | solution.py:65
  79.7 5.9 %all-to-all-done.2 = bf16[8,2,2,24,128]{4,3,2,1,0:T(8,128)(2,1)S(1)} async-done(((bf16[8,2,2,24,128]{4,3,2,1,0:T(8,128)(2,1)}), bf16[8,2,2,24,128]{4,3,2,1,0:T(8,128)(2,1)S(1)}, u32[]{:S(2)}, u32[]{:S(2)}) %all-to-all-start.2) | async-done | bytes 196640 | tf_op jit(solution)/shard_map/all_to_all | solution.py:65
  86.3 0.7 fusion.2
  86.9 6.9 %fusion = f32[4,2,2,24,5,384]{5,3,4,2,1,0:T(8,128)S(1)} fusion(bf16[4,2,2,24,2560,1]{4,3,5,2,1,0:T(8,128)(2,1)S(1)} %fusion.2, bf16[2560,5,384]{2,0,1:T(8,128)(2,1)} %param.12), kind=kOutput, calls=%fused_computation.2 | convolution fusion | flops 3774873600 | bytes 14745600 | tf_op jit(solution)/shard_map/...d,dhe->...he/dot_general | solution.py:148
  93.9 3.0 %collective-permute-start.3 = (f32[4,2,24,5,384]{4,2,3,1,0:T(8,128)S(1)}, f32[4,2,24,5,384]{4,2,3,1,0:T(8,128)S(1)}, u32[]{:S(2)}, u32[]{:S(2)}) collective-permute-start(f32[4,2,24,5,384]{4,2,3,1,0:T(8,128)S(1)} %slice_bitcast_fusion), channel_id=1, source_target_pairs={{0,1},{1,0},{2,3},{3,2},{4,5},{5,4},{6,7},{7,6},{8,9},{9,8},{10,11... | collective-permute-start | bytes 4423688 | tf_op jit(solution)/shard_map/ppermute | solution.py:26
  96.9 2.9 %collective-permute-done.3 = f32[4,2,24,5,384]{4,2,3,1,0:T(8,128)S(1)} collective-permute-done((f32[4,2,24,5,384]{4,2,3,1,0:T(8,128)S(1)}, f32[4,2,24,5,384]{4,2,3,1,0:T(8,128)S(1)}, u32[]{:S(2)}, u32[]{:S(2)}) %collective-permute-start.3) | collective-permute-done | bytes 1474592 | tf_op jit(solution)/shard_map/ppermute | solution.py:26
  100.0 2.3 %collective-permute-start.4 = (bf16[4,2,24,5,256]{4,2,3,1,0:T(8,128)(2,1)S(1)}, bf16[4,2,24,5,256]{4,2,3,1,0:T(8,128)(2,1)S(1)}, u32[]{:S(2)}, u32[]{:S(2)}) collective-permute-start(bf16[4,2,24,5,256]{4,2,3,1,0:T(8,128)(2,1)S(1)} %slice.72), channel_id=1, source_target_pairs={{0,1},{1,0},{2,3},{3,2},{4,5},{5,4},{6,7},{7,6},{8,9},{9,8},{10,11... | collective-permute-start | bytes 1474568 | tf_op jit(solution)/shard_map/ppermute | solution.py:26
  103.1 0.7 collective-permute-done.4
  105.2 0.8 convolution_convert_fusion.1
  106.0 1.1 multiply_reduce_fusion
  108.3 2.4 %collective-permute-start.5 = (bf16[2,4,2,24,5,128]{5,3,2,1,4,0:T(8,128)(2,1)S(1)}, bf16[2,4,2,24,5,128]{5,3,2,1,4,0:T(8,128)(2,1)S(1)}, u32[]{:S(2)}, u32[]{:S(2)}) collective-permute-start(bf16[2,4,2,24,5,128]{5,3,2,1,4,0:T(8,128)(2,1)S(1)} %fusion.16), channel_id=1, source_target_pairs={{0,1},{1,0},{2,3},{3,2},{4,5},{5,4},{6,7},{7,6},{8,9},{9,8},{10,11... | collective-permute-start | bytes 1474568 | tf_op jit(solution)/shard_map/ppermute | solution.py:26
  111.1 0.7 copy.50
  111.8 0.7 copy.49
  112.7 0.7 copy.51
  113.5 0.7 copy.52
  (45 shorter events, 4.7 us)
Async XLA Ops:
  0.6 85.6 %copy-start = (bf16[128,2560]{1,0:T(8,128)(2,1)S(1)}, bf16[128,2560]{1,0:T(8,128)(2,1)}, u32[]{:S(2)}) copy-start(bf16[128,2560]{1,0:T(8,128)(2,1)} %param.11) | copy-start | bytes 1966084
  0.6 31.4 %collective-permute-start = (bf16[1,2,2,24,128]{4,3,2,1,0:T(8,128)(2,1)}, bf16[1,2,2,24,128]{4,3,2,1,0:T(8,128)(2,1)S(1)}, u32[]{:S(2)}, u32[]{:S(2)}) collective-permute-start(bf16[1,2,2,24,128]{4,3,2,1,0:T(8,128)(2,1)} %param.7), channel_id=1, source_target_pairs={{0,14},{2,0},{4,2},{6,4},{8,6},{10,8},{12,10},{14,12},{1,15},{3,1}... | collective-permute-start | bytes 73736 | tf_op jit(solution)/shard_map/ppermute | solution.py:48
  7.9 23.8 %all-to-all-start = ((s32[12,1,1]{2,1,0:T(1,128)}), s32[12,1,1]{2,1,0:T(1,128)S(1)}, u32[]{:S(2)}, u32[]{:S(2)}) async-start(s32[12,1,1]{2,1,0:T(1,128)} %broadcast_in_dim.65), calls=%async_computation | async-start | bytes 12288 | tf_op jit(solution)/shard_map/all_to_all | solution.py:65
  32.8 5.8 %collective-permute-start.1 = (bf16[2,2,2,24,128]{4,3,2,1,0:T(8,128)(2,1)S(1)}, bf16[2,2,2,24,128]{4,3,2,1,0:T(8,128)(2,1)S(1)}, u32[]{:S(2)}, u32[]{:S(2)}) collective-permute-start(bf16[2,2,2,24,128]{4,3,2,1,0:T(8,128)(2,1)S(1)} %pad_maximum_fusion.4), channel_id=1, source_target_pairs={{0,12},{2,14},{4,0},{6,2},{8,4},{10,6},{12,8},{14,10},{1,13},{3,15... | collective-permute-start | bytes 147464 | tf_op jit(solution)/shard_map/ppermute | solution.py:48
  39.4 9.3 %collective-permute-start.2 = (bf16[4,2,2,24,128]{4,3,2,1,0:T(8,128)(2,1)S(1)}, bf16[4,2,2,24,128]{4,3,2,1,0:T(8,128)(2,1)S(1)}, u32[]{:S(2)}, u32[]{:S(2)}) collective-permute-start(bf16[4,2,2,24,128]{4,3,2,1,0:T(8,128)(2,1)S(1)} %pad_maximum_fusion.3), channel_id=1, source_target_pairs={{0,8},{2,10},{4,12},{6,14},{8,0},{10,2},{12,4},{14,6},{1,9},{3,11}... | collective-permute-start | bytes 294920 | tf_op jit(solution)/shard_map/ppermute | solution.py:48
  50.1 35.5 %copy-start.3 = (bf16[3,128,128]{2,1,0:T(8,128)(2,1)S(1)}, bf16[3,128,128]{2,1,0:T(8,128)(2,1)}, u32[]{:S(2)}) copy-start(bf16[3,128,128]{2,1,0:T(8,128)(2,1)} %param.10) | copy-start | bytes 294916
  51.5 17.2 %all-to-all-start.1 = ((bf16[12,2,2,24,128]{4,3,2,1,0:T(8,128)(2,1)}), bf16[12,2,2,24,128]{4,3,2,1,0:T(8,128)(2,1)S(1)}, u32[]{:S(2)}, u32[]{:S(2)}) async-start(bf16[12,2,2,24,128]{4,3,2,1,0:T(8,128)(2,1)} %select_select_fusion), calls=%async_computation.1 | async-start | bytes 589824 | tf_op jit(solution)/shard_map/all_to_all | solution.py:95
  69.4 16.1 %all-to-all-start.2 = ((bf16[8,2,2,24,128]{4,3,2,1,0:T(8,128)(2,1)}), bf16[8,2,2,24,128]{4,3,2,1,0:T(8,128)(2,1)S(1)}, u32[]{:S(2)}, u32[]{:S(2)}) async-start(bf16[8,2,2,24,128]{4,3,2,1,0:T(8,128)(2,1)} %broadcast_in_dim.73), calls=%async_computation.2 | async-start | bytes 393216 | tf_op jit(solution)/shard_map/all_to_all | solution.py:65
  93.9 9.1 %copy-start.2 = (bf16[1,4,2,24,5,128]{5,3,4,2,1,0:T(8,128)(2,1)S(1)}, bf16[1,4,2,24,5,128]{5,3,4,2,1,0:T(8,128)(2,1)}, u32[]{:S(2)}) copy-start(bf16[1,4,2,24,5,128]{5,3,4,2,1,0:T(8,128)(2,1)} %param.13) | copy-start | bytes 737284
  93.9 5.9 %collective-permute-start.3 = (f32[4,2,24,5,384]{4,2,3,1,0:T(8,128)S(1)}, f32[4,2,24,5,384]{4,2,3,1,0:T(8,128)S(1)}, u32[]{:S(2)}, u32[]{:S(2)}) collective-permute-start(f32[4,2,24,5,384]{4,2,3,1,0:T(8,128)S(1)} %slice_bitcast_fusion), channel_id=1, source_target_pairs={{0,1},{1,0},{2,3},{3,2},{4,5},{5,4},{6,7},{7,6},{8,9},{9,8},{10,11... | collective-permute-start | bytes 4423688 | tf_op jit(solution)/shard_map/ppermute | solution.py:26
  100.0 3.8 %collective-permute-start.4 = (bf16[4,2,24,5,256]{4,2,3,1,0:T(8,128)(2,1)S(1)}, bf16[4,2,24,5,256]{4,2,3,1,0:T(8,128)(2,1)S(1)}, u32[]{:S(2)}, u32[]{:S(2)}) collective-permute-start(bf16[4,2,24,5,256]{4,2,3,1,0:T(8,128)(2,1)S(1)} %slice.72), channel_id=1, source_target_pairs={{0,1},{1,0},{2,3},{3,2},{4,5},{5,4},{6,7},{7,6},{8,9},{9,8},{10,11... | collective-permute-start | bytes 1474568 | tf_op jit(solution)/shard_map/ppermute | solution.py:26
  108.2 3.6 %copy-start.1 = (bf16[5,128,192]{1,2,0:T(8,128)(2,1)S(1)}, bf16[5,128,192]{1,2,0:T(8,128)(2,1)}, u32[]{:S(2)}) copy-start(bf16[5,128,192]{1,2,0:T(8,128)(2,1)} %get-tuple-element.31) | copy-start | bytes 737284
  108.3 4.2 %collective-permute-start.5 = (bf16[2,4,2,24,5,128]{5,3,2,1,4,0:T(8,128)(2,1)S(1)}, bf16[2,4,2,24,5,128]{5,3,2,1,4,0:T(8,128)(2,1)S(1)}, u32[]{:S(2)}, u32[]{:S(2)}) collective-permute-start(bf16[2,4,2,24,5,128]{5,3,2,1,4,0:T(8,128)(2,1)S(1)} %fusion.16), channel_id=1, source_target_pairs={{0,1},{1,0},{2,3},{3,2},{4,5},{5,4},{6,7},{7,6},{8,9},{9,8},{10,11... | collective-permute-start | bytes 1474568 | tf_op jit(solution)/shard_map/ppermute | solution.py:26

commit v6 on v5

--- a/solution.py
+++ b/solution.py
@@ -11,7 +11,7 @@
 INNER = "mp_inner"
 MP = (OUTER, INNER)
 SLOT_MODE = 'a2a'
-ROW_MODE = 'bruck'
+ROW_MODE = 'a2a'
 FANOUT = 'a2a'
 RAW = True
 

time: 115 us -> 108 us (0.939)
  starting transfers between devices: 50.5 us -> 44.3 us
  other arithmetic: 4.71 us -> 2.33 us
    ppermute x3 -> x0, starting transfers between devices: 14.1 us -> none  [gather_rotated(): lax.ppermute(have[:need], axis, pairs)]
    all_to_all x2 -> x3, waiting for transfers between devices: 14.7 us -> 23.1 us  [gather_a2a(): return lax.all_to_all(send, axis, 0, 0, tiled=True)]
    all_to_all x2 -> x3, starting transfers between devices: 25.1 us -> 33 us  [gather_a2a(): return lax.all_to_all(send, axis, 0, 0, tiled=True)]
    ppermute x3 -> x0, waiting for transfers between devices: 6.96 us -> none  [gather_rotated(): lax.ppermute(have[:need], axis, pairs)]
    concatenate x3 -> x0, other arithmetic: 2.25 us -> none  [gather_rotated(): jnp.concatenate([have, lax.ppermute(have[:need], axis, pairs)], axis=0)]
    broadcast_in_dim x3 -> x4, local copies, waits for them, and re-layouts: 1.31 us -> 2.75 us  [gather_a2a(): send = jnp.broadcast_to(x[None], (n,) + x.shape)]
  transfers between devices with their start and end apart: 9 -> 7, of which waited for: 7 -> 6; matrix products, arithmetic and copies ran while one was open for 3% -> 2% of each run, Pallas kernels for 0% -> 0%
where the time goes in v6:
time: 108 us; the launch traced here: 107 us
  starting transfers between devices  44.3 us (41%)
  waiting for transfers between devices  39.4 us (36%)
  matrix products  11.7 us (11%)
  local copies, waits for them, and re-layouts  6.98 us (6%)
  between operations  2.34 us (2%)
  other arithmetic  2.33 us (2%)
    all_to_all x3, starting transfers between devices, gather_a2a(): return lax.all_to_all(send, axis, 0, 0, tiled=True)  33 us
    all_to_all x3, waiting for transfers between devices, gather_a2a(): return lax.all_to_all(send, axis, 0, 0, tiled=True)  23.1 us
    all_to_all x1, waiting for transfers between devices, route(): got = lax.all_to_all(send, OUTER, 0, 0, tiled=True)  12.7 us
    ppermute x3, starting transfers between devices, swap_seq(): return lax.ppermute(x, 'seq', [(0, 1), (1, 0)])  7.71 us
    dot_general x1, matrix products, project(): jnp.einsum('...d,dhe->...he', hidden, qkv_w, preferred_element_type=jnp.f...  6.87 us
    ppermute x3, waiting for transfers between devices, swap_seq(): return lax.ppermute(x, 'seq', [(0, 1), (1, 0)])  3.55 us
    all_to_all x1, starting transfers between devices, route(): got = lax.all_to_all(send, OUTER, 0, 0, tiled=True)  3.55 us
    unnamed x13, local copies, waits for them, and re-layouts  2.93 us
  transfers between devices with their start and end apart: 7, of which 6 were waited for; matrix products, arithmetic and copies ran while one was open for 2% of the time, Pallas kernels for 0%

profile of v6, /device:TPU:1, one launch (start us, length us, event | category | flops | bytes accessed | tf_op | source)
XLA Modules:
  0.0 107.0 jit_solution(3845962622214599198)
XLA Ops:
  1.4 0.6 broadcast_in_dim.62
  2.0 15.7 %all-to-all-start = ((s32[12,1,1]{2,1,0:T(1,128)}), s32[12,1,1]{2,1,0:T(1,128)S(1)}, u32[]{:S(2)}, u32[]{:S(2)}) async-start(s32[12,1,1]{2,1,0:T(1,128)} %broadcast_in_dim.62), calls=%async_computation | async-start | bytes 12288 | tf_op jit(solution)/shard_map/all_to_all | solution.py:65
  17.7 8.9 %all-to-all-done = s32[12,1,1]{2,1,0:T(1,128)S(1)} async-done(((s32[12,1,1]{2,1,0:T(1,128)}), s32[12,1,1]{2,1,0:T(1,128)S(1)}, u32[]{:S(2)}, u32[]{:S(2)}) %all-to-all-start) | async-done | bytes 80 | tf_op jit(solution)/shard_map/all_to_all | solution.py:65
  26.5 1.4 %broadcast_in_dim.66 = bf16[8,2,2,24,128]{4,3,2,1,0:T(8,128)(2,1)} broadcast(bf16[2,2,24,128]{3,2,1,0:T(8,128)(2,1)} %bitcast.128), dimensions={1,2,3,4} | broadcast | bytes 221184 | tf_op jit(solution)/shard_map/broadcast_in_dim | solution.py:64
  28.0 6.8 %all-to-all-start.1 = ((bf16[8,2,2,24,128]{4,3,2,1,0:T(8,128)(2,1)}), bf16[8,2,2,24,128]{4,3,2,1,0:T(8,128)(2,1)S(1)}, u32[]{:S(2)}, u32[]{:S(2)}) async-start(bf16[8,2,2,24,128]{4,3,2,1,0:T(8,128)(2,1)} %broadcast_in_dim.66), calls=%async_computation.1 | async-start | bytes 393216 | tf_op jit(solution)/shard_map/all_to_all | solution.py:65
  34.8 0.3 reduce
  35.2 8.4 %all-to-all-done.1 = bf16[8,2,2,24,128]{4,3,2,1,0:T(8,128)(2,1)S(1)} async-done(((bf16[8,2,2,24,128]{4,3,2,1,0:T(8,128)(2,1)}), bf16[8,2,2,24,128]{4,3,2,1,0:T(8,128)(2,1)S(1)}, u32[]{:S(2)}, u32[]{:S(2)}) %all-to-all-start.1) | async-done | bytes 196640 | tf_op jit(solution)/shard_map/all_to_all | solution.py:65
  43.5 0.6 gather_fusion
  44.1 0.8 select_select_fusion
  45.0 3.5 %all-to-all-start.2 = ((bf16[12,2,2,24,128]{4,3,2,1,0:T(8,128)(2,1)}), bf16[12,2,2,24,128]{4,3,2,1,0:T(8,128)(2,1)S(1)}, u32[]{:S(2)}, u32[]{:S(2)}) async-start(bf16[12,2,2,24,128]{4,3,2,1,0:T(8,128)(2,1)} %select_select_fusion), calls=%async_computation.2 | async-start | bytes 589824 | tf_op jit(solution)/shard_map/all_to_all | solution.py:95
  48.6 12.7 %all-to-all-done.2 = bf16[12,2,2,24,128]{4,3,2,1,0:T(8,128)(2,1)S(1)} async-done(((bf16[12,2,2,24,128]{4,3,2,1,0:T(8,128)(2,1)}), bf16[12,2,2,24,128]{4,3,2,1,0:T(8,128)(2,1)S(1)}, u32[]{:S(2)}, u32[]{:S(2)}) %all-to-all-start.2) | async-done | bytes 294944 | tf_op jit(solution)/shard_map/all_to_all | solution.py:95
  61.3 0.7 broadcast_in_dim.70
  62.0 10.5 %all-to-all-start.3 = ((bf16[8,2,2,24,128]{4,3,2,1,0:T(8,128)(2,1)}), bf16[8,2,2,24,128]{4,3,2,1,0:T(8,128)(2,1)S(1)}, u32[]{:S(2)}, u32[]{:S(2)}) async-start(bf16[8,2,2,24,128]{4,3,2,1,0:T(8,128)(2,1)} %broadcast_in_dim.70), calls=%async_computation.3 | async-start | bytes 393216 | tf_op jit(solution)/shard_map/all_to_all | solution.py:65
  72.5 5.9 %all-to-all-done.3 = bf16[8,2,2,24,128]{4,3,2,1,0:T(8,128)(2,1)S(1)} async-done(((bf16[8,2,2,24,128]{4,3,2,1,0:T(8,128)(2,1)}), bf16[8,2,2,24,128]{4,3,2,1,0:T(8,128)(2,1)S(1)}, u32[]{:S(2)}, u32[]{:S(2)}) %all-to-all-start.3) | async-done | bytes 196640 | tf_op jit(solution)/shard_map/all_to_all | solution.py:65
  79.1 0.7 fusion.2
  79.7 6.9 %fusion = f32[4,2,2,24,5,384]{5,3,4,2,1,0:T(8,128)S(1)} fusion(bf16[4,2,2,24,2560,1]{4,3,5,2,1,0:T(8,128)(2,1)S(1)} %fusion.2, bf16[2560,5,384]{2,0,1:T(8,128)(2,1)} %param.12), kind=kOutput, calls=%fused_computation.1 | convolution fusion | flops 3774873600 | bytes 14745600 | tf_op jit(solution)/shard_map/...d,dhe->...he/dot_general | solution.py:148
  86.7 3.0 %collective-permute-start = (f32[4,2,24,5,384]{4,2,3,1,0:T(8,128)S(1)}, f32[4,2,24,5,384]{4,2,3,1,0:T(8,128)S(1)}, u32[]{:S(2)}, u32[]{:S(2)}) collective-permute-start(f32[4,2,24,5,384]{4,2,3,1,0:T(8,128)S(1)} %slice_bitcast_fusion), channel_id=1, source_target_pairs={{0,1},{1,0},{2,3},{3,2},{4,5},{5,4},{6,7},{7,6},{8,9},{9,8},{10,11... | collective-permute-start | bytes 4423688 | tf_op jit(solution)/shard_map/ppermute | solution.py:26
  89.7 2.9 %collective-permute-done = f32[4,2,24,5,384]{4,2,3,1,0:T(8,128)S(1)} collective-permute-done((f32[4,2,24,5,384]{4,2,3,1,0:T(8,128)S(1)}, f32[4,2,24,5,384]{4,2,3,1,0:T(8,128)S(1)}, u32[]{:S(2)}, u32[]{:S(2)}) %collective-permute-start) | collective-permute-done | bytes 1474592 | tf_op jit(solution)/shard_map/ppermute | solution.py:26
  92.9 2.3 %collective-permute-start.1 = (bf16[4,2,24,5,256]{4,2,3,1,0:T(8,128)(2,1)S(1)}, bf16[4,2,24,5,256]{4,2,3,1,0:T(8,128)(2,1)S(1)}, u32[]{:S(2)}, u32[]{:S(2)}) collective-permute-start(bf16[4,2,24,5,256]{4,2,3,1,0:T(8,128)(2,1)S(1)} %slice.70), channel_id=1, source_target_pairs={{0,1},{1,0},{2,3},{3,2},{4,5},{5,4},{6,7},{7,6},{8,9},{9,8},{10,11... | collective-permute-start | bytes 1474568 | tf_op jit(solution)/shard_map/ppermute | solution.py:26
  96.0 0.7 collective-permute-done.1
  96.9 0.5 fusion.44
  97.4 0.6 exponential_reduce_fusion
  98.0 0.8 convolution_convert_fusion.1
  98.8 1.1 %multiply_reduce_fusion = (f32[192,5]{0,1:T(8,128)S(1)}, bf16[5,128,192]{1,2,0:T(8,128)(2,1)}) fusion(bf16[192,5,128]{2,0,1:T(8,128)(2,1)S(1)} %bitcast.116, bf16[384,5,128]{2,0,1:T(8,128)(2,1)S(1)} %bitcast.107, f32[5,192,384]{2,1,0:T(8,128)S(1)} %get-tuple-element.29, f32[5,192]{1,0:T(8,128)S(1)} %log_add_fusion), kind=kOutput, calls=%fused_computation.37 | convolution fusion | flops 95722560 | bytes 2465280 | tf_op jit(solution)/shard_map/hqk,khd->qhd/dot_general | solution.py:169
  99.9 0.5 fusion.5
  100.4 0.4 fusion.8
  101.1 2.4 %collective-permute-start.2 = (bf16[2,4,2,24,5,128]{5,3,2,1,4,0:T(8,128)(2,1)S(1)}, bf16[2,4,2,24,5,128]{5,3,2,1,4,0:T(8,128)(2,1)S(1)}, u32[]{:S(2)}, u32[]{:S(2)}) collective-permute-start(bf16[2,4,2,24,5,128]{5,3,2,1,4,0:T(8,128)(2,1)S(1)} %fusion.16), channel_id=1, source_target_pairs={{0,1},{1,0},{2,3},{3,2},{4,5},{5,4},{6,7},{7,6},{8,9},{9,8},{10,11... | collective-permute-start | bytes 1474568 | tf_op jit(solution)/shard_map/ppermute | solution.py:26
  103.6 0.4 fusion.9
  103.9 0.7 copy.50
  104.6 0.7 copy.49
  105.6 0.7 copy.51
  106.3 0.7 copy.52
  (34 shorter events, 2.0 us)
Async XLA Ops:
  0.6 78.4 %copy-start = (bf16[128,2560]{1,0:T(8,128)(2,1)S(1)}, bf16[128,2560]{1,0:T(8,128)(2,1)}, u32[]{:S(2)}) copy-start(bf16[128,2560]{1,0:T(8,128)(2,1)} %param.11) | copy-start | bytes 1966084
  2.0 24.6 %all-to-all-start = ((s32[12,1,1]{2,1,0:T(1,128)}), s32[12,1,1]{2,1,0:T(1,128)S(1)}, u32[]{:S(2)}, u32[]{:S(2)}) async-start(s32[12,1,1]{2,1,0:T(1,128)} %broadcast_in_dim.62), calls=%async_computation | async-start | bytes 12288 | tf_op jit(solution)/shard_map/all_to_all | solution.py:65
  28.0 15.6 %all-to-all-start.1 = ((bf16[8,2,2,24,128]{4,3,2,1,0:T(8,128)(2,1)}), bf16[8,2,2,24,128]{4,3,2,1,0:T(8,128)(2,1)S(1)}, u32[]{:S(2)}, u32[]{:S(2)}) async-start(bf16[8,2,2,24,128]{4,3,2,1,0:T(8,128)(2,1)} %broadcast_in_dim.66), calls=%async_computation.1 | async-start | bytes 393216 | tf_op jit(solution)/shard_map/all_to_all | solution.py:65
  35.2 43.3 %copy-start.3 = (bf16[3,128,128]{2,1,0:T(8,128)(2,1)S(1)}, bf16[3,128,128]{2,1,0:T(8,128)(2,1)}, u32[]{:S(2)}) copy-start(bf16[3,128,128]{2,1,0:T(8,128)(2,1)} %param.10) | copy-start | bytes 294916
  45.0 16.3 %all-to-all-start.2 = ((bf16[12,2,2,24,128]{4,3,2,1,0:T(8,128)(2,1)}), bf16[12,2,2,24,128]{4,3,2,1,0:T(8,128)(2,1)S(1)}, u32[]{:S(2)}, u32[]{:S(2)}) async-start(bf16[12,2,2,24,128]{4,3,2,1,0:T(8,128)(2,1)} %select_select_fusion), calls=%async_computation.2 | async-start | bytes 589824 | tf_op jit(solution)/shard_map/all_to_all | solution.py:95
  62.0 16.4 %all-to-all-start.3 = ((bf16[8,2,2,24,128]{4,3,2,1,0:T(8,128)(2,1)}), bf16[8,2,2,24,128]{4,3,2,1,0:T(8,128)(2,1)S(1)}, u32[]{:S(2)}, u32[]{:S(2)}) async-start(bf16[8,2,2,24,128]{4,3,2,1,0:T(8,128)(2,1)} %broadcast_in_dim.70), calls=%async_computation.3 | async-start | bytes 393216 | tf_op jit(solution)/shard_map/all_to_all | solution.py:65
  86.7 9.1 %copy-start.2 = (bf16[1,4,2,24,5,128]{5,3,4,2,1,0:T(8,128)(2,1)S(1)}, bf16[1,4,2,24,5,128]{5,3,4,2,1,0:T(8,128)(2,1)}, u32[]{:S(2)}) copy-start(bf16[1,4,2,24,5,128]{5,3,4,2,1,0:T(8,128)(2,1)} %param.13) | copy-start | bytes 737284
  86.7 5.9 %collective-permute-start = (f32[4,2,24,5,384]{4,2,3,1,0:T(8,128)S(1)}, f32[4,2,24,5,384]{4,2,3,1,0:T(8,128)S(1)}, u32[]{:S(2)}, u32[]{:S(2)}) collective-permute-start(f32[4,2,24,5,384]{4,2,3,1,0:T(8,128)S(1)} %slice_bitcast_fusion), channel_id=1, source_target_pairs={{0,1},{1,0},{2,3},{3,2},{4,5},{5,4},{6,7},{7,6},{8,9},{9,8},{10,11... | collective-permute-start | bytes 4423688 | tf_op jit(solution)/shard_map/ppermute | solution.py:26
  92.9 3.8 %collective-permute-start.1 = (bf16[4,2,24,5,256]{4,2,3,1,0:T(8,128)(2,1)S(1)}, bf16[4,2,24,5,256]{4,2,3,1,0:T(8,128)(2,1)S(1)}, u32[]{:S(2)}, u32[]{:S(2)}) collective-permute-start(bf16[4,2,24,5,256]{4,2,3,1,0:T(8,128)(2,1)S(1)} %slice.70), channel_id=1, source_target_pairs={{0,1},{1,0},{2,3},{3,2},{4,5},{5,4},{6,7},{7,6},{8,9},{9,8},{10,11... | collective-permute-start | bytes 1474568 | tf_op jit(solution)/shard_map/ppermute | solution.py:26
  101.1 3.6 %copy-start.1 = (bf16[5,128,192]{1,2,0:T(8,128)(2,1)S(1)}, bf16[5,128,192]{1,2,0:T(8,128)(2,1)}, u32[]{:S(2)}) copy-start(bf16[5,128,192]{1,2,0:T(8,128)(2,1)} %get-tuple-element.31) | copy-start | bytes 737284
  101.1 4.2 %collective-permute-start.2 = (bf16[2,4,2,24,5,128]{5,3,2,1,4,0:T(8,128)(2,1)S(1)}, bf16[2,4,2,24,5,128]{5,3,2,1,4,0:T(8,128)(2,1)S(1)}, u32[]{:S(2)}, u32[]{:S(2)}) collective-permute-start(bf16[2,4,2,24,5,128]{5,3,2,1,4,0:T(8,128)(2,1)S(1)} %fusion.16), channel_id=1, source_target_pairs={{0,1},{1,0},{2,3},{3,2},{4,5},{5,4},{6,7},{7,6},{8,9},{9,8},{10,11... | collective-permute-start | bytes 1474568 | tf_op jit(solution)/shard_map/ppermute | solution.py:26

commit v7 on v6

--- a/solution.py
+++ b/solution.py
@@ -13,7 +13,7 @@
 SLOT_MODE = 'a2a'
 ROW_MODE = 'a2a'
 FANOUT = 'a2a'
-RAW = True
+RAW = False
 
 
 def passed_along(shard, axis, by):

time: 108 us -> 104 us (0.963)
  waiting for transfers between devices: 39.4 us -> 30 us
  starting transfers between devices: 44.3 us -> 47.4 us
  matrix products: 11.7 us -> 13.8 us
    all_to_all x3, waiting for transfers between devices: 23.1 us -> 15.8 us  [gather_a2a(): return lax.all_to_all(send, axis, 0, 0, tiled=True)]
    ppermute x0 -> x1, starting transfers between devices: none -> 3.1 us  [passed_along(): return lax.ppermute(shard, axis, pairs)]
    all_to_all x1, starting transfers between devices: 3.55 us -> 5.9 us  [route(): got = lax.all_to_all(send, OUTER, 0, 0, tiled=True)]
    all_to_all x3, starting transfers between devices: 33 us -> 30.9 us  [gather_a2a(): return lax.all_to_all(send, axis, 0, 0, tiled=True)]
    dot_general x3, matrix products: 0.59 us -> 2.73 us  [the longest x1 0.91 us: causal_conv(): jnp.einsum('rcx,xy->rcy', frames[0], conv_w[1], preferred_element_type=jn...]
    all_to_all x1, waiting for transfers between devices: 12.7 us -> 10.7 us  [route(): got = lax.all_to_all(send, OUTER, 0, 0, tiled=True)]
    unnamed x13 -> x11, local copies, waits for them, and re-layouts: 2.93 us -> 2.92 us
  transfers between devices with their start and end apart: 7 -> 8, of which waited for: 6 -> 6; matrix products, arithmetic and copies ran while one was open for 2% -> 5% of each run, Pallas kernels for 0% -> 0%
where the time goes in v7:
time: 104 us; the launch traced here: 103 us
  starting transfers between devices  47.4 us (46%)
  waiting for transfers between devices  30 us (29%)
  matrix products  13.8 us (13%)
  local copies, waits for them, and re-layouts  6.78 us (7%)
  between operations  2.3 us (2%)
  other arithmetic  2.26 us (2%)
    all_to_all x3, starting transfers between devices, gather_a2a(): return lax.all_to_all(send, axis, 0, 0, tiled=True)  30.9 us
    all_to_all x3, waiting for transfers between devices, gather_a2a(): return lax.all_to_all(send, axis, 0, 0, tiled=True)  15.8 us
    all_to_all x1, waiting for transfers between devices, route(): got = lax.all_to_all(send, OUTER, 0, 0, tiled=True)  10.7 us
    ppermute x3, starting transfers between devices, swap_seq(): return lax.ppermute(x, 'seq', [(0, 1), (1, 0)])  7.55 us
    dot_general x1, matrix products, project(): jnp.einsum('...d,dhe->...he', hidden, qkv_w, preferred_element_type=jnp.f...  6.88 us
    all_to_all x1, starting transfers between devices, route(): got = lax.all_to_all(send, OUTER, 0, 0, tiled=True)  5.9 us
    ppermute x3, waiting for transfers between devices, swap_seq(): return lax.ppermute(x, 'seq', [(0, 1), (1, 0)])  3.55 us
    ppermute x1, starting transfers between devices, passed_along(): return lax.ppermute(shard, axis, pairs)  3.1 us
  transfers between devices with their start and end apart: 8, of which 6 were waited for; matrix products, arithmetic and copies ran while one was open for 5% of the time, Pallas kernels for 0%

profile of v7, /device:TPU:1, one launch (start us, length us, event | category | flops | bytes accessed | tf_op | source)
XLA Modules:
  0.0 102.6 jit_solution(7414949692732603843)
XLA Ops:
  1.4 0.6 broadcast_in_dim.60
  2.0 15.7 %all-to-all-start = ((s32[12,1,1]{2,1,0:T(1,128)}), s32[12,1,1]{2,1,0:T(1,128)S(1)}, u32[]{:S(2)}, u32[]{:S(2)}) async-start(s32[12,1,1]{2,1,0:T(1,128)} %broadcast_in_dim.60), calls=%async_computation | async-start | bytes 12288 | tf_op jit(solution)/shard_map/all_to_all | solution.py:65
  17.7 0.7 slice_bitcast_fusion.2
  18.4 3.1 %collective-permute-start = (bf16[1,2,24,128]{3,2,1,0:T(8,128)(2,1)S(1)}, bf16[1,2,24,128]{3,2,1,0:T(8,128)(2,1)S(1)}, u32[]{:S(2)}, u32[]{:S(2)}) collective-permute-start(bf16[1,2,24,128]{3,2,1,0:T(8,128)(2,1)S(1)} %slice_bitcast_fusion.2), channel_id=1, source_target_pairs={{0,192},{192,384},{384,576},{1,193},{193,385},{385,577},{2,194},{1... | collective-permute-start | bytes 36872 | tf_op jit(solution)/shard_map/ppermute | solution.py:22
  21.5 0.9 fusion.23
  22.4 0.9 convolution_add_fusion.1
  23.3 3.2 %all-to-all-done = s32[12,1,1]{2,1,0:T(1,128)S(1)} async-done(((s32[12,1,1]{2,1,0:T(1,128)}), s32[12,1,1]{2,1,0:T(1,128)S(1)}, u32[]{:S(2)}, u32[]{:S(2)}) %all-to-all-start) | async-done | bytes 80 | tf_op jit(solution)/shard_map/all_to_all | solution.py:65
  26.9 0.9 multiply_convert_fusion
  27.8 0.7 broadcast_in_dim.63
  28.5 6.8 %all-to-all-start.1 = ((bf16[8,2,24,128]{3,2,1,0:T(8,128)(2,1)}), bf16[8,2,24,128]{3,2,1,0:T(8,128)(2,1)S(1)}, u32[]{:S(2)}, u32[]{:S(2)}) async-start(bf16[8,2,24,128]{3,2,1,0:T(8,128)(2,1)} %broadcast_in_dim.63), calls=%async_computation.1 | async-start | bytes 196608 | tf_op jit(solution)/shard_map/all_to_all | solution.py:65
  35.3 7.6 %all-to-all-done.1 = bf16[8,2,24,128]{3,2,1,0:T(8,128)(2,1)S(1)} async-done(((bf16[8,2,24,128]{3,2,1,0:T(8,128)(2,1)}), bf16[8,2,24,128]{3,2,1,0:T(8,128)(2,1)S(1)}, u32[]{:S(2)}, u32[]{:S(2)}) %all-to-all-start.1) | async-done | bytes 98336 | tf_op jit(solution)/shard_map/all_to_all | solution.py:65
  42.9 0.6 gather_fusion
  43.4 0.8 select_select_fusion
  44.2 5.9 %all-to-all-start.2 = ((bf16[12,2,24,128]{3,2,1,0:T(8,128)(2,1)}), bf16[12,2,24,128]{3,2,1,0:T(8,128)(2,1)S(1)}, u32[]{:S(2)}, u32[]{:S(2)}) async-start(bf16[12,2,24,128]{3,2,1,0:T(8,128)(2,1)} %select_select_fusion), calls=%async_computation.2 | async-start | bytes 294912 | tf_op jit(solution)/shard_map/all_to_all | solution.py:95
  50.1 10.7 %all-to-all-done.2 = bf16[12,2,24,128]{3,2,1,0:T(8,128)(2,1)S(1)} async-done(((bf16[12,2,24,128]{3,2,1,0:T(8,128)(2,1)}), bf16[12,2,24,128]{3,2,1,0:T(8,128)(2,1)S(1)}, u32[]{:S(2)}, u32[]{:S(2)}) %all-to-all-start.2) | async-done | bytes 147488 | tf_op jit(solution)/shard_map/all_to_all | solution.py:95
  60.8 0.7 broadcast_in_dim.67
  61.5 8.3 %all-to-all-start.3 = ((bf16[8,2,24,128]{3,2,1,0:T(8,128)(2,1)}), bf16[8,2,24,128]{3,2,1,0:T(8,128)(2,1)S(1)}, u32[]{:S(2)}, u32[]{:S(2)}) async-start(bf16[8,2,24,128]{3,2,1,0:T(8,128)(2,1)} %broadcast_in_dim.67), calls=%async_computation.3 | async-start | bytes 196608 | tf_op jit(solution)/shard_map/all_to_all | solution.py:65
  69.8 5.0 %all-to-all-done.3 = bf16[8,2,24,128]{3,2,1,0:T(8,128)(2,1)S(1)} async-done(((bf16[8,2,24,128]{3,2,1,0:T(8,128)(2,1)}), bf16[8,2,24,128]{3,2,1,0:T(8,128)(2,1)S(1)}, u32[]{:S(2)}, u32[]{:S(2)}) %all-to-all-start.3) | async-done | bytes 98336 | tf_op jit(solution)/shard_map/all_to_all | solution.py:65
  74.8 0.7 fusion.2
  75.5 6.9 %fusion = f32[4,2,2,24,5,384]{5,3,4,2,1,0:T(8,128)S(1)} fusion(bf16[4,2,2,24,2560,1]{4,3,5,2,1,0:T(8,128)(2,1)S(1)} %fusion.2, bf16[2560,5,384]{2,0,1:T(8,128)(2,1)} %param.12), kind=kOutput, calls=%fused_computation.1 | convolution fusion | flops 3774873600 | bytes 14745600 | tf_op jit(solution)/shard_map/...d,dhe->...he/dot_general | solution.py:148
  82.5 2.9 %collective-permute-start.1 = (f32[4,2,24,5,384]{4,2,3,1,0:T(8,128)S(1)}, f32[4,2,24,5,384]{4,2,3,1,0:T(8,128)S(1)}, u32[]{:S(2)}, u32[]{:S(2)}) collective-permute-start(f32[4,2,24,5,384]{4,2,3,1,0:T(8,128)S(1)} %slice_bitcast_fusion), channel_id=1, source_target_pairs={{0,1},{1,0},{2,3},{3,2},{4,5},{5,4},{6,7},{7,6},{8,9},{9,8},{10,11... | collective-permute-start | bytes 4423688 | tf_op jit(solution)/shard_map/ppermute | solution.py:26
  85.4 2.9 %collective-permute-done.1 = f32[4,2,24,5,384]{4,2,3,1,0:T(8,128)S(1)} collective-permute-done((f32[4,2,24,5,384]{4,2,3,1,0:T(8,128)S(1)}, f32[4,2,24,5,384]{4,2,3,1,0:T(8,128)S(1)}, u32[]{:S(2)}, u32[]{:S(2)}) %collective-permute-start.1) | collective-permute-done | bytes 1474592 | tf_op jit(solution)/shard_map/ppermute | solution.py:26
  88.5 2.3 %collective-permute-start.2 = (bf16[4,2,24,5,256]{4,2,3,1,0:T(8,128)(2,1)S(1)}, bf16[4,2,24,5,256]{4,2,3,1,0:T(8,128)(2,1)S(1)}, u32[]{:S(2)}, u32[]{:S(2)}) collective-permute-start(bf16[4,2,24,5,256]{4,2,3,1,0:T(8,128)(2,1)S(1)} %slice.71), channel_id=1, source_target_pairs={{0,1},{1,0},{2,3},{3,2},{4,5},{5,4},{6,7},{7,6},{8,9},{9,8},{10,11... | collective-permute-start | bytes 1474568 | tf_op jit(solution)/shard_map/ppermute | solution.py:26
  91.6 0.7 collective-permute-done.2
  93.0 0.6 exponential_reduce_fusion
  93.7 0.8 convolution_convert_fusion.1
  94.4 1.1 %multiply_reduce_fusion = (f32[192,5]{0,1:T(8,128)S(1)}, bf16[5,128,192]{1,2,0:T(8,128)(2,1)}) fusion(bf16[192,5,128]{2,0,1:T(8,128)(2,1)S(1)} %bitcast.115, bf16[384,5,128]{2,0,1:T(8,128)(2,1)S(1)} %bitcast.106, f32[5,192,384]{2,1,0:T(8,128)S(1)} %get-tuple-element.29, f32[5,192]{1,0:T(8,128)S(1)} %log_add_fusion), kind=kOutput, calls=%fused_computation.37 | convolution fusion | flops 95722560 | bytes 2465280 | tf_op jit(solution)/shard_map/hqk,khd->qhd/dot_general | solution.py:169
  96.8 2.4 %collective-permute-start.3 = (bf16[2,4,2,24,5,128]{5,3,2,1,4,0:T(8,128)(2,1)S(1)}, bf16[2,4,2,24,5,128]{5,3,2,1,4,0:T(8,128)(2,1)S(1)}, u32[]{:S(2)}, u32[]{:S(2)}) collective-permute-start(bf16[2,4,2,24,5,128]{5,3,2,1,4,0:T(8,128)(2,1)S(1)} %fusion.15), channel_id=1, source_target_pairs={{0,1},{1,0},{2,3},{3,2},{4,5},{5,4},{6,7},{7,6},{8,9},{9,8},{10,11... | collective-permute-start | bytes 1474568 | tf_op jit(solution)/shard_map/ppermute | solution.py:26
  99.5 0.7 copy.47
  100.3 0.7 copy.46
  101.2 0.7 copy.48
  101.9 0.7 copy.49
  (33 shorter events, 3.3 us)
Async XLA Ops:
  0.6 74.2 %copy-start = (bf16[128,2560]{1,0:T(8,128)(2,1)S(1)}, bf16[128,2560]{1,0:T(8,128)(2,1)}, u32[]{:S(2)}) copy-start(bf16[128,2560]{1,0:T(8,128)(2,1)} %param.11) | copy-start | bytes 1966084
  2.0 24.6 %all-to-all-start = ((s32[12,1,1]{2,1,0:T(1,128)}), s32[12,1,1]{2,1,0:T(1,128)S(1)}, u32[]{:S(2)}, u32[]{:S(2)}) async-start(s32[12,1,1]{2,1,0:T(1,128)} %broadcast_in_dim.60), calls=%async_computation | async-start | bytes 12288 | tf_op jit(solution)/shard_map/all_to_all | solution.py:65
  18.4 8.5 %collective-permute-start = (bf16[1,2,24,128]{3,2,1,0:T(8,128)(2,1)S(1)}, bf16[1,2,24,128]{3,2,1,0:T(8,128)(2,1)S(1)}, u32[]{:S(2)}, u32[]{:S(2)}) collective-permute-start(bf16[1,2,24,128]{3,2,1,0:T(8,128)(2,1)S(1)} %slice_bitcast_fusion.2), channel_id=1, source_target_pairs={{0,192},{192,384},{384,576},{1,193},{193,385},{385,577},{2,194},{1... | collective-permute-start | bytes 36872 | tf_op jit(solution)/shard_map/ppermute | solution.py:22
  28.5 14.4 %all-to-all-start.1 = ((bf16[8,2,24,128]{3,2,1,0:T(8,128)(2,1)}), bf16[8,2,24,128]{3,2,1,0:T(8,128)(2,1)S(1)}, u32[]{:S(2)}, u32[]{:S(2)}) async-start(bf16[8,2,24,128]{3,2,1,0:T(8,128)(2,1)} %broadcast_in_dim.63), calls=%async_computation.1 | async-start | bytes 196608 | tf_op jit(solution)/shard_map/all_to_all | solution.py:65
  44.2 16.6 %all-to-all-start.2 = ((bf16[12,2,24,128]{3,2,1,0:T(8,128)(2,1)}), bf16[12,2,24,128]{3,2,1,0:T(8,128)(2,1)S(1)}, u32[]{:S(2)}, u32[]{:S(2)}) async-start(bf16[12,2,24,128]{3,2,1,0:T(8,128)(2,1)} %select_select_fusion), calls=%async_computation.2 | async-start | bytes 294912 | tf_op jit(solution)/shard_map/all_to_all | solution.py:95
  61.5 13.3 %all-to-all-start.3 = ((bf16[8,2,24,128]{3,2,1,0:T(8,128)(2,1)}), bf16[8,2,24,128]{3,2,1,0:T(8,128)(2,1)S(1)}, u32[]{:S(2)}, u32[]{:S(2)}) async-start(bf16[8,2,24,128]{3,2,1,0:T(8,128)(2,1)} %broadcast_in_dim.67), calls=%async_computation.3 | async-start | bytes 196608 | tf_op jit(solution)/shard_map/all_to_all | solution.py:65
  82.5 9.0 %copy-start.2 = (bf16[1,4,2,24,5,128]{5,3,4,2,1,0:T(8,128)(2,1)S(1)}, bf16[1,4,2,24,5,128]{5,3,4,2,1,0:T(8,128)(2,1)}, u32[]{:S(2)}) copy-start(bf16[1,4,2,24,5,128]{5,3,4,2,1,0:T(8,128)(2,1)} %param.13) | copy-start | bytes 737284
  82.5 5.7 %collective-permute-start.1 = (f32[4,2,24,5,384]{4,2,3,1,0:T(8,128)S(1)}, f32[4,2,24,5,384]{4,2,3,1,0:T(8,128)S(1)}, u32[]{:S(2)}, u32[]{:S(2)}) collective-permute-start(f32[4,2,24,5,384]{4,2,3,1,0:T(8,128)S(1)} %slice_bitcast_fusion), channel_id=1, source_target_pairs={{0,1},{1,0},{2,3},{3,2},{4,5},{5,4},{6,7},{7,6},{8,9},{9,8},{10,11... | collective-permute-start | bytes 4423688 | tf_op jit(solution)/shard_map/ppermute | solution.py:26
  88.5 3.8 %collective-permute-start.2 = (bf16[4,2,24,5,256]{4,2,3,1,0:T(8,128)(2,1)S(1)}, bf16[4,2,24,5,256]{4,2,3,1,0:T(8,128)(2,1)S(1)}, u32[]{:S(2)}, u32[]{:S(2)}) collective-permute-start(bf16[4,2,24,5,256]{4,2,3,1,0:T(8,128)(2,1)S(1)} %slice.71), channel_id=1, source_target_pairs={{0,1},{1,0},{2,3},{3,2},{4,5},{5,4},{6,7},{7,6},{8,9},{9,8},{10,11... | collective-permute-start | bytes 1474568 | tf_op jit(solution)/shard_map/ppermute | solution.py:26
  96.7 3.6 %copy-start.1 = (bf16[5,128,192]{1,2,0:T(8,128)(2,1)S(1)}, bf16[5,128,192]{1,2,0:T(8,128)(2,1)}, u32[]{:S(2)}) copy-start(bf16[5,128,192]{1,2,0:T(8,128)(2,1)} %get-tuple-element.31) | copy-start | bytes 737284
  96.8 4.2 %collective-permute-start.3 = (bf16[2,4,2,24,5,128]{5,3,2,1,4,0:T(8,128)(2,1)S(1)}, bf16[2,4,2,24,5,128]{5,3,2,1,4,0:T(8,128)(2,1)S(1)}, u32[]{:S(2)}, u32[]{:S(2)}) collective-permute-start(bf16[2,4,2,24,5,128]{5,3,2,1,4,0:T(8,128)(2,1)S(1)} %fusion.15), channel_id=1, source_target_pairs={{0,1},{1,0},{2,3},{3,2},{4,5},{5,4},{6,7},{7,6},{8,9},{9,8},{10,11... | collective-permute-start | bytes 1474568 | tf_op jit(solution)/shard_map/ppermute | solution.py:26

commit v8 on v7

--- a/solution.py
+++ b/solution.py
@@ -78,21 +78,15 @@
     n_out = lax.axis_size(OUTER)
     my_out = lax.axis_index(OUTER)
     source = tokenizer_slot[0]
-    wanted = gather(tokenizer_slot, OUTER, SLOT_MODE)[:, 0]
-    row = gather(piece, INNER, ROW_MODE)
-    pick = jnp.clip(wanted % n_in, 0, n_in - 1)
-    mine = (wanted // n_in) == my_out
-    send = jnp.take(row, pick, axis=0)
-    send = jnp.where(mine.reshape((n_out,) + (1,) * piece.ndim), send, jnp.zeros_like(send))
-    origin = jnp.clip(source // n_in, 0, n_out - 1)
-    if FANOUT == "merged":
-        n_grp = lax.axis_size("segment") * lax.axis_size("seq")
-        wide = jnp.broadcast_to(send[:, None], (n_out, n_grp) + piece.shape)
-        wide = wide.reshape((n_out * n_grp,) + piece.shape)
-        got = lax.all_to_all(wide, (OUTER, "segment", "seq"), 0, 0, tiled=True)
-        got = got.reshape((n_out, n_grp) + piece.shape)
-        return lax.dynamic_index_in_dim(got, origin, 0, keepdims=False)
-    got = lax.all_to_all(send, OUTER, 0, 0, tiled=True)
+    my_in = lax.axis_index(INNER)
+    wanted = gather(tokenizer_slot, INNER, SLOT_MODE)[:, 0]
+    column = gather(piece, OUTER, ROW_MODE)
+    pick = jnp.clip(wanted // n_in, 0, n_out - 1)
+    mine = (wanted % n_in) == my_in
+    send = jnp.take(column, pick, axis=0)
+    send = jnp.where(mine.reshape((n_in,) + (1,) * piece.ndim), send, jnp.zeros_like(send))
+    origin = jnp.clip(source % n_in, 0, n_in - 1)
+    got = lax.all_to_all(send, INNER, 0, 0, tiled=True)
     routed = lax.dynamic_index_in_dim(got, origin, 0, keepdims=False)
     return gather(routed, ("segment", "seq"), FANOUT)
 

time: 104 us -> 102 us (0.981)
  waiting for transfers between devices: 30 us -> 27.6 us
    all_to_all x1, waiting for transfers between devices: 10.7 us -> 7.58 us  [route(): got = lax.all_to_all(send, INNER, 0, 0, tiled=True)]
where the time goes in v8:
time: 102 us; the launch traced here: 101 us
  starting transfers between devices  48 us (47%)
  waiting for transfers between devices  27.6 us (27%)
  matrix products  13.9 us (14%)
  local copies, waits for them, and re-layouts  6.79 us (7%)
  between operations  2.26 us (2%)
  other arithmetic  2.16 us (2%)
    all_to_all x3, starting transfers between devices, gather_a2a(): return lax.all_to_all(send, axis, 0, 0, tiled=True)  31.5 us
    all_to_all x3, waiting for transfers between devices, gather_a2a(): return lax.all_to_all(send, axis, 0, 0, tiled=True)  16.5 us
    all_to_all x1, waiting for transfers between devices, route(): got = lax.all_to_all(send, INNER, 0, 0, tiled=True)  7.58 us
    ppermute x3, starting transfers between devices, swap_seq(): return lax.ppermute(x, 'seq', [(0, 1), (1, 0)])  7.56 us
    dot_general x1, matrix products, project(): jnp.einsum('...d,dhe->...he', hidden, qkv_w, preferred_element_type=jnp.f...  6.87 us
    all_to_all x1, starting transfers between devices, route(): got = lax.all_to_all(send, INNER, 0, 0, tiled=True)  5.82 us
    ppermute x3, waiting for transfers between devices, swap_seq(): return lax.ppermute(x, 'seq', [(0, 1), (1, 0)])  3.55 us
    ppermute x1, starting transfers between devices, passed_along(): return lax.ppermute(shard, axis, pairs)  3.1 us
  transfers between devices with their start and end apart: 8, of which 6 were waited for; matrix products, arithmetic and copies ran while one was open for 5% of the time, Pallas kernels for 0%

profile of v8, /device:TPU:1, one launch (start us, length us, event | category | flops | bytes accessed | tf_op | source)
XLA Modules:
  0.0 100.7 jit_solution(4323348918736773576)
XLA Ops:
  1.4 0.6 broadcast_in_dim.60
  2.0 7.6 %all-to-all-start = ((s32[8,1,1]{2,1,0:T(1,128)}), s32[8,1,1]{2,1,0:T(1,128)S(1)}, u32[]{:S(2)}, u32[]{:S(2)}) async-start(s32[8,1,1]{2,1,0:T(1,128)} %broadcast_in_dim.60), calls=%async_computation | async-start | bytes 8192 | tf_op jit(solution)/shard_map/all_to_all | solution.py:65
  9.6 0.7 slice_bitcast_fusion.2
  10.3 3.1 %collective-permute-start = (bf16[1,2,24,128]{3,2,1,0:T(8,128)(2,1)S(1)}, bf16[1,2,24,128]{3,2,1,0:T(8,128)(2,1)S(1)}, u32[]{:S(2)}, u32[]{:S(2)}) collective-permute-start(bf16[1,2,24,128]{3,2,1,0:T(8,128)(2,1)S(1)} %slice_bitcast_fusion.2), channel_id=1, source_target_pairs={{0,192},{192,384},{384,576},{1,193},{193,385},{385,577},{2,194},{1... | collective-permute-start | bytes 36872 | tf_op jit(solution)/shard_map/ppermute | solution.py:22
  13.4 0.9 fusion.23
  14.3 0.9 convolution_add_fusion.1
  15.2 0.8 all-to-all-done
  16.3 0.9 multiply_convert_fusion
  17.2 0.7 broadcast_in_dim.63
  17.9 14.9 %all-to-all-start.1 = ((bf16[12,2,24,128]{3,2,1,0:T(8,128)(2,1)}), bf16[12,2,24,128]{3,2,1,0:T(8,128)(2,1)S(1)}, u32[]{:S(2)}, u32[]{:S(2)}) async-start(bf16[12,2,24,128]{3,2,1,0:T(8,128)(2,1)} %broadcast_in_dim.63), calls=%async_computation.1 | async-start | bytes 294912 | tf_op jit(solution)/shard_map/all_to_all | solution.py:65
  32.9 10.7 %all-to-all-done.1 = bf16[12,2,24,128]{3,2,1,0:T(8,128)(2,1)S(1)} async-done(((bf16[12,2,24,128]{3,2,1,0:T(8,128)(2,1)}), bf16[12,2,24,128]{3,2,1,0:T(8,128)(2,1)S(1)}, u32[]{:S(2)}, u32[]{:S(2)}) %all-to-all-start.1) | async-done | bytes 147488 | tf_op jit(solution)/shard_map/all_to_all | solution.py:65
  43.5 0.6 gather_fusion
  44.1 0.7 select_select_fusion
  44.9 5.8 %all-to-all-start.2 = ((bf16[8,2,24,128]{3,2,1,0:T(8,128)(2,1)}), bf16[8,2,24,128]{3,2,1,0:T(8,128)(2,1)S(1)}, u32[]{:S(2)}, u32[]{:S(2)}) async-start(bf16[8,2,24,128]{3,2,1,0:T(8,128)(2,1)} %select_select_fusion), calls=%async_computation.2 | async-start | bytes 196608 | tf_op jit(solution)/shard_map/all_to_all | solution.py:89
  50.7 7.6 %all-to-all-done.2 = bf16[8,2,24,128]{3,2,1,0:T(8,128)(2,1)S(1)} async-done(((bf16[8,2,24,128]{3,2,1,0:T(8,128)(2,1)}), bf16[8,2,24,128]{3,2,1,0:T(8,128)(2,1)S(1)}, u32[]{:S(2)}, u32[]{:S(2)}) %all-to-all-start.2) | async-done | bytes 98336 | tf_op jit(solution)/shard_map/all_to_all | solution.py:89
  58.2 0.7 broadcast_in_dim.67
  58.9 9.0 %all-to-all-start.3 = ((bf16[8,2,24,128]{3,2,1,0:T(8,128)(2,1)}), bf16[8,2,24,128]{3,2,1,0:T(8,128)(2,1)S(1)}, u32[]{:S(2)}, u32[]{:S(2)}) async-start(bf16[8,2,24,128]{3,2,1,0:T(8,128)(2,1)} %broadcast_in_dim.67), calls=%async_computation.3 | async-start | bytes 196608 | tf_op jit(solution)/shard_map/all_to_all | solution.py:65
  67.9 5.0 %all-to-all-done.3 = bf16[8,2,24,128]{3,2,1,0:T(8,128)(2,1)S(1)} async-done(((bf16[8,2,24,128]{3,2,1,0:T(8,128)(2,1)}), bf16[8,2,24,128]{3,2,1,0:T(8,128)(2,1)S(1)}, u32[]{:S(2)}, u32[]{:S(2)}) %all-to-all-start.3) | async-done | bytes 98336 | tf_op jit(solution)/shard_map/all_to_all | solution.py:65
  72.9 0.7 fusion.2
  73.6 6.9 %fusion = f32[4,2,2,24,5,384]{5,3,4,2,1,0:T(8,128)S(1)} fusion(bf16[4,2,2,24,2560,1]{4,3,5,2,1,0:T(8,128)(2,1)S(1)} %fusion.2, bf16[2560,5,384]{2,0,1:T(8,128)(2,1)} %param.12), kind=kOutput, calls=%fused_computation.1 | convolution fusion | flops 3774873600 | bytes 14745600 | tf_op jit(solution)/shard_map/...d,dhe->...he/dot_general | solution.py:142
  80.6 2.9 %collective-permute-start.1 = (f32[4,2,24,5,384]{4,2,3,1,0:T(8,128)S(1)}, f32[4,2,24,5,384]{4,2,3,1,0:T(8,128)S(1)}, u32[]{:S(2)}, u32[]{:S(2)}) collective-permute-start(f32[4,2,24,5,384]{4,2,3,1,0:T(8,128)S(1)} %slice_bitcast_fusion), channel_id=1, source_target_pairs={{0,1},{1,0},{2,3},{3,2},{4,5},{5,4},{6,7},{7,6},{8,9},{9,8},{10,11... | collective-permute-start | bytes 4423688 | tf_op jit(solution)/shard_map/ppermute | solution.py:26
  83.4 2.9 %collective-permute-done.1 = f32[4,2,24,5,384]{4,2,3,1,0:T(8,128)S(1)} collective-permute-done((f32[4,2,24,5,384]{4,2,3,1,0:T(8,128)S(1)}, f32[4,2,24,5,384]{4,2,3,1,0:T(8,128)S(1)}, u32[]{:S(2)}, u32[]{:S(2)}) %collective-permute-start.1) | collective-permute-done | bytes 1474592 | tf_op jit(solution)/shard_map/ppermute | solution.py:26
  86.6 2.3 %collective-permute-start.2 = (bf16[4,2,24,5,256]{4,2,3,1,0:T(8,128)(2,1)S(1)}, bf16[4,2,24,5,256]{4,2,3,1,0:T(8,128)(2,1)S(1)}, u32[]{:S(2)}, u32[]{:S(2)}) collective-permute-start(bf16[4,2,24,5,256]{4,2,3,1,0:T(8,128)(2,1)S(1)} %slice.71), channel_id=1, source_target_pairs={{0,1},{1,0},{2,3},{3,2},{4,5},{5,4},{6,7},{7,6},{8,9},{9,8},{10,11... | collective-permute-start | bytes 1474568 | tf_op jit(solution)/shard_map/ppermute | solution.py:26
  89.7 0.7 collective-permute-done.2
  91.1 0.6 exponential_reduce_fusion
  91.7 0.8 convolution_convert_fusion.1
  92.5 1.1 %multiply_reduce_fusion = (f32[192,5]{0,1:T(8,128)S(1)}, bf16[5,128,192]{1,2,0:T(8,128)(2,1)}) fusion(bf16[192,5,128]{2,0,1:T(8,128)(2,1)S(1)} %bitcast.122, bf16[384,5,128]{2,0,1:T(8,128)(2,1)S(1)} %bitcast.113, f32[5,192,384]{2,1,0:T(8,128)S(1)} %get-tuple-element.29, f32[5,192]{1,0:T(8,128)S(1)} %log_add_fusion), kind=kOutput, calls=%fused_computation.37 | convolution fusion | flops 95722560 | bytes 2465280 | tf_op jit(solution)/shard_map/hqk,khd->qhd/dot_general | solution.py:163
  94.8 2.4 %collective-permute-start.3 = (bf16[2,4,2,24,5,128]{5,3,2,1,4,0:T(8,128)(2,1)S(1)}, bf16[2,4,2,24,5,128]{5,3,2,1,4,0:T(8,128)(2,1)S(1)}, u32[]{:S(2)}, u32[]{:S(2)}) collective-permute-start(bf16[2,4,2,24,5,128]{5,3,2,1,4,0:T(8,128)(2,1)S(1)} %fusion.15), channel_id=1, source_target_pairs={{0,1},{1,0},{2,3},{3,2},{4,5},{5,4},{6,7},{7,6},{8,9},{9,8},{10,11... | collective-permute-start | bytes 1474568 | tf_op jit(solution)/shard_map/ppermute | solution.py:26
  97.6 0.7 copy.47
  98.4 0.7 copy.46
  99.3 0.7 copy.48
  100.0 0.7 copy.49
  (33 shorter events, 3.3 us)
Async XLA Ops:
  0.6 72.3 %copy-start = (bf16[128,2560]{1,0:T(8,128)(2,1)S(1)}, bf16[128,2560]{1,0:T(8,128)(2,1)}, u32[]{:S(2)}) copy-start(bf16[128,2560]{1,0:T(8,128)(2,1)} %param.11) | copy-start | bytes 1966084
  2.0 14.1 %all-to-all-start = ((s32[8,1,1]{2,1,0:T(1,128)}), s32[8,1,1]{2,1,0:T(1,128)S(1)}, u32[]{:S(2)}, u32[]{:S(2)}) async-start(s32[8,1,1]{2,1,0:T(1,128)} %broadcast_in_dim.60), calls=%async_computation | async-start | bytes 8192 | tf_op jit(solution)/shard_map/all_to_all | solution.py:65
  10.3 6.0 %collective-permute-start = (bf16[1,2,24,128]{3,2,1,0:T(8,128)(2,1)S(1)}, bf16[1,2,24,128]{3,2,1,0:T(8,128)(2,1)S(1)}, u32[]{:S(2)}, u32[]{:S(2)}) collective-permute-start(bf16[1,2,24,128]{3,2,1,0:T(8,128)(2,1)S(1)} %slice_bitcast_fusion.2), channel_id=1, source_target_pairs={{0,192},{192,384},{384,576},{1,193},{193,385},{385,577},{2,194},{1... | collective-permute-start | bytes 36872 | tf_op jit(solution)/shard_map/ppermute | solution.py:22
  17.9 25.6 %all-to-all-start.1 = ((bf16[12,2,24,128]{3,2,1,0:T(8,128)(2,1)}), bf16[12,2,24,128]{3,2,1,0:T(8,128)(2,1)S(1)}, u32[]{:S(2)}, u32[]{:S(2)}) async-start(bf16[12,2,24,128]{3,2,1,0:T(8,128)(2,1)} %broadcast_in_dim.63), calls=%async_computation.1 | async-start | bytes 294912 | tf_op jit(solution)/shard_map/all_to_all | solution.py:65
  44.9 13.4 %all-to-all-start.2 = ((bf16[8,2,24,128]{3,2,1,0:T(8,128)(2,1)}), bf16[8,2,24,128]{3,2,1,0:T(8,128)(2,1)S(1)}, u32[]{:S(2)}, u32[]{:S(2)}) async-start(bf16[8,2,24,128]{3,2,1,0:T(8,128)(2,1)} %select_select_fusion), calls=%async_computation.2 | async-start | bytes 196608 | tf_op jit(solution)/shard_map/all_to_all | solution.py:89
  58.9 14.0 %all-to-all-start.3 = ((bf16[8,2,24,128]{3,2,1,0:T(8,128)(2,1)}), bf16[8,2,24,128]{3,2,1,0:T(8,128)(2,1)S(1)}, u32[]{:S(2)}, u32[]{:S(2)}) async-start(bf16[8,2,24,128]{3,2,1,0:T(8,128)(2,1)} %broadcast_in_dim.67), calls=%async_computation.3 | async-start | bytes 196608 | tf_op jit(solution)/shard_map/all_to_all | solution.py:65
  80.6 9.0 %copy-start.2 = (bf16[1,4,2,24,5,128]{5,3,4,2,1,0:T(8,128)(2,1)S(1)}, bf16[1,4,2,24,5,128]{5,3,4,2,1,0:T(8,128)(2,1)}, u32[]{:S(2)}) copy-start(bf16[1,4,2,24,5,128]{5,3,4,2,1,0:T(8,128)(2,1)} %param.13) | copy-start | bytes 737284
  80.6 5.7 %collective-permute-start.1 = (f32[4,2,24,5,384]{4,2,3,1,0:T(8,128)S(1)}, f32[4,2,24,5,384]{4,2,3,1,0:T(8,128)S(1)}, u32[]{:S(2)}, u32[]{:S(2)}) collective-permute-start(f32[4,2,24,5,384]{4,2,3,1,0:T(8,128)S(1)} %slice_bitcast_fusion), channel_id=1, source_target_pairs={{0,1},{1,0},{2,3},{3,2},{4,5},{5,4},{6,7},{7,6},{8,9},{9,8},{10,11... | collective-permute-start | bytes 4423688 | tf_op jit(solution)/shard_map/ppermute | solution.py:26
  86.6 3.8 %collective-permute-start.2 = (bf16[4,2,24,5,256]{4,2,3,1,0:T(8,128)(2,1)S(1)}, bf16[4,2,24,5,256]{4,2,3,1,0:T(8,128)(2,1)S(1)}, u32[]{:S(2)}, u32[]{:S(2)}) collective-permute-start(bf16[4,2,24,5,256]{4,2,3,1,0:T(8,128)(2,1)S(1)} %slice.71), channel_id=1, source_target_pairs={{0,1},{1,0},{2,3},{3,2},{4,5},{5,4},{6,7},{7,6},{8,9},{9,8},{10,11... | collective-permute-start | bytes 1474568 | tf_op jit(solution)/shard_map/ppermute | solution.py:26
  94.8 3.6 %copy-start.1 = (bf16[5,128,192]{1,2,0:T(8,128)(2,1)S(1)}, bf16[5,128,192]{1,2,0:T(8,128)(2,1)}, u32[]{:S(2)}) copy-start(bf16[5,128,192]{1,2,0:T(8,128)(2,1)} %get-tuple-element.31) | copy-start | bytes 737284
  94.8 4.2 %collective-permute-start.3 = (bf16[2,4,2,24,5,128]{5,3,2,1,4,0:T(8,128)(2,1)S(1)}, bf16[2,4,2,24,5,128]{5,3,2,1,4,0:T(8,128)(2,1)S(1)}, u32[]{:S(2)}, u32[]{:S(2)}) collective-permute-start(bf16[2,4,2,24,5,128]{5,3,2,1,4,0:T(8,128)(2,1)S(1)} %fusion.15), channel_id=1, source_target_pairs={{0,1},{1,0},{2,3},{3,2},{4,5},{5,4},{6,7},{7,6},{8,9},{9,8},{10,11... | collective-permute-start | bytes 1474568 | tf_op jit(solution)/shard_map/ppermute | solution.py:26

commit v9 on v8

--- a/solution.py
+++ b/solution.py
@@ -142,9 +142,10 @@
         return jnp.einsum("...d,dhe->...he", hidden, qkv_w, preferred_element_type=jnp.float32)
 
     partial_qkv = project(latent)
-    own_qkv = (partial_qkv[:, 0] + swap_seq(partial_qkv[:, 1])).astype(jnp.bfloat16)
+    got_rows, got_pair = swap_seq((partial_qkv[:, 1], partial_qkv[:, 0, ..., head_size:]))
+    own_qkv = (partial_qkv[:, 0] + got_rows).astype(jnp.bfloat16)
     own_pair = own_qkv[..., head_size:]
-    other_pair = swap_seq(own_pair)
+    other_pair = (partial_qkv[:, 1, ..., head_size:] + got_pair).astype(jnp.bfloat16)
     all_pair = jnp.concatenate([own_pair, other_pair], axis=1)
     queries5 = own_qkv[..., :head_size]
     scale = 1.0 / math.sqrt(head_size)

time: 102 us -> 99.5 us (0.975)
  waiting for transfers between devices: 27.6 us -> 25.9 us
    ppermute x3, waiting for transfers between devices: 3.55 us -> 1.83 us  [swap_seq(): return lax.ppermute(x, 'seq', [(0, 1), (1, 0)])]
  transfers between devices with their start and end apart: 8 -> 8, of which waited for: 6 -> 5; matrix products, arithmetic and copies ran while one was open for 5% -> 5% of each run, Pallas kernels for 0% -> 0%
where the time goes in v9:
time: 99.5 us; the launch traced here: 98.6 us
  starting transfers between devices  47.4 us (48%)
  waiting for transfers between devices  25.9 us (26%)
  matrix products  13.9 us (14%)
  local copies, waits for them, and re-layouts  6.87 us (7%)
  other arithmetic  2.3 us (2%)
  between operations  2.28 us (2%)
    all_to_all x3, starting transfers between devices, gather_a2a(): return lax.all_to_all(send, axis, 0, 0, tiled=True)  31.5 us
    all_to_all x3, waiting for transfers between devices, gather_a2a(): return lax.all_to_all(send, axis, 0, 0, tiled=True)  16.5 us
    all_to_all x1, waiting for transfers between devices, route(): got = lax.all_to_all(send, INNER, 0, 0, tiled=True)  7.58 us
    ppermute x3, starting transfers between devices, swap_seq(): return lax.ppermute(x, 'seq', [(0, 1), (1, 0)])  6.96 us
    dot_general x1, matrix products, project(): jnp.einsum('...d,dhe->...he', hidden, qkv_w, preferred_element_type=jnp.f...  6.87 us
    all_to_all x1, starting transfers between devices, route(): got = lax.all_to_all(send, INNER, 0, 0, tiled=True)  5.82 us
    ppermute x1, starting transfers between devices, passed_along(): return lax.ppermute(shard, axis, pairs)  3.1 us
    unnamed x11, local copies, waits for them, and re-layouts  2.92 us
  transfers between devices with their start and end apart: 8, of which 5 were waited for; matrix products, arithmetic and copies ran while one was open for 5% of the time, Pallas kernels for 0%

profile of v9, /device:TPU:1, one launch (start us, length us, event | category | flops | bytes accessed | tf_op | source)
XLA Modules:
  0.0 98.6 jit_solution(11217719102870181642)
XLA Ops:
  1.4 0.6 broadcast_in_dim.60
  2.0 7.6 %all-to-all-start = ((s32[8,1,1]{2,1,0:T(1,128)}), s32[8,1,1]{2,1,0:T(1,128)S(1)}, u32[]{:S(2)}, u32[]{:S(2)}) async-start(s32[8,1,1]{2,1,0:T(1,128)} %broadcast_in_dim.60), calls=%async_computation | async-start | bytes 8192 | tf_op jit(solution)/shard_map/all_to_all | solution.py:65
  9.6 0.7 slice_bitcast_fusion.4
  10.3 3.1 %collective-permute-start = (bf16[1,2,24,128]{3,2,1,0:T(8,128)(2,1)S(1)}, bf16[1,2,24,128]{3,2,1,0:T(8,128)(2,1)S(1)}, u32[]{:S(2)}, u32[]{:S(2)}) collective-permute-start(bf16[1,2,24,128]{3,2,1,0:T(8,128)(2,1)S(1)} %slice_bitcast_fusion.4), channel_id=1, source_target_pairs={{0,192},{192,384},{384,576},{1,193},{193,385},{385,577},{2,194},{1... | collective-permute-start | bytes 36872 | tf_op jit(solution)/shard_map/ppermute | solution.py:22
  13.4 0.9 fusion.25
  14.3 0.9 convolution_add_fusion.1
  15.2 0.8 all-to-all-done
  16.3 0.9 multiply_convert_fusion
  17.2 0.7 broadcast_in_dim.63
  17.9 14.9 %all-to-all-start.1 = ((bf16[12,2,24,128]{3,2,1,0:T(8,128)(2,1)}), bf16[12,2,24,128]{3,2,1,0:T(8,128)(2,1)S(1)}, u32[]{:S(2)}, u32[]{:S(2)}) async-start(bf16[12,2,24,128]{3,2,1,0:T(8,128)(2,1)} %broadcast_in_dim.63), calls=%async_computation.1 | async-start | bytes 294912 | tf_op jit(solution)/shard_map/all_to_all | solution.py:65
  32.9 10.7 %all-to-all-done.1 = bf16[12,2,24,128]{3,2,1,0:T(8,128)(2,1)S(1)} async-done(((bf16[12,2,24,128]{3,2,1,0:T(8,128)(2,1)}), bf16[12,2,24,128]{3,2,1,0:T(8,128)(2,1)S(1)}, u32[]{:S(2)}, u32[]{:S(2)}) %all-to-all-start.1) | async-done | bytes 147488 | tf_op jit(solution)/shard_map/all_to_all | solution.py:65
  43.5 0.6 gather_fusion
  44.1 0.7 select_select_fusion
  44.9 5.8 %all-to-all-start.2 = ((bf16[8,2,24,128]{3,2,1,0:T(8,128)(2,1)}), bf16[8,2,24,128]{3,2,1,0:T(8,128)(2,1)S(1)}, u32[]{:S(2)}, u32[]{:S(2)}) async-start(bf16[8,2,24,128]{3,2,1,0:T(8,128)(2,1)} %select_select_fusion), calls=%async_computation.2 | async-start | bytes 196608 | tf_op jit(solution)/shard_map/all_to_all | solution.py:89
  50.7 7.6 %all-to-all-done.2 = bf16[8,2,24,128]{3,2,1,0:T(8,128)(2,1)S(1)} async-done(((bf16[8,2,24,128]{3,2,1,0:T(8,128)(2,1)}), bf16[8,2,24,128]{3,2,1,0:T(8,128)(2,1)S(1)}, u32[]{:S(2)}, u32[]{:S(2)}) %all-to-all-start.2) | async-done | bytes 98336 | tf_op jit(solution)/shard_map/all_to_all | solution.py:89
  58.2 0.7 broadcast_in_dim.67
  58.9 9.0 %all-to-all-start.3 = ((bf16[8,2,24,128]{3,2,1,0:T(8,128)(2,1)}), bf16[8,2,24,128]{3,2,1,0:T(8,128)(2,1)S(1)}, u32[]{:S(2)}, u32[]{:S(2)}) async-start(bf16[8,2,24,128]{3,2,1,0:T(8,128)(2,1)} %broadcast_in_dim.67), calls=%async_computation.3 | async-start | bytes 196608 | tf_op jit(solution)/shard_map/all_to_all | solution.py:65
  67.9 5.0 %all-to-all-done.3 = bf16[8,2,24,128]{3,2,1,0:T(8,128)(2,1)S(1)} async-done(((bf16[8,2,24,128]{3,2,1,0:T(8,128)(2,1)}), bf16[8,2,24,128]{3,2,1,0:T(8,128)(2,1)S(1)}, u32[]{:S(2)}, u32[]{:S(2)}) %all-to-all-start.3) | async-done | bytes 98336 | tf_op jit(solution)/shard_map/all_to_all | solution.py:65
  72.9 0.7 fusion.2
  73.6 6.9 %fusion = f32[4,2,2,24,5,384]{5,3,4,2,1,0:T(8,128)S(1)} fusion(bf16[4,2,2,24,2560,1]{4,3,5,2,1,0:T(8,128)(2,1)S(1)} %fusion.2, bf16[2560,5,384]{2,0,1:T(8,128)(2,1)} %param.12), kind=kOutput, calls=%fused_computation.1 | convolution fusion | flops 3774873600 | bytes 14745600 | tf_op jit(solution)/shard_map/...d,dhe->...he/dot_general | solution.py:142
  80.6 2.9 %collective-permute-start.1 = (f32[4,2,24,5,384]{4,2,3,1,0:T(8,128)S(1)}, f32[4,2,24,5,384]{4,2,3,1,0:T(8,128)S(1)}, u32[]{:S(2)}, u32[]{:S(2)}) collective-permute-start(f32[4,2,24,5,384]{4,2,3,1,0:T(8,128)S(1)} %slice_bitcast_fusion), channel_id=1, source_target_pairs={{0,1},{1,0},{2,3},{3,2},{4,5},{5,4},{6,7},{7,6},{8,9},{9,8},{10,11... | collective-permute-start | bytes 4423688 | tf_op jit(solution)/shard_map/ppermute | solution.py:26
  83.5 1.9 %collective-permute-start.2 = (f32[4,2,24,5,256]{4,2,3,1,0:T(8,128)S(1)}, f32[4,2,24,5,256]{4,2,3,1,0:T(8,128)S(1)}, u32[]{:S(2)}, u32[]{:S(2)}) collective-permute-start(f32[4,2,24,5,256]{4,2,3,1,0:T(8,128)S(1)} %slice_bitcast_fusion.2), channel_id=1, source_target_pairs={{0,1},{1,0},{2,3},{3,2},{4,5},{5,4},{6,7},{7,6},{8,9},{9,8},{10,11... | collective-permute-start | bytes 2949128 | tf_op jit(solution)/shard_map/ppermute | solution.py:26
  86.2 1.8 %collective-permute-done.2 = f32[4,2,24,5,256]{4,2,3,1,0:T(8,128)S(1)} collective-permute-done((f32[4,2,24,5,256]{4,2,3,1,0:T(8,128)S(1)}, f32[4,2,24,5,256]{4,2,3,1,0:T(8,128)S(1)}, u32[]{:S(2)}, u32[]{:S(2)}) %collective-permute-start.2) | collective-permute-done | bytes 983072 | tf_op jit(solution)/shard_map/ppermute | solution.py:26
  88.7 0.5 fusion.45
  89.2 0.6 exponential_reduce_fusion
  89.9 0.8 convolution_convert_fusion.1
  90.6 1.1 %multiply_reduce_fusion = (f32[192,5]{0,1:T(8,128)S(1)}, bf16[5,128,192]{1,2,0:T(8,128)(2,1)}) fusion(bf16[192,5,128]{2,0,1:T(8,128)(2,1)S(1)} %bitcast.134, bf16[384,5,128]{2,0,1:T(8,128)(2,1)S(1)} %bitcast.125, f32[5,192,384]{2,1,0:T(8,128)S(1)} %get-tuple-element.29, f32[5,192]{1,0:T(8,128)S(1)} %log_add_fusion), kind=kOutput, calls=%fused_computation.41 | convolution fusion | flops 95722560 | bytes 2465280 | tf_op jit(solution)/shard_map/hqk,khd->qhd/dot_general | solution.py:164
  93.0 2.2 %collective-permute-start.3 = (bf16[2,4,2,24,5,128]{5,3,2,1,4,0:T(8,128)(2,1)S(1)}, bf16[2,4,2,24,5,128]{5,3,2,1,4,0:T(8,128)(2,1)S(1)}, u32[]{:S(2)}, u32[]{:S(2)}) collective-permute-start(bf16[2,4,2,24,5,128]{5,3,2,1,4,0:T(8,128)(2,1)S(1)} %fusion.17), channel_id=1, source_target_pairs={{0,1},{1,0},{2,3},{3,2},{4,5},{5,4},{6,7},{7,6},{8,9},{9,8},{10,11... | collective-permute-start | bytes 1474568 | tf_op jit(solution)/shard_map/ppermute | solution.py:26
  95.6 0.7 copy.55
  96.3 0.7 copy.54
  97.2 0.7 copy.56
  97.9 0.7 copy.57
  (35 shorter events, 3.0 us)
Async XLA Ops:
  0.6 72.3 %copy-start = (bf16[128,2560]{1,0:T(8,128)(2,1)S(1)}, bf16[128,2560]{1,0:T(8,128)(2,1)}, u32[]{:S(2)}) copy-start(bf16[128,2560]{1,0:T(8,128)(2,1)} %param.11) | copy-start | bytes 1966084
  2.0 14.1 %all-to-all-start = ((s32[8,1,1]{2,1,0:T(1,128)}), s32[8,1,1]{2,1,0:T(1,128)S(1)}, u32[]{:S(2)}, u32[]{:S(2)}) async-start(s32[8,1,1]{2,1,0:T(1,128)} %broadcast_in_dim.60), calls=%async_computation | async-start | bytes 8192 | tf_op jit(solution)/shard_map/all_to_all | solution.py:65
  10.3 6.0 %collective-permute-start = (bf16[1,2,24,128]{3,2,1,0:T(8,128)(2,1)S(1)}, bf16[1,2,24,128]{3,2,1,0:T(8,128)(2,1)S(1)}, u32[]{:S(2)}, u32[]{:S(2)}) collective-permute-start(bf16[1,2,24,128]{3,2,1,0:T(8,128)(2,1)S(1)} %slice_bitcast_fusion.4), channel_id=1, source_target_pairs={{0,192},{192,384},{384,576},{1,193},{193,385},{385,577},{2,194},{1... | collective-permute-start | bytes 36872 | tf_op jit(solution)/shard_map/ppermute | solution.py:22
  17.9 25.6 %all-to-all-start.1 = ((bf16[12,2,24,128]{3,2,1,0:T(8,128)(2,1)}), bf16[12,2,24,128]{3,2,1,0:T(8,128)(2,1)S(1)}, u32[]{:S(2)}, u32[]{:S(2)}) async-start(bf16[12,2,24,128]{3,2,1,0:T(8,128)(2,1)} %broadcast_in_dim.63), calls=%async_computation.1 | async-start | bytes 294912 | tf_op jit(solution)/shard_map/all_to_all | solution.py:65
  44.9 13.4 %all-to-all-start.2 = ((bf16[8,2,24,128]{3,2,1,0:T(8,128)(2,1)}), bf16[8,2,24,128]{3,2,1,0:T(8,128)(2,1)S(1)}, u32[]{:S(2)}, u32[]{:S(2)}) async-start(bf16[8,2,24,128]{3,2,1,0:T(8,128)(2,1)} %select_select_fusion), calls=%async_computation.2 | async-start | bytes 196608 | tf_op jit(solution)/shard_map/all_to_all | solution.py:89
  58.9 14.0 %all-to-all-start.3 = ((bf16[8,2,24,128]{3,2,1,0:T(8,128)(2,1)}), bf16[8,2,24,128]{3,2,1,0:T(8,128)(2,1)S(1)}, u32[]{:S(2)}, u32[]{:S(2)}) async-start(bf16[8,2,24,128]{3,2,1,0:T(8,128)(2,1)} %broadcast_in_dim.67), calls=%async_computation.3 | async-start | bytes 196608 | tf_op jit(solution)/shard_map/all_to_all | solution.py:65
  80.6 5.5 %copy-start.2 = (bf16[1,4,2,24,5,128]{5,3,4,2,1,0:T(8,128)(2,1)S(1)}, bf16[1,4,2,24,5,128]{5,3,4,2,1,0:T(8,128)(2,1)}, u32[]{:S(2)}) copy-start(bf16[1,4,2,24,5,128]{5,3,4,2,1,0:T(8,128)(2,1)} %param.13) | copy-start | bytes 737284
  80.6 7.6 %collective-permute-start.1 = (f32[4,2,24,5,384]{4,2,3,1,0:T(8,128)S(1)}, f32[4,2,24,5,384]{4,2,3,1,0:T(8,128)S(1)}, u32[]{:S(2)}, u32[]{:S(2)}) collective-permute-start(f32[4,2,24,5,384]{4,2,3,1,0:T(8,128)S(1)} %slice_bitcast_fusion), channel_id=1, source_target_pairs={{0,1},{1,0},{2,3},{3,2},{4,5},{5,4},{6,7},{7,6},{8,9},{9,8},{10,11... | collective-permute-start | bytes 4423688 | tf_op jit(solution)/shard_map/ppermute | solution.py:26
  83.5 4.5 %collective-permute-start.2 = (f32[4,2,24,5,256]{4,2,3,1,0:T(8,128)S(1)}, f32[4,2,24,5,256]{4,2,3,1,0:T(8,128)S(1)}, u32[]{:S(2)}, u32[]{:S(2)}) collective-permute-start(f32[4,2,24,5,256]{4,2,3,1,0:T(8,128)S(1)} %slice_bitcast_fusion.2), channel_id=1, source_target_pairs={{0,1},{1,0},{2,3},{3,2},{4,5},{5,4},{6,7},{7,6},{8,9},{9,8},{10,11... | collective-permute-start | bytes 2949128 | tf_op jit(solution)/shard_map/ppermute | solution.py:26
  92.9 3.4 %copy-start.1 = (bf16[5,128,192]{1,2,0:T(8,128)(2,1)S(1)}, bf16[5,128,192]{1,2,0:T(8,128)(2,1)}, u32[]{:S(2)}) copy-start(bf16[5,128,192]{1,2,0:T(8,128)(2,1)} %get-tuple-element.31) | copy-start | bytes 737284
  93.0 4.0 %collective-permute-start.3 = (bf16[2,4,2,24,5,128]{5,3,2,1,4,0:T(8,128)(2,1)S(1)}, bf16[2,4,2,24,5,128]{5,3,2,1,4,0:T(8,128)(2,1)S(1)}, u32[]{:S(2)}, u32[]{:S(2)}) collective-permute-start(bf16[2,4,2,24,5,128]{5,3,2,1,4,0:T(8,128)(2,1)S(1)} %fusion.17), channel_id=1, source_target_pairs={{0,1},{1,0},{2,3},{3,2},{4,5},{5,4},{6,7},{7,6},{8,9},{9,8},{10,11... | collective-permute-start | bytes 1474568 | tf_op jit(solution)/shard_map/ppermute | solution.py:26
